TPU v7x, 512 devices: a whole 4x4x16 slice. The times are simulated.
512 devices in a mesh: trk: 128 (over x, z, core), cam: 4 (over y).
Axes of the slice: x: 4, y: 4, z: 16, core: 2. Of those that a mesh axis runs over, the one named last changes fastest.
Arguments:
- residuals: float32 [2, 393216], P(None, ('trk', 'cam')), may hold values from -6 to 6
- camera_jac: float32 [18, 393216], P(None, ('trk', 'cam')), may hold values from -9 to 9
- point_jac: float32 [6, 393216], P(None, ('trk', 'cam')), may hold values from -6 to 6
- obs_index: int32 [3, 393216], P(None, ('trk', 'cam')), may hold values from 0 to 4095, as said below
- damping: float32 [32768], P('trk'), may hold values from 0.5 to 4
Outputs:
- elimination_tiles: float32 [128, 4, 7, 20736], P('trk', 'cam')
Inputs may be any that keep to these rules, and one draw needn't show every extreme that they name: For each c and e, the values obs_index[0, n] of the rows n = ((t * 4 + c) * 128 + e) * 6 + q over all t and q are a permutation of 0 to 767. The camera obs_index[1, n] of such a row lies in a block (camera // 16) among 2 * e to 2 * e + 7, taken modulo 256. obs_index[2, n] is 1 for a live observation and 0 for a padded slot.
All inputs are finite; a program needn't handle non-finite values.
Results may differ from a plain program's by a relative error of at most 0.0003.
Values sent between devices are 32-bit elements; how exact they have to be, the bound alone decides.
No kernel may reach another device: no remote copies, remote signals or barrier semaphores. Data moves between devices by JAX's collectives and lax.ppermute only.
A program may use at most 64 MiB of HBM per device.

v0:
```python
import jax
import jax.numpy as jnp
from jax import lax
from jax.sharding import PartitionSpec as P

CAMERAS_PER_BLK = 16
TS = 144
HOPS = 3


HUBER_DELTA = 1.0
UPPER_PAIRS = ((0, 0), (0, 1), (0, 2), (1, 1), (1, 2), (2, 2))


def from_behind(x, axis, by):
    size = lax.axis_size(axis)
    return lax.ppermute(x, axis, [(i, (i + by) % size) for i in range(size)])


def body(residuals, camera_jac, point_jac, obs_index, damping):
    strip_count = lax.axis_size("trk")
    tracks = damping.shape[0]
    rows = residuals.shape[1]
    per_dest = rows // strip_count
    fields = jnp.concatenate(
        [residuals, camera_jac, point_jac, obs_index.astype(jnp.float32)], axis=0
    )
    nf = fields.shape[0]
    send = fields.reshape((nf, strip_count, per_dest)).transpose((1, 0, 2))
    send = send.reshape((strip_count, nf * per_dest))
    got = lax.all_to_all(send, "trk", split_axis=0, concat_axis=0, tiled=True)
    got = got.reshape((strip_count, nf, per_dest)).transpose((1, 0, 2)).reshape((nf, rows))
    position = got[nf - 3].astype(jnp.int32)
    local_slots = rows // tracks
    onehot = (position[:, None] == jnp.arange(rows, dtype=jnp.int32)[None, :]).astype(jnp.float32)
    kept = jnp.concatenate([got[: nf - 3], got[nf - 2 :]], axis=0)
    placed = jnp.dot(kept, onehot, precision=lax.Precision.HIGHEST)
    gathered = lax.all_gather(placed, "cam", axis=1, tiled=False)
    n_cam = gathered.shape[1]
    slots = n_cam * local_slots
    g = gathered.reshape((kept.shape[0], slots, tracks))
    res = g[0:2]
    cj = g[2:20]
    pj = g[20:26]
    cam = g[26].astype(jnp.int32)
    alive = g[27]
    magnitude = jnp.sqrt(res[0] * res[0] + res[1] * res[1])
    w = alive * (HUBER_DELTA / jnp.maximum(magnitude, HUBER_DELTA))
    coup = (cj[:9, None] * pj[None, :3] + cj[9:, None] * pj[None, 3:]) * w
    terms = [
        (w * (pj[k] * pj[l] + pj[3 + k] * pj[3 + l])).sum(axis=0) for k, l in UPPER_PAIRS
    ]
    a, b, c, d, e, f = terms
    a = a + damping
    d = d + damping
    f = f + damping
    cof = [d * f - e * e, c * e - b * f, b * e - c * d, a * f - c * c, b * c - a * e, a * d - b * b]
    det = a * cof[0] + b * cof[1] + c * cof[2]
    sc = [x / det for x in cof]
    inv = [[sc[0], sc[1], sc[2]], [sc[1], sc[3], sc[4]], [sc[2], sc[4], sc[5]]]
    left = jnp.stack(
        [coup[:, 0] * inv[0][l] + coup[:, 1] * inv[1][l] + coup[:, 2] * inv[2][l] for l in range(3)],
        axis=1,
    )
    strip_index = lax.axis_index("trk")
    column = lax.axis_index("cam")
    visible = jnp.mod(cam // CAMERAS_PER_BLK - 2 * strip_index, 2 * strip_count)
    key = visible * CAMERAS_PER_BLK + cam % CAMERAS_PER_BLK
    owners = HOPS + 1
    grp = jnp.arange(owners * CAMERAS_PER_BLK, dtype=jnp.int32)
    base = (2 * (grp // CAMERAS_PER_BLK)) * CAMERAS_PER_BLK + grp % CAMERAS_PER_BLK
    key_left = base + (column // 2) * CAMERAS_PER_BLK
    key_right = base + (column % 2) * CAMERAS_PER_BLK
    left3 = left.transpose((0, 2, 1, 3)).reshape((9, slots, 3 * tracks))
    coup3 = coup.transpose((0, 2, 1, 3)).reshape((9, slots, 3 * tracks))
    key3 = jnp.tile(key, (1, 3))
    groups = owners * CAMERAS_PER_BLK
    width = owners * TS
    full = (groups, 9, slots, 3 * tracks)

    def panel(keys, values):
        sel = (key3[None] == keys[:, None, None]).astype(jnp.float32)
        sel = jnp.broadcast_to(sel[:, None], full).reshape((width, slots, 3 * tracks))
        vals = jnp.broadcast_to(values[None], full).reshape((width, slots, 3 * tracks))
        return jnp.sum(sel * vals, axis=1)

    left_flat = panel(key_left, left3)
    right_flat = panel(key_right, coup3)
    product = lax.dot_general(
        left_flat, right_flat, (((1,), (1,)), ((), ())), precision=lax.Precision.HIGH
    )
    tiles = product.reshape((owners, TS, owners, TS)).transpose((0, 2, 1, 3))
    tiles = tiles.reshape((owners, owners, TS * TS))
    tile_count = 2 * HOPS + 1
    summed = jnp.pad(tiles[0], ((HOPS, 0), (0, 0)))
    for distance in range(owners - 1, 0, -1):
        arrived = from_behind(tiles[distance], "trk", distance)
        summed = summed + jnp.pad(arrived, ((HOPS - distance, distance), (0, 0)))
    return summed.reshape((1, 1, tile_count, TS * TS))


def solution(mesh):
    placed = (
        P(None, ("trk", "cam")),
        P(None, ("trk", "cam")),
        P(None, ("trk", "cam")),
        P(None, ("trk", "cam")),
        P("trk"),
    )
    return jax.shard_map(
        body, mesh=mesh, in_specs=placed, out_specs=P("trk", "cam", None, None), check_vma=False
    )
```

profile of v0, /device:TPU:1, one launch (start us, length us, event | category | flops | bytes accessed | tf_op | source)
XLA Modules:
  0.0 107.4 jit_solution(2551399275987566152)
XLA Ops:
  0.0 0.7 convert_element_type.46
  0.7 0.9 pad_maximum_fusion
  1.6 0.2 copy.30
  1.8 0.1 reshape.231
  1.9 0.2 copy.31
  2.1 0.8 copy.32
  2.9 20.4 %all-to-all-start = ((f32[128,1,174]{2,1,0:T(1,128)}), f32[128,1,174]{2,1,0:T(1,128)S(1)}, u32[]{:S(2)}, u32[]{:S(2)}) async-start(f32[128,1,174]{2,1,0:T(1,128)} %copy.32), calls=%async_computation | async-start | bytes 262144 | tf_op jit(solution)/shard_map/all_to_all | solution.py:31
  23.3 17.3 %all-to-all-done = f32[128,1,174]{2,1,0:T(1,128)S(1)} async-done(((f32[128,1,174]{2,1,0:T(1,128)}), f32[128,1,174]{2,1,0:T(1,128)S(1)}, u32[]{:S(2)}, u32[]{:S(2)}) %all-to-all-start) | async-done | bytes 89120 | tf_op jit(solution)/shard_map/all_to_all | solution.py:31
  40.6 0.1 copy.33
  40.8 0.1 copy.37
  40.9 0.1 convert_element_type.48
  41.0 0.1 copy.35
  41.1 0.1 slice.144
  41.3 0.3 copy.34
  41.6 0.2 copy.36
  41.8 0.9 fusion
  42.7 10.3 %all-gather = f32[28,3072]{1,0:T(8,128)S(1)} all-gather(f32[28,768]{1,0:T(8,128)S(1)} %fusion), channel_id=2, replica_groups=mesh['trk'=128,'cam'=4] {'cam'}, dimensions={1}, use_global_device_ids=true | all-gather | bytes 430080 | tf_op jit(solution)/shard_map/all_gather | solution.py:38
  53.1 0.3 add_reduce_fusion.4
  53.9 0.0 copy-done
  54.0 0.1 add_multiply_fusion.1
  54.1 0.5 multiply_add_fusion.2
  54.7 0.3 maximum_bitcast_fusion
  55.0 0.2 broadcast_in_dim.11
  55.3 0.1 mul.554
  55.3 0.2 mul.555
  55.6 0.1 mul.560
  55.7 0.2 mul.561
  55.9 0.6 compare_convert_fusion.1
  56.5 0.1 add_multiply_fusion
  56.5 5.4 %multiply_reduce_fusion = (f32[64,9,768]{2,0,1:T(8,128)}, f32[64,9,768]{2,0,1:T(8,128)}) fusion(f32[9,12,768]{2,1,0:T(8,128)S(1)} %add_multiply_fusion, f32[64,12,768]{2,0,1:T(8,128)S(1)} %get-tuple-element.33, f32[9,12,768]{2,1,0:T(8,128)S(1)} %broadcast_in_dim.11, f32[64,12,768]{2,0,1:T(8,128)S(1)} %get-tuple-element.32), kind=kLoop, calls=%fused_computation | loop fusion | flops 20348928 | bytes 8921088 | tf_op jit(solution)/shard_map/reduce_sum | solution.py:85
  62.0 2.6 %copy.43 = f32[64,9,768]{2,1,0:T(8,128)S(1)} copy(f32[64,9,768]{2,0,1:T(8,128)} %get-tuple-element.39) | data formatting | bytes 3538944 | tf_op jit(solution)/shard_map/reduce_sum | solution.py:85
  64.5 1.6 %reshape.293 = f32[4,144,768,1]{2,1,0,3:T(8,128)} reshape(f32[64,9,768]{2,1,0:T(8,128)S(1)} %copy.43) | data formatting | bytes 3538944 | tf_op jit(solution)/shard_map/dot_general | solution.py:89
  66.1 2.6 %copy.40 = f32[64,9,768]{2,1,0:T(8,128)S(1)} copy(f32[64,9,768]{2,0,1:T(8,128)} %get-tuple-element.40) | data formatting | bytes 3538944 | tf_op jit(solution)/shard_map/reduce_sum | solution.py:85
  68.7 1.4 %reshape.292 = f32[4,144,768,1]{2,1,0,3:T(8,128)} reshape(f32[64,9,768]{2,1,0:T(8,128)S(1)} %copy.40) | data formatting | bytes 3538944 | tf_op jit(solution)/shard_map/dot_general | solution.py:89
  70.1 5.0 %fusion.3 = f32[4,4,144,144]{3,2,1,0:T(8,128)S(1)} fusion(f32[4,144,768,1]{2,1,0,3:T(8,128)} %reshape.293, f32[4,144,768,1]{2,1,0,3:T(8,128)} %reshape.292), kind=kOutput, calls=%fused_computation.8 | convolution fusion | flops 1528823808 | bytes 4866048 | tf_op jit(solution)/shard_map/dot_general | solution.py:89
  75.1 0.2 fusion.24
  75.2 0.4 squeeze.14
  75.6 0.4 squeeze.13
  76.1 0.4 squeeze.12
  76.5 6.7 %collective-permute-start = (f32[4,20736]{1,0:T(4,128)S(1)}, f32[4,20736]{1,0:T(4,128)S(1)}, u32[]{:S(2)}, u32[]{:S(2)}) collective-permute-start(f32[4,20736]{1,0:T(4,128)S(1)} %squeeze.12), channel_id=1, source_target_pairs={{0,12},{4,16},{8,20},{12,24},{16,28},{20,32},{24,36},{28,40},{32,4... | collective-permute-start | bytes 995336 | tf_op jit(solution)/shard_map/ppermute | solution.py:17
  83.2 2.5 %collective-permute-start.1 = (f32[4,20736]{1,0:T(4,128)S(1)}, f32[4,20736]{1,0:T(4,128)S(1)}, u32[]{:S(2)}, u32[]{:S(2)}) collective-permute-start(f32[4,20736]{1,0:T(4,128)S(1)} %squeeze.13), channel_id=1, source_target_pairs={{0,8},{4,12},{8,16},{12,20},{16,24},{20,28},{24,32},{28,36},{32,40... | collective-permute-start | bytes 995336 | tf_op jit(solution)/shard_map/ppermute | solution.py:17
  85.7 1.9 %collective-permute-start.2 = (f32[4,20736]{1,0:T(4,128)S(1)}, f32[4,20736]{1,0:T(4,128)}, u32[]{:S(2)}, u32[]{:S(2)}) collective-permute-start(f32[4,20736]{1,0:T(4,128)S(1)} %squeeze.14), channel_id=1, source_target_pairs={{0,4},{4,8},{8,12},{12,16},{16,20},{20,24},{24,28},{28,32},{32,36}... | collective-permute-start | bytes 995336 | tf_op jit(solution)/shard_map/ppermute | solution.py:17
  87.6 0.4 squeeze.11
  88.0 4.4 %collective-permute-done = f32[4,20736]{1,0:T(4,128)S(1)} collective-permute-done((f32[4,20736]{1,0:T(4,128)S(1)}, f32[4,20736]{1,0:T(4,128)S(1)}, u32[]{:S(2)}, u32[]{:S(2)}) %collective-permute-start) | collective-permute-done | bytes 331808 | tf_op jit(solution)/shard_map/ppermute | solution.py:17
  92.4 10.6 %collective-permute-done.1 = f32[4,20736]{1,0:T(4,128)S(1)} collective-permute-done((f32[4,20736]{1,0:T(4,128)S(1)}, f32[4,20736]{1,0:T(4,128)S(1)}, u32[]{:S(2)}, u32[]{:S(2)}) %collective-permute-start.1) | collective-permute-done | bytes 331808 | tf_op jit(solution)/shard_map/ppermute | solution.py:17
  103.0 2.0 %collective-permute-done.2 = f32[4,20736]{1,0:T(4,128)} collective-permute-done((f32[4,20736]{1,0:T(4,128)S(1)}, f32[4,20736]{1,0:T(4,128)}, u32[]{:S(2)}, u32[]{:S(2)}) %collective-permute-start.2) | collective-permute-done | bytes 331808 | tf_op jit(solution)/shard_map/ppermute | solution.py:17
  105.0 1.3 %pad_add_fusion = f32[7,20736]{1,0:T(8,128)S(1)} fusion(f32[4,20736]{1,0:T(4,128)} %collective-permute-done.2, f32[4,20736]{1,0:T(4,128)S(1)} %collective-permute-done.1, f32[4,20736]{1,0:T(4,128)S(1)} %collective-permute-done, f32[4,20736]{1,0:T(4,128)S(1)} %squeeze.11), kind=kLoop, calls=%fused_computation.10 | loop fusion | flops 435456 | bytes 1907712 | tf_op jit(solution)/shard_map/add | solution.py:98
  106.2 1.2 %reshape.233 = f32[1,1,7,20736]{3,1,2,0:T(1,128)} reshape(f32[7,20736]{1,0:T(8,128)S(1)} %pad_add_fusion) | data formatting | bytes 1161216 | tf_op jit(solution)/shard_map/reshape | solution.py:99
  (36 shorter events, 0.5 us)
Async XLA Ops:
  2.9 37.7 %all-to-all-start = ((f32[128,1,174]{2,1,0:T(1,128)}), f32[128,1,174]{2,1,0:T(1,128)S(1)}, u32[]{:S(2)}, u32[]{:S(2)}) async-start(f32[128,1,174]{2,1,0:T(1,128)} %copy.32), calls=%async_computation | async-start | bytes 262144 | tf_op jit(solution)/shard_map/all_to_all | solution.py:31
  41.8 12.2 %copy-start = (f32[256]{0:T(256)S(1)}, f32[256]{0:T(256)}, u32[]{:S(2)}) copy-start(f32[256]{0:T(256)} %param.9) | copy-start | bytes 3076
  76.5 15.9 %collective-permute-start = (f32[4,20736]{1,0:T(4,128)S(1)}, f32[4,20736]{1,0:T(4,128)S(1)}, u32[]{:S(2)}, u32[]{:S(2)}) collective-permute-start(f32[4,20736]{1,0:T(4,128)S(1)} %squeeze.12), channel_id=1, source_target_pairs={{0,12},{4,16},{8,20},{12,24},{16,28},{20,32},{24,36},{28,40},{32,4... | collective-permute-start | bytes 995336 | tf_op jit(solution)/shard_map/ppermute | solution.py:17
  83.2 19.8 %collective-permute-start.1 = (f32[4,20736]{1,0:T(4,128)S(1)}, f32[4,20736]{1,0:T(4,128)S(1)}, u32[]{:S(2)}, u32[]{:S(2)}) collective-permute-start(f32[4,20736]{1,0:T(4,128)S(1)} %squeeze.13), channel_id=1, source_target_pairs={{0,8},{4,12},{8,16},{12,20},{16,24},{20,28},{24,32},{28,36},{32,40... | collective-permute-start | bytes 995336 | tf_op jit(solution)/shard_map/ppermute | solution.py:17
  85.7 19.3 %collective-permute-start.2 = (f32[4,20736]{1,0:T(4,128)S(1)}, f32[4,20736]{1,0:T(4,128)}, u32[]{:S(2)}, u32[]{:S(2)}) collective-permute-start(f32[4,20736]{1,0:T(4,128)S(1)} %squeeze.14), channel_id=1, source_target_pairs={{0,4},{4,8},{8,12},{12,16},{16,20},{20,24},{24,28},{28,32},{32,36}... | collective-permute-start | bytes 995336 | tf_op jit(solution)/shard_map/ppermute | solution.py:17
where the time goes:
time: 109 us; the launch traced here: 107 us
  waiting for transfers between devices  34.2 us (31%)
  starting transfers between devices  31.5 us (29%)
  local copies, waits for them, and re-layouts  14.6 us (13%)
  other arithmetic  10.4 us (10%)
  blocking collectives  10.3 us (9%)
  matrix products  5.89 us (5%)
    all_to_all x1, starting transfers between devices, body(): got = lax.all_to_all(send, 'trk', split_axis=0, concat_axis=0, tiled=True)  20.4 us
    all_to_all x1, waiting for transfers between devices, body(): got = lax.all_to_all(send, 'trk', split_axis=0, concat_axis=0, tiled=True)  17.3 us
    ppermute x3, waiting for transfers between devices, from_behind(): return lax.ppermute(x, axis, [(i, (i + by) % size) for i in range(size)])  17 us
    ppermute x3, starting transfers between devices, from_behind(): return lax.ppermute(x, axis, [(i, (i + by) % size) for i in range(size)])  11.1 us
    all_gather x1, blocking collectives, body(): gathered = lax.all_gather(placed, 'cam', axis=1, tiled=False)  10.3 us
    reduce_sum x1, other arithmetic, panel(): return jnp.sum(sel * vals, axis=1)  5.4 us
    reduce_sum x2, local copies, waits for them, and re-layouts, panel(): return jnp.sum(sel * vals, axis=1)  5.16 us
    dot_general x1, matrix products, body(): lax.dot_general(left_flat, right_flat, (((1,), (1,)), ((), ())), precisio...  4.95 us
  transfers between devices with their start and end apart: 4, of which 4 were waited for; matrix products, arithmetic and copies ran while one was open for 0% of the time, Pallas kernels for 0%

commit v1 on v0

--- a/solution.py
+++ b/solution.py
@@ -6,6 +6,8 @@
 CAMERAS_PER_BLK = 16
 TS = 144
 HOPS = 3
+SHIFT = 2
+CAM_BY_ALL_TO_ALL = True
 
 
 HUBER_DELTA = 1.0
@@ -28,6 +30,7 @@
     nf = fields.shape[0]
     send = fields.reshape((nf, strip_count, per_dest)).transpose((1, 0, 2))
     send = send.reshape((strip_count, nf * per_dest))
+    send = jnp.roll(send, SHIFT, axis=0)
     got = lax.all_to_all(send, "trk", split_axis=0, concat_axis=0, tiled=True)
     got = got.reshape((strip_count, nf, per_dest)).transpose((1, 0, 2)).reshape((nf, rows))
     position = got[nf - 3].astype(jnp.int32)
@@ -35,8 +38,14 @@
     onehot = (position[:, None] == jnp.arange(rows, dtype=jnp.int32)[None, :]).astype(jnp.float32)
     kept = jnp.concatenate([got[: nf - 3], got[nf - 2 :]], axis=0)
     placed = jnp.dot(kept, onehot, precision=lax.Precision.HIGHEST)
-    gathered = lax.all_gather(placed, "cam", axis=1, tiled=False)
-    n_cam = gathered.shape[1]
+    if CAM_BY_ALL_TO_ALL:
+        n_cam = lax.axis_size("cam")
+        copies = jnp.broadcast_to(placed[None], (n_cam,) + placed.shape)
+        gathered = lax.all_to_all(copies, "cam", 0, 0, tiled=True).transpose((1, 0, 2))
+    else:
+        gathered = lax.all_gather(placed, "cam", axis=1, tiled=False)
+        n_cam = gathered.shape[1]
+    damping = from_behind(damping, "trk", SHIFT)
     slots = n_cam * local_slots
     g = gathered.reshape((kept.shape[0], slots, tracks))
     res = g[0:2]
@@ -62,7 +71,7 @@
         [coup[:, 0] * inv[0][l] + coup[:, 1] * inv[1][l] + coup[:, 2] * inv[2][l] for l in range(3)],
         axis=1,
     )
-    strip_index = lax.axis_index("trk")
+    strip_index = jnp.mod(lax.axis_index("trk") - SHIFT, strip_count)
     column = lax.axis_index("cam")
     visible = jnp.mod(cam // CAMERAS_PER_BLK - 2 * strip_index, 2 * strip_count)
     key = visible * CAMERAS_PER_BLK + cam % CAMERAS_PER_BLK
@@ -92,9 +101,10 @@
     tiles = product.reshape((owners, TS, owners, TS)).transpose((0, 2, 1, 3))
     tiles = tiles.reshape((owners, owners, TS * TS))
     tile_count = 2 * HOPS + 1
-    summed = jnp.pad(tiles[0], ((HOPS, 0), (0, 0)))
-    for distance in range(owners - 1, 0, -1):
-        arrived = from_behind(tiles[distance], "trk", distance)
+    summed = jnp.zeros((tile_count, TS * TS), jnp.float32)
+    for distance in range(owners - 1, -1, -1):
+        by = distance - SHIFT
+        arrived = tiles[distance] if by == 0 else from_behind(tiles[distance], "trk", by)
         summed = summed + jnp.pad(arrived, ((HOPS - distance, distance), (0, 0)))
     return summed.reshape((1, 1, tile_count, TS * TS))
 

time: 109 us -> 98.5 us (0.904)
  blocking collectives: 10.3 us -> 37.4 us
  waiting for transfers between devices: 34.2 us -> 9.05 us
  starting transfers between devices: 31.5 us -> 17.9 us
    all_to_all x0 -> x1, blocking collectives: none -> 37.4 us  [body(): got = lax.all_to_all(send, 'trk', split_axis=0, concat_axis=0, tiled=True)]
    all_to_all x1, starting transfers between devices: 20.4 us -> 4.18 us  [body(): lax.all_to_all(copies, 'cam', 0, 0, tiled=True).transpose((1, 0, 2))]
    all_to_all x1, waiting for transfers between devices: 17.3 us -> 3.13 us  [body(): lax.all_to_all(copies, 'cam', 0, 0, tiled=True).transpose((1, 0, 2))]
    ppermute x3 -> x4, waiting for transfers between devices: 17 us -> 5.92 us  [from_behind(): return lax.ppermute(x, axis, [(i, (i + by) % size) for i in range(size)])]
    all_gather x1 -> x0, blocking collectives: 10.3 us -> none  [body(): gathered = lax.all_gather(placed, 'cam', axis=1, tiled=False)]
    ppermute x3 -> x4, starting transfers between devices: 11.1 us -> 13.8 us  [from_behind(): return lax.ppermute(x, axis, [(i, (i + by) % size) for i in range(size)])]
  transfers between devices with their start and end apart: 4 -> 5, of which waited for: 4 -> 2; matrix products, arithmetic and copies ran while one was open for 0% -> 2% of each run, Pallas kernels for 0% -> 0%
where the time goes in v1:
time: 98.5 us; the launch traced here: 96.9 us
  blocking collectives  37.4 us (38%)
  starting transfers between devices  17.9 us (18%)
  local copies, waits for them, and re-layouts  15.5 us (16%)
  other arithmetic  10.5 us (11%)
  waiting for transfers between devices  9.05 us (9%)
  matrix products  5.89 us (6%)
    all_to_all x1, blocking collectives, body(): got = lax.all_to_all(send, 'trk', split_axis=0, concat_axis=0, tiled=True)  37.4 us
    ppermute x4, starting transfers between devices, from_behind(): return lax.ppermute(x, axis, [(i, (i + by) % size) for i in range(size)])  13.8 us
    ppermute x4, waiting for transfers between devices, from_behind(): return lax.ppermute(x, axis, [(i, (i + by) % size) for i in range(size)])  5.92 us
    reduce_sum x1, other arithmetic, panel(): return jnp.sum(sel * vals, axis=1)  5.4 us
    reduce_sum x2, local copies, waits for them, and re-layouts, panel(): return jnp.sum(sel * vals, axis=1)  5.16 us
    dot_general x1, matrix products, body(): lax.dot_general(left_flat, right_flat, (((1,), (1,)), ((), ())), precisio...  4.95 us
    all_to_all x1, starting transfers between devices, body(): lax.all_to_all(copies, 'cam', 0, 0, tiled=True).transpose((1, 0, 2))  4.18 us
    all_to_all x1, waiting for transfers between devices, body(): lax.all_to_all(copies, 'cam', 0, 0, tiled=True).transpose((1, 0, 2))  3.13 us
  transfers between devices with their start and end apart: 5, of which 2 were waited for; matrix products, arithmetic and copies ran while one was open for 2% of the time, Pallas kernels for 0%

profile of v1, /device:TPU:1, one launch (start us, length us, event | category | flops | bytes accessed | tf_op | source)
XLA Modules:
  0.0 96.9 jit_solution(13683238585455690315)
XLA Ops:
  0.0 0.7 convert_element_type.46
  0.7 0.9 pad_maximum_fusion
  1.6 0.2 copy.54
  1.9 0.2 copy.56
  2.2 0.1 copy.55
  2.3 0.1 slice.156
  2.4 0.1 copy.57
  2.5 0.1 maximum_bitcast_fusion.1
  2.6 0.1 copy.58
  2.8 37.4 %all_to_all.14 = f32[128,1,174]{2,1,0:T(1,128)S(1)} all-to-all(f32[128,1,174]{2,1,0:T(1,128)S(1)} %copy.58), channel_id=1, replica_groups=mesh['trk'=128,'cam'=4] {'trk'}, dimensions={0} | all-to-all | bytes 178176 | tf_op jit(solution)/shard_map/all_to_all | solution.py:34
  40.2 0.1 copy.59
  40.4 0.1 copy.63
  40.5 0.1 convert_element_type.48
  40.6 0.1 copy.61
  40.7 0.1 slice.162
  40.9 0.3 copy.60
  41.2 0.2 copy.62
  41.4 0.9 fusion
  42.3 0.8 broadcast_in_dim.12
  43.1 4.2 %all-to-all-start.1 = ((f32[4,28,768]{2,1,0:T(8,128)}), f32[4,28,768]{2,1,0:T(8,128)S(1)}, u32[]{:S(2)}, u32[]{:S(2)}) async-start(f32[4,28,768]{2,1,0:T(8,128)} %broadcast_in_dim.12), calls=%async_computation.1 | async-start | bytes 786432 | tf_op jit(solution)/shard_map/all_to_all | solution.py:44
  47.3 3.0 %collective-permute-start = (f32[256]{0:T(256)S(1)}, f32[256]{0:T(256)S(1)}, u32[]{:S(2)}, u32[]{:S(2)}) collective-permute-start(f32[256]{0:T(256)S(1)} %copy-done), channel_id=1, source_target_pairs={{0,8},{4,12},{8,16},{12,20},{16,24},{20,28},{24,32},{28,36},{32,40... | collective-permute-start | bytes 3080 | tf_op jit(solution)/shard_map/ppermute | solution.py:19
  50.4 3.1 %all-to-all-done.1 = f32[4,28,768]{2,1,0:T(8,128)S(1)} async-done(((f32[4,28,768]{2,1,0:T(8,128)}), f32[4,28,768]{2,1,0:T(8,128)S(1)}, u32[]{:S(2)}, u32[]{:S(2)}) %all-to-all-start.1) | async-done | bytes 344096 | tf_op jit(solution)/shard_map/all_to_all | solution.py:44
  53.6 0.3 add_reduce_fusion.4
  54.5 0.1 add_multiply_fusion.1
  55.0 0.5 multiply_add_fusion.2
  55.6 0.3 maximum_bitcast_fusion
  55.9 0.2 broadcast_in_dim.14
  56.2 0.1 mul.554
  56.2 0.2 mul.555
  56.6 0.2 mul.561
  56.8 0.6 compare_convert_fusion.1
  57.4 5.4 %multiply_reduce_fusion = (f32[64,9,768]{2,0,1:T(8,128)}, f32[64,9,768]{2,0,1:T(8,128)}) fusion(f32[9,12,768]{2,1,0:T(8,128)S(1)} %add_multiply_fusion, f32[64,12,768]{2,0,1:T(8,128)S(1)} %get-tuple-element.33, f32[9,12,768]{2,1,0:T(8,128)S(1)} %broadcast_in_dim.14, f32[64,12,768]{2,0,1:T(8,128)S(1)} %get-tuple-element.32), kind=kLoop, calls=%fused_computation | loop fusion | flops 20348928 | bytes 8921088 | tf_op jit(solution)/shard_map/reduce_sum | solution.py:94
  62.9 2.6 %copy.73 = f32[64,9,768]{2,1,0:T(8,128)S(1)} copy(f32[64,9,768]{2,0,1:T(8,128)} %get-tuple-element.39) | data formatting | bytes 3538944 | tf_op jit(solution)/shard_map/reduce_sum | solution.py:94
  65.4 1.6 %reshape.240 = f32[4,144,768,1]{2,1,0,3:T(8,128)} reshape(f32[64,9,768]{2,1,0:T(8,128)S(1)} %copy.73) | data formatting | bytes 3538944 | tf_op jit(solution)/shard_map/dot_general | solution.py:98
  67.0 2.6 %copy.70 = f32[64,9,768]{2,1,0:T(8,128)S(1)} copy(f32[64,9,768]{2,0,1:T(8,128)} %get-tuple-element.40) | data formatting | bytes 3538944 | tf_op jit(solution)/shard_map/reduce_sum | solution.py:94
  69.6 1.4 %reshape.239 = f32[4,144,768,1]{2,1,0,3:T(8,128)} reshape(f32[64,9,768]{2,1,0:T(8,128)S(1)} %copy.70) | data formatting | bytes 3538944 | tf_op jit(solution)/shard_map/dot_general | solution.py:98
  71.0 5.0 %fusion.3 = f32[4,4,144,144]{3,2,1,0:T(8,128)S(1)} fusion(f32[4,144,768,1]{2,1,0,3:T(8,128)} %reshape.240, f32[4,144,768,1]{2,1,0,3:T(8,128)} %reshape.239), kind=kOutput, calls=%fused_computation.8 | convolution fusion | flops 1528823808 | bytes 4866048 | tf_op jit(solution)/shard_map/dot_general | solution.py:98
  76.0 0.2 fusion.24
  76.1 0.4 squeeze.11
  76.5 0.4 squeeze.14
  77.0 0.4 squeeze.13
  77.4 5.3 %collective-permute-start.2 = (f32[4,20736]{1,0:T(4,128)S(1)}, f32[4,20736]{1,0:T(4,128)S(1)}, u32[]{:S(2)}, u32[]{:S(2)}) collective-permute-start(f32[4,20736]{1,0:T(4,128)S(1)} %squeeze.13), channel_id=1, source_target_pairs={{0,508},{4,0},{8,4},{12,8},{16,12},{20,16},{24,20},{28,24},{32,28}... | collective-permute-start | bytes 995336 | tf_op jit(solution)/shard_map/ppermute | solution.py:19
  82.6 3.2 %collective-permute-start.3 = (f32[4,20736]{1,0:T(4,128)S(1)}, f32[4,20736]{1,0:T(4,128)S(1)}, u32[]{:S(2)}, u32[]{:S(2)}) collective-permute-start(f32[4,20736]{1,0:T(4,128)S(1)} %squeeze.14), channel_id=1, source_target_pairs={{0,504},{4,508},{8,0},{12,4},{16,8},{20,12},{24,16},{28,20},{32,24... | collective-permute-start | bytes 995336 | tf_op jit(solution)/shard_map/ppermute | solution.py:19
  85.9 2.2 %collective-permute-start.1 = (f32[4,20736]{1,0:T(4,128)S(1)}, f32[4,20736]{1,0:T(4,128)}, u32[]{:S(2)}, u32[]{:S(2)}) collective-permute-start(f32[4,20736]{1,0:T(4,128)S(1)} %squeeze.11), channel_id=1, source_target_pairs={{0,4},{4,8},{8,12},{12,16},{16,20},{20,24},{24,28},{28,32},{32,36}... | collective-permute-start | bytes 995336 | tf_op jit(solution)/shard_map/ppermute | solution.py:19
  88.1 0.4 squeeze.12
  88.6 5.9 %collective-permute-done.3 = f32[4,20736]{1,0:T(4,128)S(1)} collective-permute-done((f32[4,20736]{1,0:T(4,128)S(1)}, f32[4,20736]{1,0:T(4,128)S(1)}, u32[]{:S(2)}, u32[]{:S(2)}) %collective-permute-start.3) | collective-permute-done | bytes 331808 | tf_op jit(solution)/shard_map/ppermute | solution.py:19
  94.5 1.3 %pad_add_fusion = f32[7,20736]{1,0:T(8,128)S(1)} fusion(f32[4,20736]{1,0:T(4,128)S(1)} %collective-permute-done.3, f32[4,20736]{1,0:T(4,128)S(1)} %collective-permute-done.2, f32[4,20736]{1,0:T(4,128)S(1)} %squeeze.12, f32[4,20736]{1,0:T(4,128)} %collective-permute-done.1), kind=kLoop, calls=%fused_computation.10 | loop fusion | flops 435456 | bytes 1907712 | tf_op jit(solution)/shard_map/add | solution.py:108
  95.7 1.2 %reshape.235 = f32[1,1,7,20736]{3,1,2,0:T(1,128)} reshape(f32[7,20736]{1,0:T(8,128)S(1)} %pad_add_fusion) | data formatting | bytes 1161216 | tf_op jit(solution)/shard_map/reshape | solution.py:109
  (53 shorter events, 1.2 us)
Async XLA Ops:
  40.3 7.0 %copy-start = (f32[256]{0:T(256)S(1)}, f32[256]{0:T(256)}, u32[]{:S(2)}) copy-start(f32[256]{0:T(256)} %param.9) | copy-start | bytes 3076
  43.1 10.4 %all-to-all-start.1 = ((f32[4,28,768]{2,1,0:T(8,128)}), f32[4,28,768]{2,1,0:T(8,128)S(1)}, u32[]{:S(2)}, u32[]{:S(2)}) async-start(f32[4,28,768]{2,1,0:T(8,128)} %broadcast_in_dim.12), calls=%async_computation.1 | async-start | bytes 786432 | tf_op jit(solution)/shard_map/all_to_all | solution.py:44
  47.3 7.7 %collective-permute-start = (f32[256]{0:T(256)S(1)}, f32[256]{0:T(256)S(1)}, u32[]{:S(2)}, u32[]{:S(2)}) collective-permute-start(f32[256]{0:T(256)S(1)} %copy-done), channel_id=1, source_target_pairs={{0,8},{4,12},{8,16},{12,20},{16,24},{20,28},{24,32},{28,36},{32,40... | collective-permute-start | bytes 3080 | tf_op jit(solution)/shard_map/ppermute | solution.py:19
  77.4 11.2 %collective-permute-start.2 = (f32[4,20736]{1,0:T(4,128)S(1)}, f32[4,20736]{1,0:T(4,128)S(1)}, u32[]{:S(2)}, u32[]{:S(2)}) collective-permute-start(f32[4,20736]{1,0:T(4,128)S(1)} %squeeze.13), channel_id=1, source_target_pairs={{0,508},{4,0},{8,4},{12,8},{16,12},{20,16},{24,20},{28,24},{32,28}... | collective-permute-start | bytes 995336 | tf_op jit(solution)/shard_map/ppermute | solution.py:19
  82.6 11.8 %collective-permute-start.3 = (f32[4,20736]{1,0:T(4,128)S(1)}, f32[4,20736]{1,0:T(4,128)S(1)}, u32[]{:S(2)}, u32[]{:S(2)}) collective-permute-start(f32[4,20736]{1,0:T(4,128)S(1)} %squeeze.14), channel_id=1, source_target_pairs={{0,504},{4,508},{8,0},{12,4},{16,8},{20,12},{24,16},{28,20},{32,24... | collective-permute-start | bytes 995336 | tf_op jit(solution)/shard_map/ppermute | solution.py:19
  85.9 8.6 %collective-permute-start.1 = (f32[4,20736]{1,0:T(4,128)S(1)}, f32[4,20736]{1,0:T(4,128)}, u32[]{:S(2)}, u32[]{:S(2)}) collective-permute-start(f32[4,20736]{1,0:T(4,128)S(1)} %squeeze.11), channel_id=1, source_target_pairs={{0,4},{4,8},{8,12},{12,16},{16,20},{20,24},{24,28},{28,32},{32,36}... | collective-permute-start | bytes 995336 | tf_op jit(solution)/shard_map/ppermute | solution.py:19

commit v2 on v1

--- a/solution.py
+++ b/solution.py
@@ -85,16 +85,16 @@
     key3 = jnp.tile(key, (1, 3))
     groups = owners * CAMERAS_PER_BLK
     width = owners * TS
-    full = (groups, 9, slots, 3 * tracks)
 
     def panel(keys, values):
         sel = (key3[None] == keys[:, None, None]).astype(jnp.float32)
-        sel = jnp.broadcast_to(sel[:, None], full).reshape((width, slots, 3 * tracks))
-        vals = jnp.broadcast_to(values[None], full).reshape((width, slots, 3 * tracks))
-        return jnp.sum(sel * vals, axis=1)
+        return jnp.sum(sel[None] * values[:, None], axis=2).reshape((width, 3 * tracks))
 
-    left_flat = panel(key_left, left3)
-    right_flat = panel(key_right, coup3)
+    new_row = jnp.arange(width, dtype=jnp.int32)
+    old_row = (new_row % 9) * groups + new_row // 9
+    reorder = (old_row[:, None] == jnp.arange(width, dtype=jnp.int32)[None, :]).astype(jnp.float32)
+    left_flat = jnp.dot(reorder, panel(key_left, left3), precision=lax.Precision.HIGH)
+    right_flat = jnp.dot(reorder, panel(key_right, coup3), precision=lax.Precision.HIGH)
     product = lax.dot_general(
         left_flat, right_flat, (((1,), (1,)), ((), ())), precision=lax.Precision.HIGH
     )

time: 98.5 us -> 106 us (1.076)
  blocking collectives: 37.4 us -> 0 us
  starting transfers between devices: 17.9 us -> 41.5 us
  waiting for transfers between devices: 9.05 us -> 27.3 us
  matrix products: 5.89 us -> 9.44 us
  other arithmetic: 10.5 us -> 12.8 us
  local copies, waits for them, and re-layouts: 15.5 us -> 13.4 us
    all_to_all x1 -> x0, blocking collectives: 37.4 us -> none  [body(): got = lax.all_to_all(send, 'trk', split_axis=0, concat_axis=0, tiled=True)]
    all_to_all x0 -> x1, starting transfers between devices: none -> 20.4 us  [body(): got = lax.all_to_all(send, 'trk', split_axis=0, concat_axis=0, tiled=True)]
    all_to_all x0 -> x1, waiting for transfers between devices: none -> 14 us  [body(): got = lax.all_to_all(send, 'trk', split_axis=0, concat_axis=0, tiled=True)]
    reduce_sum x2 -> x0, local copies, waits for them, and re-layouts: 5.16 us -> none  [panel(): return jnp.sum(sel * vals, axis=1)]
    dot_general x0 -> x2, matrix products: none -> 4.75 us  [the longest x1 3.11 us: body(): jnp.dot(reorder, panel(key_right, coup3), precision=lax.Precision.HIGH)]
    ppermute x4, starting transfers between devices: 13.8 us -> 16.9 us  [from_behind(): return lax.ppermute(x, axis, [(i, (i + by) % size) for i in range(size)])]
    reshape x0 -> x1, local copies, waits for them, and re-layouts: none -> 3.1 us  [body(): tiles = product.reshape((owners, TS, owners, TS)).transpose((0, 2, 1, 3))]
    all_to_all x1, waiting for transfers between devices: 3.13 us -> 6.2 us  [body(): lax.all_to_all(copies, 'cam', 0, 0, tiled=True).transpose((1, 0, 2))]
  transfers between devices with their start and end apart: 5 -> 6, of which waited for: 2 -> 4; matrix products, arithmetic and copies ran while one was open for 2% -> 5% of each run, Pallas kernels for 0% -> 0%
where the time goes in v2:
time: 106 us; the launch traced here: 105 us
  starting transfers between devices  41.5 us (39%)
  waiting for transfers between devices  27.3 us (26%)
  local copies, waits for them, and re-layouts  13.4 us (13%)
  other arithmetic  12.8 us (12%)
  matrix products  9.44 us (9%)
    all_to_all x1, starting transfers between devices, body(): got = lax.all_to_all(send, 'trk', split_axis=0, concat_axis=0, tiled=True)  20.4 us
    ppermute x4, starting transfers between devices, from_behind(): return lax.ppermute(x, axis, [(i, (i + by) % size) for i in range(size)])  16.9 us
    all_to_all x1, waiting for transfers between devices, body(): got = lax.all_to_all(send, 'trk', split_axis=0, concat_axis=0, tiled=True)  14 us
    ppermute x4, waiting for transfers between devices, from_behind(): return lax.ppermute(x, axis, [(i, (i + by) % size) for i in range(size)])  7.04 us
    reduce_sum x1, other arithmetic, panel(): jnp.sum(sel[None] * values[:, None], axis=2).reshape((width, 3 * tracks))  6.81 us
    all_to_all x1, waiting for transfers between devices, body(): lax.all_to_all(copies, 'cam', 0, 0, tiled=True).transpose((1, 0, 2))  6.2 us
    all_to_all x1, starting transfers between devices, body(): lax.all_to_all(copies, 'cam', 0, 0, tiled=True).transpose((1, 0, 2))  4.18 us
    dot_general x1, matrix products, body(): lax.dot_general(left_flat, right_flat, (((1,), (1,)), ((), ())), precisio...  3.76 us
  transfers between devices with their start and end apart: 6, of which 4 were waited for; matrix products, arithmetic and copies ran while one was open for 5% of the time, Pallas kernels for 0%

profile of v2, /device:TPU:1, one launch (start us, length us, event | category | flops | bytes accessed | tf_op | source)
XLA Modules:
  0.0 105.0 jit_solution(1006127471944514340)
XLA Ops:
  0.0 0.7 convert_element_type.47
  0.7 0.9 pad_maximum_fusion
  1.6 0.2 copy.74
  1.9 0.2 copy.76
  2.4 0.1 copy.77
  2.6 0.8 copy.78
  3.4 20.4 %all-to-all-start = ((f32[128,1,174]{2,1,0:T(1,128)}), f32[128,1,174]{2,1,0:T(1,128)S(1)}, u32[]{:S(2)}, u32[]{:S(2)}) async-start(f32[128,1,174]{2,1,0:T(1,128)} %copy.78), calls=%async_computation | async-start | bytes 262144 | tf_op jit(solution)/shard_map/all_to_all | solution.py:34
  23.8 3.3 %collective-permute-start = (f32[256]{0:T(256)S(1)}, f32[256]{0:T(256)S(1)}, u32[]{:S(2)}, u32[]{:S(2)}) collective-permute-start(f32[256]{0:T(256)S(1)} %copy-done.1), channel_id=1, source_target_pairs={{0,8},{4,12},{8,16},{12,20},{16,24},{20,28},{24,32},{28,36},{32,40... | collective-permute-start | bytes 3080 | tf_op jit(solution)/shard_map/ppermute | solution.py:19
  27.1 14.0 %all-to-all-done = f32[128,1,174]{2,1,0:T(1,128)S(1)} async-done(((f32[128,1,174]{2,1,0:T(1,128)}), f32[128,1,174]{2,1,0:T(1,128)S(1)}, u32[]{:S(2)}, u32[]{:S(2)}) %all-to-all-start) | async-done | bytes 89120 | tf_op jit(solution)/shard_map/all_to_all | solution.py:34
  41.3 0.3 copy.80
  41.6 0.2 copy.82
  41.7 0.1 copy.81
  41.9 0.1 slice.162
  42.2 0.1 convert_element_type.49
  42.3 0.9 fusion
  43.2 0.8 broadcast_in_dim.2
  44.0 4.2 %all-to-all-start.1 = ((f32[4,28,768]{2,1,0:T(8,128)}), f32[4,28,768]{2,1,0:T(8,128)S(1)}, u32[]{:S(2)}, u32[]{:S(2)}) async-start(f32[4,28,768]{2,1,0:T(8,128)} %broadcast_in_dim.2), calls=%async_computation.1 | async-start | bytes 786432 | tf_op jit(solution)/shard_map/all_to_all | solution.py:44
  48.2 6.2 %all-to-all-done.1 = f32[4,28,768]{2,1,0:T(8,128)S(1)} async-done(((f32[4,28,768]{2,1,0:T(8,128)}), f32[4,28,768]{2,1,0:T(8,128)S(1)}, u32[]{:S(2)}, u32[]{:S(2)}) %all-to-all-start.1) | async-done | bytes 344096 | tf_op jit(solution)/shard_map/all_to_all | solution.py:44
  54.4 0.3 add_reduce_fusion.4
  55.3 0.1 add_multiply_fusion.1
  55.6 0.5 multiply_add_fusion.2
  56.1 0.3 maximum_bitcast_fusion
  56.4 1.0 mul.587
  57.7 0.2 mul.593
  58.0 0.2 mul.599
  58.5 0.6 compare_convert_fusion
  59.0 0.8 add_multiply_fusion
  59.9 6.8 %multiply_reduce_fusion = (f32[9,64,768]{2,1,0:T(8,128)}, f32[9,64,768]{2,1,0:T(8,128)S(1)}) fusion(f32[9,12,768]{2,1,0:T(8,128)} %add_multiply_fusion, f32[64,12,768]{2,0,1:T(8,128)S(1)} %get-tuple-element.32, f32[9,12,768]{2,1,0:T(8,128)} %mul.587, f32[64,12,768]{2,0,1:T(8,128)S(1)} %get-tuple-element.33), kind=kLoop, calls=%fused_computation | loop fusion | flops 20348928 | bytes 8921088 | tf_op jit(solution)/shard_map/reduce_sum | solution.py:91
  66.7 3.1 %fusion.1 = f32[576,768]{1,0:T(8,128)S(1)} fusion(f32[576,768]{1,0:T(8,128)} %bitcast.48, s32[576]{0:T(1024)S(1)} %fusion.23), kind=kOutput, calls=%fused_computation.7 | convolution fusion | flops 1529155584 | bytes 3541248 | tf_op jit(solution)/shard_map/dot_general | solution.py:97
  69.8 1.6 %fusion.2 = f32[576,768]{1,0:T(8,128)S(1)} fusion(f32[576,768]{1,0:T(8,128)S(1)} %bitcast.47, s32[576]{0:T(1024)S(1)} %fusion.23), kind=kOutput, calls=%fused_computation.8 | convolution fusion | flops 1529155584 | bytes 3541248 | tf_op jit(solution)/shard_map/dot_general | solution.py:96
  71.5 3.8 %fusion.35 = f32[576,576]{1,0:T(8,128)} fusion(f32[576,768]{1,0:T(8,128)S(1)} %fusion.2, f32[576,768]{1,0:T(8,128)S(1)} %fusion.1), kind=kOutput, calls=%fused_computation.94 | convolution fusion | flops 1528823808 | bytes 4866048 | tf_op jit(solution)/shard_map/dot_general | solution.py:98
  75.2 3.1 %reshape.254 = f32[4,144,4,144]{3,2,1,0:T(4,128)S(1)} reshape(f32[576,576]{1,0:T(8,128)} %fusion.35) | data formatting | bytes 2654208 | tf_op jit(solution)/shard_map/reshape | solution.py:101
  78.3 1.2 %fusion.32 = (f32[1,4,144,144]{3,1,2,0:T(4,128)S(1)}, f32[1,4,144,144]{3,1,2,0:T(4,128)S(1)}, f32[1,4,144,144]{3,1,2,0:T(4,128)}, f32[1,4,144,144]{3,1,2,0:T(4,128)S(1)}) fusion(f32[4,4,144,144]{3,1,2,0:T(4,128)S(1)} %bitcast.46), kind=kLoop, calls=%fused_computation.91 | loop fusion | bytes 2654208 | tf_op jit(solution)/shard_map/slice | solution.py:107
  79.5 0.1 copy.92
  79.7 0.4 squeeze.11
  80.1 5.5 %collective-permute-start.1 = (f32[4,20736]{1,0:T(4,128)S(1)}, f32[4,20736]{1,0:T(4,128)}, u32[]{:S(2)}, u32[]{:S(2)}) collective-permute-start(f32[4,20736]{1,0:T(4,128)S(1)} %squeeze.11), channel_id=1, source_target_pairs={{0,4},{4,8},{8,12},{12,16},{16,20},{20,24},{24,28},{28,32},{32,36}... | collective-permute-start | bytes 995336 | tf_op jit(solution)/shard_map/ppermute | solution.py:19
  85.6 0.1 copy.94
  85.7 0.4 squeeze.13
  86.1 1.9 %collective-permute-start.2 = (f32[4,20736]{1,0:T(4,128)S(1)}, f32[4,20736]{1,0:T(4,128)}, u32[]{:S(2)}, u32[]{:S(2)}) collective-permute-start(f32[4,20736]{1,0:T(4,128)S(1)} %squeeze.13), channel_id=1, source_target_pairs={{0,508},{4,0},{8,4},{12,8},{16,12},{20,16},{24,20},{28,24},{32,28}... | collective-permute-start | bytes 995336 | tf_op jit(solution)/shard_map/ppermute | solution.py:19
  88.1 0.1 copy.95
  88.2 0.4 squeeze.14
  88.6 6.3 %collective-permute-start.3 = (f32[4,20736]{1,0:T(4,128)S(1)}, f32[4,20736]{1,0:T(4,128)S(1)}, u32[]{:S(2)}, u32[]{:S(2)}) collective-permute-start(f32[4,20736]{1,0:T(4,128)S(1)} %squeeze.14), channel_id=1, source_target_pairs={{0,504},{4,508},{8,0},{12,4},{16,8},{20,12},{24,16},{28,20},{32,24... | collective-permute-start | bytes 995336 | tf_op jit(solution)/shard_map/ppermute | solution.py:19
  94.9 0.1 copy.93
  95.0 0.4 squeeze.12
  95.4 0.9 collective-permute-done.2
  96.3 6.1 %collective-permute-done.3 = f32[4,20736]{1,0:T(4,128)S(1)} collective-permute-done((f32[4,20736]{1,0:T(4,128)S(1)}, f32[4,20736]{1,0:T(4,128)S(1)}, u32[]{:S(2)}, u32[]{:S(2)}) %collective-permute-start.3) | collective-permute-done | bytes 331808 | tf_op jit(solution)/shard_map/ppermute | solution.py:19
  102.5 1.4 %pad_add_fusion = f32[7,20736]{1,0:T(8,128)S(1)} fusion(f32[4,20736]{1,0:T(4,128)S(1)} %collective-permute-done.3, f32[4,20736]{1,0:T(4,128)} %collective-permute-done.2, f32[4,20736]{1,0:T(4,128)S(1)} %squeeze.12, f32[4,20736]{1,0:T(4,128)} %collective-permute-done.1), kind=kLoop, calls=%fused_computation.12 | loop fusion | flops 435456 | bytes 1907712 | tf_op jit(solution)/shard_map/add | solution.py:108
  103.8 1.2 %reshape.255 = f32[1,1,7,20736]{3,1,2,0:T(1,128)} reshape(f32[7,20736]{1,0:T(8,128)S(1)} %pad_add_fusion) | data formatting | bytes 1161216 | tf_op jit(solution)/shard_map/reshape | solution.py:109
  (60 shorter events, 1.7 us)
Async XLA Ops:
  1.8 22.0 %copy-start.1 = (f32[256]{0:T(256)S(1)}, f32[256]{0:T(256)}, u32[]{:S(2)}) copy-start(f32[256]{0:T(256)} %param.9) | copy-start | bytes 3076
  3.4 37.7 %all-to-all-start = ((f32[128,1,174]{2,1,0:T(1,128)}), f32[128,1,174]{2,1,0:T(1,128)S(1)}, u32[]{:S(2)}, u32[]{:S(2)}) async-start(f32[128,1,174]{2,1,0:T(1,128)} %copy.78), calls=%async_computation | async-start | bytes 262144 | tf_op jit(solution)/shard_map/all_to_all | solution.py:34
  23.8 31.7 %collective-permute-start = (f32[256]{0:T(256)S(1)}, f32[256]{0:T(256)S(1)}, u32[]{:S(2)}, u32[]{:S(2)}) collective-permute-start(f32[256]{0:T(256)S(1)} %copy-done.1), channel_id=1, source_target_pairs={{0,8},{4,12},{8,16},{12,20},{16,24},{20,28},{24,32},{28,36},{32,40... | collective-permute-start | bytes 3080 | tf_op jit(solution)/shard_map/ppermute | solution.py:19
  44.0 10.4 %all-to-all-start.1 = ((f32[4,28,768]{2,1,0:T(8,128)}), f32[4,28,768]{2,1,0:T(8,128)S(1)}, u32[]{:S(2)}, u32[]{:S(2)}) async-start(f32[4,28,768]{2,1,0:T(8,128)} %broadcast_in_dim.2), calls=%async_computation.1 | async-start | bytes 786432 | tf_op jit(solution)/shard_map/all_to_all | solution.py:44
  79.5 6.0 %copy-start = (f32[1,4,144,144]{3,1,2,0:T(4,128)S(1)}, f32[1,4,144,144]{3,1,2,0:T(4,128)}, u32[]{:S(2)}) copy-start(f32[1,4,144,144]{3,1,2,0:T(4,128)} %get-tuple-element.22) | copy-start | bytes 995332
  80.1 15.3 %collective-permute-start.1 = (f32[4,20736]{1,0:T(4,128)S(1)}, f32[4,20736]{1,0:T(4,128)}, u32[]{:S(2)}, u32[]{:S(2)}) collective-permute-start(f32[4,20736]{1,0:T(4,128)S(1)} %squeeze.11), channel_id=1, source_target_pairs={{0,4},{4,8},{8,12},{12,16},{16,20},{20,24},{24,28},{28,32},{32,36}... | collective-permute-start | bytes 995336 | tf_op jit(solution)/shard_map/ppermute | solution.py:19
  86.1 10.2 %collective-permute-start.2 = (f32[4,20736]{1,0:T(4,128)S(1)}, f32[4,20736]{1,0:T(4,128)}, u32[]{:S(2)}, u32[]{:S(2)}) collective-permute-start(f32[4,20736]{1,0:T(4,128)S(1)} %squeeze.13), channel_id=1, source_target_pairs={{0,508},{4,0},{8,4},{12,8},{16,12},{20,16},{24,20},{28,24},{32,28}... | collective-permute-start | bytes 995336 | tf_op jit(solution)/shard_map/ppermute | solution.py:19
  88.6 13.9 %collective-permute-start.3 = (f32[4,20736]{1,0:T(4,128)S(1)}, f32[4,20736]{1,0:T(4,128)S(1)}, u32[]{:S(2)}, u32[]{:S(2)}) collective-permute-start(f32[4,20736]{1,0:T(4,128)S(1)} %squeeze.14), channel_id=1, source_target_pairs={{0,504},{4,508},{8,0},{12,4},{16,8},{20,12},{24,16},{28,20},{32,24... | collective-permute-start | bytes 995336 | tf_op jit(solution)/shard_map/ppermute | solution.py:19

commit v3 on v2

--- a/solution.py
+++ b/solution.py
@@ -95,10 +95,9 @@
     reorder = (old_row[:, None] == jnp.arange(width, dtype=jnp.int32)[None, :]).astype(jnp.float32)
     left_flat = jnp.dot(reorder, panel(key_left, left3), precision=lax.Precision.HIGH)
     right_flat = jnp.dot(reorder, panel(key_right, coup3), precision=lax.Precision.HIGH)
-    product = lax.dot_general(
-        left_flat, right_flat, (((1,), (1,)), ((), ())), precision=lax.Precision.HIGH
-    )
-    tiles = product.reshape((owners, TS, owners, TS)).transpose((0, 2, 1, 3))
+    left4 = left_flat.reshape((owners, TS, 3 * tracks))
+    right4 = right_flat.reshape((owners, TS, 3 * tracks))
+    tiles = jnp.einsum("kic,mjc->kmij", left4, right4, precision=lax.Precision.HIGH)
     tiles = tiles.reshape((owners, owners, TS * TS))
     tile_count = 2 * HOPS + 1
     summed = jnp.zeros((tile_count, TS * TS), jnp.float32)

time: 106 us -> 101 us (0.953)
  local copies, waits for them, and re-layouts: 13.4 us -> 10.1 us
    reshape x1 -> x0, local copies, waits for them, and re-layouts: 3.1 us -> none  [body(): tiles = product.reshape((owners, TS, owners, TS)).transpose((0, 2, 1, 3))]
    dot_general x1, matrix products: 3.11 us -> 1.64 us  [body(): jnp.dot(reorder, panel(key_right, coup3), precision=lax.Precision.HIGH)]
    dot_general x1, matrix products: 1.65 us -> 3.1 us  [body(): jnp.dot(reorder, panel(key_left, left3), precision=lax.Precision.HIGH)]
    reshape x0 -> x1, other arithmetic: none -> 1.36 us  [body(): return summed.reshape((1, 1, tile_count, TS * TS))]
    add x1 -> x0, other arithmetic: 1.36 us -> none  [body(): summed = summed + jnp.pad(arrived, ((HOPS - distance, distance), (0, 0)))]
  transfers between devices with their start and end apart: 6 -> 6, of which waited for: 4 -> 4; matrix products, arithmetic and copies ran while one was open for 5% -> 6% of each run, Pallas kernels for 0% -> 0%
where the time goes in v3:
time: 101 us
  starting transfers between devices  41.5 us (41%)
  waiting for transfers between devices  27.1 us (27%)
  other arithmetic  12.8 us (13%)
  local copies, waits for them, and re-layouts  10.1 us (10%)
  matrix products  8.89 us (9%)
    all_to_all x1, starting transfers between devices, body(): got = lax.all_to_all(send, 'trk', split_axis=0, concat_axis=0, tiled=True)  20.4 us
    ppermute x4, starting transfers between devices, from_behind(): return lax.ppermute(x, axis, [(i, (i + by) % size) for i in range(size)])  16.9 us
    all_to_all x1, waiting for transfers between devices, body(): got = lax.all_to_all(send, 'trk', split_axis=0, concat_axis=0, tiled=True)  14 us
    ppermute x4, waiting for transfers between devices, from_behind(): return lax.ppermute(x, axis, [(i, (i + by) % size) for i in range(size)])  6.86 us
    reduce_sum x1, other arithmetic, panel(): jnp.sum(sel[None] * values[:, None], axis=2).reshape((width, 3 * tracks))  6.81 us
    all_to_all x1, waiting for transfers between devices, body(): lax.all_to_all(copies, 'cam', 0, 0, tiled=True).transpose((1, 0, 2))  6.19 us
    all_to_all x1, starting transfers between devices, body(): lax.all_to_all(copies, 'cam', 0, 0, tiled=True).transpose((1, 0, 2))  4.18 us
    dot_general x1, matrix products, body(): jnp.einsum('kic,mjc->kmij', left4, right4, precision=lax.Precision.HIGH)  3.22 us
  transfers between devices with their start and end apart: 6, of which 4 were waited for; matrix products, arithmetic and copies ran while one was open for 6% of the time, Pallas kernels for 0%

profile of v3, /device:TPU:1, one launch (start us, length us, event | category | flops | bytes accessed | tf_op | source)
XLA Modules:
  0.0 101.0 jit_solution(17675877627766350162)
XLA Ops:
  0.0 0.7 convert_element_type.47
  0.7 0.9 pad_maximum_fusion
  1.6 0.2 copy.73
  1.9 0.2 copy.75
  2.4 0.1 copy.76
  2.6 0.8 copy.77
  3.4 20.4 %all-to-all-start = ((f32[128,1,174]{2,1,0:T(1,128)}), f32[128,1,174]{2,1,0:T(1,128)S(1)}, u32[]{:S(2)}, u32[]{:S(2)}) async-start(f32[128,1,174]{2,1,0:T(1,128)} %copy.77), calls=%async_computation | async-start | bytes 262144 | tf_op jit(solution)/shard_map/all_to_all | solution.py:34
  23.8 3.3 %collective-permute-start = (f32[256]{0:T(256)S(1)}, f32[256]{0:T(256)S(1)}, u32[]{:S(2)}, u32[]{:S(2)}) collective-permute-start(f32[256]{0:T(256)S(1)} %copy-done), channel_id=1, source_target_pairs={{0,8},{4,12},{8,16},{12,20},{16,24},{20,28},{24,32},{28,36},{32,40... | collective-permute-start | bytes 3080 | tf_op jit(solution)/shard_map/ppermute | solution.py:19
  27.1 14.0 %all-to-all-done = f32[128,1,174]{2,1,0:T(1,128)S(1)} async-done(((f32[128,1,174]{2,1,0:T(1,128)}), f32[128,1,174]{2,1,0:T(1,128)S(1)}, u32[]{:S(2)}, u32[]{:S(2)}) %all-to-all-start) | async-done | bytes 89120 | tf_op jit(solution)/shard_map/all_to_all | solution.py:34
  41.3 0.3 copy.79
  41.6 0.2 copy.81
  41.7 0.1 copy.80
  41.9 0.1 slice.162
  42.0 0.1 copy.82
  42.2 0.1 convert_element_type.49
  42.3 0.9 fusion
  43.2 0.8 broadcast_in_dim.2
  44.0 4.2 %all-to-all-start.1 = ((f32[4,28,768]{2,1,0:T(8,128)}), f32[4,28,768]{2,1,0:T(8,128)S(1)}, u32[]{:S(2)}, u32[]{:S(2)}) async-start(f32[4,28,768]{2,1,0:T(8,128)} %broadcast_in_dim.2), calls=%async_computation.1 | async-start | bytes 786432 | tf_op jit(solution)/shard_map/all_to_all | solution.py:44
  48.2 6.2 %all-to-all-done.1 = f32[4,28,768]{2,1,0:T(8,128)S(1)} async-done(((f32[4,28,768]{2,1,0:T(8,128)}), f32[4,28,768]{2,1,0:T(8,128)S(1)}, u32[]{:S(2)}, u32[]{:S(2)}) %all-to-all-start.1) | async-done | bytes 344096 | tf_op jit(solution)/shard_map/all_to_all | solution.py:44
  54.5 0.3 add_reduce_fusion.4
  55.4 0.1 add_multiply_fusion
  55.7 0.5 multiply_add_fusion.2
  56.2 0.3 maximum_bitcast_fusion
  56.5 1.0 mul.607
  57.7 0.2 mul.526
  58.0 0.2 mul.534
  58.4 0.6 compare_convert_fusion.1
  59.0 0.8 add_multiply_fusion.1
  59.8 6.8 %multiply_reduce_fusion = (f32[9,64,768]{2,1,0:T(8,128)}, f32[9,64,768]{2,1,0:T(8,128)S(1)}) fusion(f32[9,12,768]{2,1,0:T(8,128)} %mul.607, f32[64,12,768]{2,0,1:T(8,128)S(1)} %get-tuple-element.33, f32[9,12,768]{2,1,0:T(8,128)} %add_multiply_fusion.1, f32[64,12,768]{2,0,1:T(8,128)S(1)} %get-tuple-element.32), kind=kLoop, calls=%fused_computation | loop fusion | flops 20348928 | bytes 8921088 | tf_op jit(solution)/shard_map/reduce_sum | solution.py:91
  66.6 3.1 %fusion.10 = f32[4,144,768]{2,1,0:T(8,128)S(1)} fusion(f32[576,768,1]{1,0,2:T(8,128)} %bitcast.69, s32[4,144]{1,0:T(4,128)S(1)} %fusion.28), kind=kOutput, calls=%fused_computation.12 | convolution fusion | flops 1529155584 | bytes 3541248 | tf_op jit(solution)/shard_map/dot_general | solution.py:96
  69.7 1.6 %fusion.12 = f32[4,144,768]{2,1,0:T(8,128)S(1)} fusion(f32[576,768,1]{1,0,2:T(8,128)S(1)} %bitcast.68, s32[4,144]{1,0:T(4,128)S(1)} %fusion.28), kind=kOutput, calls=%fused_computation.13 | convolution fusion | flops 1529155584 | bytes 3541248 | tf_op jit(solution)/shard_map/dot_general | solution.py:97
  71.4 3.2 %fusion.4 = f32[4,4,144,144]{2,3,0,1:T(8,128)S(1)} fusion(f32[4,144,768]{2,1,0:T(8,128)S(1)} %fusion.10, f32[4,144,768]{2,1,0:T(8,128)S(1)} %fusion.12), kind=kOutput, calls=%fused_computation.9 | convolution fusion | flops 1528823808 | bytes 4866048 | tf_op jit(solution)/shard_map/kic,mjc->kmij/dot_general | solution.py:100
  74.6 0.2 fusion.41
  74.8 0.3 copy.88
  75.1 0.4 squeeze.11
  75.5 5.5 %collective-permute-start.1 = (f32[4,20736]{1,0:T(4,128)S(1)}, f32[4,20736]{1,0:T(4,128)}, u32[]{:S(2)}, u32[]{:S(2)}) collective-permute-start(f32[4,20736]{1,0:T(4,128)S(1)} %squeeze.11), channel_id=1, source_target_pairs={{0,4},{4,8},{8,12},{12,16},{16,20},{20,24},{24,28},{28,32},{32,36}... | collective-permute-start | bytes 995336 | tf_op jit(solution)/shard_map/ppermute | solution.py:19
  81.0 0.3 copy.90
  81.3 0.4 squeeze.13
  81.7 1.9 %collective-permute-start.2 = (f32[4,20736]{1,0:T(4,128)S(1)}, f32[4,20736]{1,0:T(4,128)}, u32[]{:S(2)}, u32[]{:S(2)}) collective-permute-start(f32[4,20736]{1,0:T(4,128)S(1)} %squeeze.13), channel_id=1, source_target_pairs={{0,508},{4,0},{8,4},{12,8},{16,12},{20,16},{24,20},{28,24},{32,28}... | collective-permute-start | bytes 995336 | tf_op jit(solution)/shard_map/ppermute | solution.py:19
  83.7 0.3 copy.91
  84.0 0.4 squeeze.14
  84.4 6.3 %collective-permute-start.3 = (f32[4,20736]{1,0:T(4,128)S(1)}, f32[4,20736]{1,0:T(4,128)S(1)}, u32[]{:S(2)}, u32[]{:S(2)}) collective-permute-start(f32[4,20736]{1,0:T(4,128)S(1)} %squeeze.14), channel_id=1, source_target_pairs={{0,504},{4,508},{8,0},{12,4},{16,8},{20,12},{24,16},{28,20},{32,24... | collective-permute-start | bytes 995336 | tf_op jit(solution)/shard_map/ppermute | solution.py:19
  90.6 0.3 copy.89
  91.0 0.4 squeeze.12
  91.4 0.4 collective-permute-done.2
  91.7 6.5 %collective-permute-done.3 = f32[4,20736]{1,0:T(4,128)S(1)} collective-permute-done((f32[4,20736]{1,0:T(4,128)S(1)}, f32[4,20736]{1,0:T(4,128)S(1)}, u32[]{:S(2)}, u32[]{:S(2)}) %collective-permute-start.3) | collective-permute-done | bytes 331808 | tf_op jit(solution)/shard_map/ppermute | solution.py:19
  98.2 1.4 %add_bitcast_fusion = f32[1,1,7,20736]{3,2,1,0:T(8,128)S(1)} fusion(f32[4,20736]{1,0:T(4,128)S(1)} %collective-permute-done.3, f32[4,20736]{1,0:T(4,128)} %collective-permute-done.2, f32[4,20736]{1,0:T(4,128)S(1)} %squeeze.12, f32[4,20736]{1,0:T(4,128)} %collective-permute-done.1), kind=kLoop, calls=%fused_computation.17 | loop fusion | flops 435456 | bytes 1907712 | tf_op jit(solution)/shard_map/reshape | solution.py:108
  99.6 1.4 %copy.92 = f32[1,1,7,20736]{3,1,2,0:T(1,128)} copy(f32[1,1,7,20736]{3,2,1,0:T(8,128)S(1)} %add_bitcast_fusion) | data formatting | bytes 1161216 | tf_op jit(solution)/shard_map/reshape | solution.py:108
  (54 shorter events, 1.5 us)
Async XLA Ops:
  1.8 22.0 %copy-start = (f32[256]{0:T(256)S(1)}, f32[256]{0:T(256)}, u32[]{:S(2)}) copy-start(f32[256]{0:T(256)} %param.9) | copy-start | bytes 3076
  3.4 37.7 %all-to-all-start = ((f32[128,1,174]{2,1,0:T(1,128)}), f32[128,1,174]{2,1,0:T(1,128)S(1)}, u32[]{:S(2)}, u32[]{:S(2)}) async-start(f32[128,1,174]{2,1,0:T(1,128)} %copy.77), calls=%async_computation | async-start | bytes 262144 | tf_op jit(solution)/shard_map/all_to_all | solution.py:34
  23.8 31.8 %collective-permute-start = (f32[256]{0:T(256)S(1)}, f32[256]{0:T(256)S(1)}, u32[]{:S(2)}, u32[]{:S(2)}) collective-permute-start(f32[256]{0:T(256)S(1)} %copy-done), channel_id=1, source_target_pairs={{0,8},{4,12},{8,16},{12,20},{16,24},{20,28},{24,32},{28,36},{32,40... | collective-permute-start | bytes 3080 | tf_op jit(solution)/shard_map/ppermute | solution.py:19
  44.0 10.4 %all-to-all-start.1 = ((f32[4,28,768]{2,1,0:T(8,128)}), f32[4,28,768]{2,1,0:T(8,128)S(1)}, u32[]{:S(2)}, u32[]{:S(2)}) async-start(f32[4,28,768]{2,1,0:T(8,128)} %broadcast_in_dim.2), calls=%async_computation.1 | async-start | bytes 786432 | tf_op jit(solution)/shard_map/all_to_all | solution.py:44
  75.5 15.9 %collective-permute-start.1 = (f32[4,20736]{1,0:T(4,128)S(1)}, f32[4,20736]{1,0:T(4,128)}, u32[]{:S(2)}, u32[]{:S(2)}) collective-permute-start(f32[4,20736]{1,0:T(4,128)S(1)} %squeeze.11), channel_id=1, source_target_pairs={{0,4},{4,8},{8,12},{12,16},{16,20},{20,24},{24,28},{28,32},{32,36}... | collective-permute-start | bytes 995336 | tf_op jit(solution)/shard_map/ppermute | solution.py:19
  81.7 10.0 %collective-permute-start.2 = (f32[4,20736]{1,0:T(4,128)S(1)}, f32[4,20736]{1,0:T(4,128)}, u32[]{:S(2)}, u32[]{:S(2)}) collective-permute-start(f32[4,20736]{1,0:T(4,128)S(1)} %squeeze.13), channel_id=1, source_target_pairs={{0,508},{4,0},{8,4},{12,8},{16,12},{20,16},{24,20},{28,24},{32,28}... | collective-permute-start | bytes 995336 | tf_op jit(solution)/shard_map/ppermute | solution.py:19
  84.4 13.9 %collective-permute-start.3 = (f32[4,20736]{1,0:T(4,128)S(1)}, f32[4,20736]{1,0:T(4,128)S(1)}, u32[]{:S(2)}, u32[]{:S(2)}) collective-permute-start(f32[4,20736]{1,0:T(4,128)S(1)} %squeeze.14), channel_id=1, source_target_pairs={{0,504},{4,508},{8,0},{12,4},{16,8},{20,12},{24,16},{28,20},{32,24... | collective-permute-start | bytes 995336 | tf_op jit(solution)/shard_map/ppermute | solution.py:19

commit v4 on v1

--- a/solution.py
+++ b/solution.py
@@ -95,16 +95,20 @@
 
     left_flat = panel(key_left, left3)
     right_flat = panel(key_right, coup3)
-    product = lax.dot_general(
-        left_flat, right_flat, (((1,), (1,)), ((), ())), precision=lax.Precision.HIGH
-    )
-    tiles = product.reshape((owners, TS, owners, TS)).transpose((0, 2, 1, 3))
-    tiles = tiles.reshape((owners, owners, TS * TS))
+
+    def owner_rows(distance):
+        rows_k = left_flat[distance * TS : (distance + 1) * TS]
+        product = lax.dot_general(
+            rows_k, right_flat, (((1,), (1,)), ((), ())), precision=lax.Precision.HIGH
+        )
+        return product.reshape((TS, owners, TS)).transpose((1, 0, 2)).reshape((owners, TS * TS))
+
     tile_count = 2 * HOPS + 1
     summed = jnp.zeros((tile_count, TS * TS), jnp.float32)
-    for distance in range(owners - 1, -1, -1):
+    for distance in sorted(range(owners), key=lambda k: (k == SHIFT, -k)):
         by = distance - SHIFT
-        arrived = tiles[distance] if by == 0 else from_behind(tiles[distance], "trk", by)
+        rows_k = owner_rows(distance)
+        arrived = rows_k if by == 0 else from_behind(rows_k, "trk", by)
         summed = summed + jnp.pad(arrived, ((HOPS - distance, distance), (0, 0)))
     return summed.reshape((1, 1, tile_count, TS * TS))
 

time: 98.5 us -> 103 us (1.046); the launches traced: 96.9 us -> 103 us
  starting transfers between devices: 17.9 us -> 21.2 us
  local copies, waits for them, and re-layouts: 15.5 us -> 18.3 us
  other arithmetic: 10.5 us -> 12.8 us
  matrix products: 5.89 us -> 4.47 us
    ppermute x4, starting transfers between devices: 13.8 us -> 17 us  [from_behind(): return lax.ppermute(x, axis, [(i, (i + by) % size) for i in range(size)])]
    reshape x0 -> x4, local copies, waits for them, and re-layouts: none -> 3.14 us  [owner_rows(): product.reshape((TS, owners, TS)).transpose((1, 0, 2))]
    slice x1 -> x9, local copies, waits for them, and re-layouts: 0.15 us -> 2.48 us  [owner_rows(): rows_k = left_flat[distance * TS:(distance + 1) * TS]]
    squeeze x4 -> x0, local copies, waits for them, and re-layouts: 1.67 us -> none  [body(): tiles[distance]]
    dot_general x1 -> x4, matrix products: 4.95 us -> 3.53 us  [owner_rows(): lax.dot_general(rows_k, right_flat, (((1,), (1,)), ((), ())), precision=l...]
    reduce_sum x1, other arithmetic: 5.4 us -> 6.74 us  [panel(): return jnp.sum(sel * vals, axis=1)]
    dot_general x2 -> x1, local copies, waits for them, and re-layouts: 2.98 us -> 2.05 us  [owner_rows(): lax.dot_general(rows_k, right_flat, (((1,), (1,)), ((), ())), precision=l...]
    reduce_sum x2 -> x1, local copies, waits for them, and re-layouts: 5.16 us -> 4.25 us  [panel(): return jnp.sum(sel * vals, axis=1)]
  transfers between devices with their start and end apart: 5 -> 5, of which waited for: 2 -> 3; matrix products, arithmetic and copies ran while one was open for 2% -> 7% of each run, Pallas kernels for 0% -> 0%
where the time goes in v4:
time: 103 us
  blocking collectives  37.4 us (36%)
  starting transfers between devices  21.2 us (21%)
  local copies, waits for them, and re-layouts  18.3 us (18%)
  other arithmetic  12.8 us (12%)
  waiting for transfers between devices  8.05 us (8%)
  matrix products  4.47 us (4%)
    all_to_all x1, blocking collectives, body(): got = lax.all_to_all(send, 'trk', split_axis=0, concat_axis=0, tiled=True)  37.4 us
    ppermute x4, starting transfers between devices, from_behind(): return lax.ppermute(x, axis, [(i, (i + by) % size) for i in range(size)])  17 us
    reduce_sum x1, other arithmetic, panel(): return jnp.sum(sel * vals, axis=1)  6.74 us
    ppermute x4, waiting for transfers between devices, from_behind(): return lax.ppermute(x, axis, [(i, (i + by) % size) for i in range(size)])  4.93 us
    reduce_sum x1, local copies, waits for them, and re-layouts, panel(): return jnp.sum(sel * vals, axis=1)  4.25 us
    all_to_all x1, starting transfers between devices, body(): lax.all_to_all(copies, 'cam', 0, 0, tiled=True).transpose((1, 0, 2))  4.18 us
    dot_general x4, matrix products, owner_rows(): lax.dot_general(rows_k, right_flat, (((1,), (1,)), ((), ())), precision=l...  3.53 us
    reshape x4, local copies, waits for them, and re-layouts, owner_rows(): product.reshape((TS, owners, TS)).transpose((1, 0, 2))  3.14 us
  transfers between devices with their start and end apart: 5, of which 3 were waited for; matrix products, arithmetic and copies ran while one was open for 7% of the time, Pallas kernels for 0%

profile of v4, /device:TPU:1, one launch (start us, length us, event | category | flops | bytes accessed | tf_op | source)
XLA Modules:
  0.0 102.9 jit_solution(213796977171328116)
XLA Ops:
  0.0 0.7 convert_element_type.46
  0.7 0.9 pad_maximum_fusion
  1.6 0.2 copy.54
  1.9 0.2 copy.56
  2.4 0.1 copy.57
  2.8 37.4 %all_to_all.14 = f32[128,1,174]{2,1,0:T(1,128)S(1)} all-to-all(f32[128,1,174]{2,1,0:T(1,128)S(1)} %copy.58), channel_id=1, replica_groups=mesh['trk'=128,'cam'=4] {'trk'}, dimensions={0} | all-to-all | bytes 178176 | tf_op jit(solution)/shard_map/all_to_all | solution.py:34
  40.5 0.1 convert_element_type.48
  40.6 0.1 copy.61
  40.7 0.1 slice.170
  40.9 0.3 copy.60
  41.2 0.2 copy.62
  41.4 0.9 fusion
  42.3 0.8 broadcast_in_dim.12
  43.1 4.2 %all-to-all-start.1 = ((f32[4,28,768]{2,1,0:T(8,128)}), f32[4,28,768]{2,1,0:T(8,128)S(1)}, u32[]{:S(2)}, u32[]{:S(2)}) async-start(f32[4,28,768]{2,1,0:T(8,128)} %broadcast_in_dim.12), calls=%async_computation.1 | async-start | bytes 786432 | tf_op jit(solution)/shard_map/all_to_all | solution.py:44
  47.3 3.0 %collective-permute-start = (f32[256]{0:T(256)S(1)}, f32[256]{0:T(256)S(1)}, u32[]{:S(2)}, u32[]{:S(2)}) collective-permute-start(f32[256]{0:T(256)S(1)} %copy-done.3), channel_id=1, source_target_pairs={{0,8},{4,12},{8,16},{12,20},{16,24},{20,28},{24,32},{28,36},{32,40... | collective-permute-start | bytes 3080 | tf_op jit(solution)/shard_map/ppermute | solution.py:19
  50.4 3.1 %all-to-all-done.1 = f32[4,28,768]{2,1,0:T(8,128)S(1)} async-done(((f32[4,28,768]{2,1,0:T(8,128)}), f32[4,28,768]{2,1,0:T(8,128)S(1)}, u32[]{:S(2)}, u32[]{:S(2)}) %all-to-all-start.1) | async-done | bytes 344096 | tf_op jit(solution)/shard_map/all_to_all | solution.py:44
  53.6 0.3 add_reduce_fusion.4
  54.5 0.1 add_multiply_fusion.1
  55.0 0.5 multiply_add_fusion.2
  55.6 0.3 maximum_bitcast_fusion
  55.9 1.0 broadcast_in_dim.14
  57.0 0.2 mul.555
  57.3 0.2 mul.561
  57.6 0.6 compare_convert_fusion
  58.1 0.8 add_multiply_fusion
  59.0 6.7 %multiply_reduce_fusion = (f32[64,9,768]{2,0,1:T(8,128)}, f32[64,9,768]{2,0,1:T(8,128)S(1)}) fusion(f32[9,12,768]{2,1,0:T(8,128)} %add_multiply_fusion, f32[64,12,768]{2,0,1:T(8,128)S(1)} %get-tuple-element.32, f32[9,12,768]{2,1,0:T(8,128)} %broadcast_in_dim.14, f32[64,12,768]{2,0,1:T(8,128)S(1)} %get-tuple-element.33), kind=kLoop, calls=%fused_computation | loop fusion | flops 20348928 | bytes 8921088 | tf_op jit(solution)/shard_map/reduce_sum | solution.py:94
  65.7 4.2 %copy.73 = f32[64,9,768]{2,1,0:T(8,128)} copy(f32[64,9,768]{2,0,1:T(8,128)} %get-tuple-element.39) | data formatting | bytes 3538944 | tf_op jit(solution)/shard_map/reduce_sum | solution.py:94
  70.0 2.0 %dot_general.18 = f32[4,144,768]{2,1,0:T(8,128)S(1)} reshape(f32[64,9,768]{2,1,0:T(8,128)} %copy.73) | data formatting | bytes 3538944 | tf_op jit(solution)/shard_map/dot_general | solution.py:101
  72.0 1.1 %fusion.19 = (f32[16,9,768]{2,0,1:T(8,128)S(1)}, f32[16,9,768]{2,0,1:T(8,128)}, f32[16,9,768]{2,0,1:T(8,128)}, f32[16,9,768]{2,0,1:T(8,128)}) fusion(f32[64,9,768]{2,0,1:T(8,128)S(1)} %get-tuple-element.40), kind=kLoop, calls=%fused_computation.77 | loop fusion | bytes 3538944 | tf_op jit(solution)/shard_map/slice | solution.py:100
  73.1 0.3 copy.70
  73.5 0.9 convolution_bitcast_fusion.3
  74.4 1.2 %reshape.249 = f32[4,20736]{1,0:T(4,128)} reshape(f32[4,144,144]{2,1,0:T(8,128)S(1)} %convolution_bitcast_fusion.3) | data formatting | bytes 663552 | tf_op jit(solution)/shard_map/reshape | solution.py:104
  75.5 5.8 %collective-permute-start.1 = (f32[4,20736]{1,0:T(4,128)}, f32[4,20736]{1,0:T(4,128)}, u32[]{:S(2)}, u32[]{:S(2)}) collective-permute-start(f32[4,20736]{1,0:T(4,128)} %reshape.249), channel_id=1, source_target_pairs={{0,4},{4,8},{8,12},{12,16},{16,20},{20,24},{24,28},{28,32},{32,36}... | collective-permute-start | bytes 995336 | tf_op jit(solution)/shard_map/ppermute | solution.py:19
  81.3 0.3 copy.75
  81.7 0.9 convolution_bitcast_fusion.1
  82.6 1.1 %reshape.251 = f32[4,20736]{1,0:T(4,128)} reshape(f32[4,144,144]{2,1,0:T(8,128)S(1)} %convolution_bitcast_fusion.1) | data formatting | bytes 663552 | tf_op jit(solution)/shard_map/reshape | solution.py:104
  83.7 6.3 %collective-permute-start.3 = (f32[4,20736]{1,0:T(4,128)}, f32[4,20736]{1,0:T(4,128)}, u32[]{:S(2)}, u32[]{:S(2)}) collective-permute-start(f32[4,20736]{1,0:T(4,128)} %reshape.251), channel_id=1, source_target_pairs={{0,504},{4,508},{8,0},{12,4},{16,8},{20,12},{24,16},{28,20},{32,24... | collective-permute-start | bytes 995336 | tf_op jit(solution)/shard_map/ppermute | solution.py:19
  90.0 0.3 copy.74
  90.4 0.9 convolution_bitcast_fusion.2
  91.3 0.4 reshape.250
  91.7 1.9 %collective-permute-start.2 = (f32[4,20736]{1,0:T(4,128)S(1)}, f32[4,20736]{1,0:T(4,128)}, u32[]{:S(2)}, u32[]{:S(2)}) collective-permute-start(f32[4,20736]{1,0:T(4,128)S(1)} %reshape.250), channel_id=1, source_target_pairs={{0,508},{4,0},{8,4},{12,8},{16,12},{20,16},{24,20},{28,24},{32,28}... | collective-permute-start | bytes 995336 | tf_op jit(solution)/shard_map/ppermute | solution.py:19
  93.6 0.3 copy.76
  94.0 0.9 convolution_bitcast_fusion
  94.9 0.4 reshape.252
  95.3 0.2 collective-permute-done.3
  95.5 4.7 %collective-permute-done.2 = f32[4,20736]{1,0:T(4,128)} collective-permute-done((f32[4,20736]{1,0:T(4,128)S(1)}, f32[4,20736]{1,0:T(4,128)}, u32[]{:S(2)}, u32[]{:S(2)}) %collective-permute-start.2) | collective-permute-done | bytes 331808 | tf_op jit(solution)/shard_map/ppermute | solution.py:19
  100.2 1.5 %pad_add_fusion = f32[7,20736]{1,0:T(8,128)S(1)} fusion(f32[4,20736]{1,0:T(4,128)S(1)} %reshape.252, f32[4,20736]{1,0:T(4,128)} %collective-permute-done.3, f32[4,20736]{1,0:T(4,128)} %collective-permute-done.2, f32[4,20736]{1,0:T(4,128)} %collective-permute-done.1), kind=kLoop, calls=%fused_computation.11 | loop fusion | flops 435456 | bytes 1907712 | tf_op jit(solution)/shard_map/add | solution.py:112
  101.7 1.2 %reshape.253 = f32[1,1,7,20736]{3,1,2,0:T(1,128)} reshape(f32[7,20736]{1,0:T(8,128)S(1)} %pad_add_fusion) | data formatting | bytes 1161216 | tf_op jit(solution)/shard_map/reshape | solution.py:113
  (68 shorter events, 2.1 us)
Async XLA Ops:
  40.3 7.0 %copy-start.3 = (f32[256]{0:T(256)S(1)}, f32[256]{0:T(256)}, u32[]{:S(2)}) copy-start(f32[256]{0:T(256)} %param.9) | copy-start | bytes 3076
  43.1 10.4 %all-to-all-start.1 = ((f32[4,28,768]{2,1,0:T(8,128)}), f32[4,28,768]{2,1,0:T(8,128)S(1)}, u32[]{:S(2)}, u32[]{:S(2)}) async-start(f32[4,28,768]{2,1,0:T(8,128)} %broadcast_in_dim.12), calls=%async_computation.1 | async-start | bytes 786432 | tf_op jit(solution)/shard_map/all_to_all | solution.py:44
  47.3 7.7 %collective-permute-start = (f32[256]{0:T(256)S(1)}, f32[256]{0:T(256)S(1)}, u32[]{:S(2)}, u32[]{:S(2)}) collective-permute-start(f32[256]{0:T(256)S(1)} %copy-done.3), channel_id=1, source_target_pairs={{0,8},{4,12},{8,16},{12,20},{16,24},{20,28},{24,32},{28,36},{32,40... | collective-permute-start | bytes 3080 | tf_op jit(solution)/shard_map/ppermute | solution.py:19
  73.4 7.9 %copy-start.2 = (f32[16,9,768]{2,0,1:T(8,128)S(1)}, f32[16,9,768]{2,0,1:T(8,128)}, u32[]{:S(2)}) copy-start(f32[16,9,768]{2,0,1:T(8,128)} %get-tuple-element.22) | copy-start | bytes 1327108
  75.5 19.8 %collective-permute-start.1 = (f32[4,20736]{1,0:T(4,128)}, f32[4,20736]{1,0:T(4,128)}, u32[]{:S(2)}, u32[]{:S(2)}) collective-permute-start(f32[4,20736]{1,0:T(4,128)} %reshape.249), channel_id=1, source_target_pairs={{0,4},{4,8},{8,12},{12,16},{16,20},{20,24},{24,28},{28,32},{32,36}... | collective-permute-start | bytes 995336 | tf_op jit(solution)/shard_map/ppermute | solution.py:19
  81.6 8.4 %copy-start.1 = (f32[16,9,768]{2,0,1:T(8,128)S(1)}, f32[16,9,768]{2,0,1:T(8,128)}, u32[]{:S(2)}) copy-start(f32[16,9,768]{2,0,1:T(8,128)} %get-tuple-element.23) | copy-start | bytes 1327108
  83.7 11.8 %collective-permute-start.3 = (f32[4,20736]{1,0:T(4,128)}, f32[4,20736]{1,0:T(4,128)}, u32[]{:S(2)}, u32[]{:S(2)}) collective-permute-start(f32[4,20736]{1,0:T(4,128)} %reshape.251), channel_id=1, source_target_pairs={{0,504},{4,508},{8,0},{12,4},{16,8},{20,12},{24,16},{28,20},{32,24... | collective-permute-start | bytes 995336 | tf_op jit(solution)/shard_map/ppermute | solution.py:19
  90.3 3.3 %copy-start = (f32[16,9,768]{2,0,1:T(8,128)S(1)}, f32[16,9,768]{2,0,1:T(8,128)}, u32[]{:S(2)}) copy-start(f32[16,9,768]{2,0,1:T(8,128)} %get-tuple-element.21) | copy-start | bytes 1327108
  91.7 8.5 %collective-permute-start.2 = (f32[4,20736]{1,0:T(4,128)S(1)}, f32[4,20736]{1,0:T(4,128)}, u32[]{:S(2)}, u32[]{:S(2)}) collective-permute-start(f32[4,20736]{1,0:T(4,128)S(1)} %reshape.250), channel_id=1, source_target_pairs={{0,508},{4,0},{8,4},{12,8},{16,12},{20,16},{24,20},{28,24},{32,28}... | collective-permute-start | bytes 995336 | tf_op jit(solution)/shard_map/ppermute | solution.py:19

commit v5 on v1

--- a/solution.py
+++ b/solution.py
@@ -24,8 +24,10 @@
     tracks = damping.shape[0]
     rows = residuals.shape[1]
     per_dest = rows // strip_count
+    magnitude = jnp.sqrt(residuals[0] * residuals[0] + residuals[1] * residuals[1])
+    weight = obs_index[2].astype(jnp.float32) * (HUBER_DELTA / jnp.maximum(magnitude, HUBER_DELTA))
     fields = jnp.concatenate(
-        [residuals, camera_jac, point_jac, obs_index.astype(jnp.float32)], axis=0
+        [camera_jac, point_jac, weight[None], obs_index[:2].astype(jnp.float32)], axis=0
     )
     nf = fields.shape[0]
     send = fields.reshape((nf, strip_count, per_dest)).transpose((1, 0, 2))
@@ -33,10 +35,10 @@
     send = jnp.roll(send, SHIFT, axis=0)
     got = lax.all_to_all(send, "trk", split_axis=0, concat_axis=0, tiled=True)
     got = got.reshape((strip_count, nf, per_dest)).transpose((1, 0, 2)).reshape((nf, rows))
-    position = got[nf - 3].astype(jnp.int32)
+    position = got[nf - 2].astype(jnp.int32)
     local_slots = rows // tracks
     onehot = (position[:, None] == jnp.arange(rows, dtype=jnp.int32)[None, :]).astype(jnp.float32)
-    kept = jnp.concatenate([got[: nf - 3], got[nf - 2 :]], axis=0)
+    kept = jnp.concatenate([got[: nf - 2], got[nf - 1 :]], axis=0)
     placed = jnp.dot(kept, onehot, precision=lax.Precision.HIGHEST)
     if CAM_BY_ALL_TO_ALL:
         n_cam = lax.axis_size("cam")
@@ -48,13 +50,10 @@
     damping = from_behind(damping, "trk", SHIFT)
     slots = n_cam * local_slots
     g = gathered.reshape((kept.shape[0], slots, tracks))
-    res = g[0:2]
-    cj = g[2:20]
-    pj = g[20:26]
-    cam = g[26].astype(jnp.int32)
-    alive = g[27]
-    magnitude = jnp.sqrt(res[0] * res[0] + res[1] * res[1])
-    w = alive * (HUBER_DELTA / jnp.maximum(magnitude, HUBER_DELTA))
+    cj = g[0:18]
+    pj = g[18:24]
+    w = g[24]
+    cam = g[25].astype(jnp.int32)
     coup = (cj[:9, None] * pj[None, :3] + cj[9:, None] * pj[None, 3:]) * w
     terms = [
         (w * (pj[k] * pj[l] + pj[3 + k] * pj[3 + l])).sum(axis=0) for k, l in UPPER_PAIRS

time: 98.5 us -> 101 us (1.025)
  local copies, waits for them, and re-layouts: 15.5 us -> 17.6 us
    unnamed x10 -> x13, local copies, waits for them, and re-layouts: 0.11 us -> 1.17 us
    concatenate x1 -> x8, local copies, waits for them, and re-layouts: 0.18 us -> 1.21 us  [body(): jnp.concatenate([camera_jac, point_jac, weight[None], obs_index[:2].astyp...]
where the time goes in v5:
time: 101 us; the launch traced here: 98.9 us
  blocking collectives  37.4 us (37%)
  starting transfers between devices  17.9 us (18%)
  local copies, waits for them, and re-layouts  17.6 us (17%)
  other arithmetic  10.4 us (10%)
  waiting for transfers between devices  9.05 us (9%)
  matrix products  5.88 us (6%)
    all_to_all x1, blocking collectives, body(): got = lax.all_to_all(send, 'trk', split_axis=0, concat_axis=0, tiled=True)  37.4 us
    ppermute x4, starting transfers between devices, from_behind(): return lax.ppermute(x, axis, [(i, (i + by) % size) for i in range(size)])  13.8 us
    ppermute x4, waiting for transfers between devices, from_behind(): return lax.ppermute(x, axis, [(i, (i + by) % size) for i in range(size)])  5.92 us
    reduce_sum x1, other arithmetic, panel(): return jnp.sum(sel * vals, axis=1)  5.4 us
    reduce_sum x2, local copies, waits for them, and re-layouts, panel(): return jnp.sum(sel * vals, axis=1)  5.16 us
    dot_general x1, matrix products, body(): lax.dot_general(left_flat, right_flat, (((1,), (1,)), ((), ())), precisio...  4.95 us
    all_to_all x1, starting transfers between devices, body(): lax.all_to_all(copies, 'cam', 0, 0, tiled=True).transpose((1, 0, 2))  4.18 us
    all_to_all x1, waiting for transfers between devices, body(): lax.all_to_all(copies, 'cam', 0, 0, tiled=True).transpose((1, 0, 2))  3.13 us
  transfers between devices with their start and end apart: 5, of which 2 were waited for; matrix products, arithmetic and copies ran while one was open for 2% of the time, Pallas kernels for 0%

profile of v5, /device:TPU:1, one launch (start us, length us, event | category | flops | bytes accessed | tf_op | source)
XLA Modules:
  0.0 98.9 jit_solution(166385360272406762)
XLA Ops:
  0.0 0.7 slice_convert_fusion.1
  0.7 0.8 fusion.16
  1.5 0.1 concatenate.21
  1.7 0.2 concatenate.22
  2.0 1.1 %copy.67 = f32[18,768]{0,1:T(8,128)S(1)} copy(f32[18,768]{1,0:T(8,128)} %param.6) | data formatting | bytes 110592 | tf_op args[1]
  3.1 0.2 copy.68
  3.3 0.4 concatenate.20
  3.6 0.2 copy.69
  4.0 0.3 copy.72
  4.4 0.1 copy.74
  4.7 0.1 copy.75
  4.8 37.4 %all_to_all.14 = f32[128,1,162]{2,1,0:T(1,128)S(1)} all-to-all(f32[128,1,162]{2,1,0:T(1,128)S(1)} %copy.75), channel_id=1, replica_groups=mesh['trk'=128,'cam'=4] {'trk'}, dimensions={0} | all-to-all | bytes 165888 | tf_op jit(solution)/shard_map/all_to_all | solution.py:36
  42.4 0.1 copy.78
  42.5 0.1 slice.166
  42.7 0.1 copy.80
  42.8 0.1 convert_element_type.53
  42.9 0.3 copy.77
  43.2 0.2 copy.79
  43.4 0.9 fusion
  44.3 0.8 broadcast_in_dim.12
  45.1 4.2 %all-to-all-start.1 = ((f32[4,26,768]{2,1,0:T(8,128)}), f32[4,26,768]{2,1,0:T(8,128)S(1)}, u32[]{:S(2)}, u32[]{:S(2)}) async-start(f32[4,26,768]{2,1,0:T(8,128)} %broadcast_in_dim.12), calls=%async_computation.1 | async-start | bytes 786432 | tf_op jit(solution)/shard_map/all_to_all | solution.py:46
  49.3 3.0 %collective-permute-start = (f32[256]{0:T(256)S(1)}, f32[256]{0:T(256)S(1)}, u32[]{:S(2)}, u32[]{:S(2)}) collective-permute-start(f32[256]{0:T(256)S(1)} %copy-done.1), channel_id=1, source_target_pairs={{0,8},{4,12},{8,16},{12,20},{16,24},{20,28},{24,32},{28,36},{32,40... | collective-permute-start | bytes 3080 | tf_op jit(solution)/shard_map/ppermute | solution.py:19
  52.4 3.1 %all-to-all-done.1 = f32[4,26,768]{2,1,0:T(8,128)S(1)} async-done(((f32[4,26,768]{2,1,0:T(8,128)}), f32[4,26,768]{2,1,0:T(8,128)S(1)}, u32[]{:S(2)}, u32[]{:S(2)}) %all-to-all-start.1) | async-done | bytes 319520 | tf_op jit(solution)/shard_map/all_to_all | solution.py:46
  55.6 0.3 add_reduce_fusion.4
  56.4 0.1 add_multiply_fusion.1
  57.0 0.5 multiply_add_fusion.2
  57.6 0.3 maximum_bitcast_fusion
  57.9 0.2 broadcast_in_dim.14
  58.2 0.2 mul.475
  58.5 0.2 mul.481
  58.8 0.6 compare_convert_fusion.1
  59.4 5.4 %multiply_reduce_fusion = (f32[64,9,768]{2,0,1:T(8,128)}, f32[64,9,768]{2,0,1:T(8,128)}) fusion(f32[9,12,768]{2,1,0:T(8,128)S(1)} %add_multiply_fusion, f32[64,12,768]{2,0,1:T(8,128)S(1)} %get-tuple-element.35, f32[9,12,768]{2,1,0:T(8,128)S(1)} %broadcast_in_dim.14, f32[64,12,768]{2,0,1:T(8,128)S(1)} %get-tuple-element.34), kind=kLoop, calls=%fused_computation | loop fusion | flops 20348928 | bytes 8921088 | tf_op jit(solution)/shard_map/reduce_sum | solution.py:93
  64.8 2.6 %copy.90 = f32[64,9,768]{2,1,0:T(8,128)S(1)} copy(f32[64,9,768]{2,0,1:T(8,128)} %get-tuple-element.41) | data formatting | bytes 3538944 | tf_op jit(solution)/shard_map/reduce_sum | solution.py:93
  67.4 1.6 %reshape.210 = f32[4,144,768,1]{2,1,0,3:T(8,128)} reshape(f32[64,9,768]{2,1,0:T(8,128)S(1)} %copy.90) | data formatting | bytes 3538944 | tf_op jit(solution)/shard_map/dot_general | solution.py:97
  69.0 2.6 %copy.87 = f32[64,9,768]{2,1,0:T(8,128)S(1)} copy(f32[64,9,768]{2,0,1:T(8,128)} %get-tuple-element.42) | data formatting | bytes 3538944 | tf_op jit(solution)/shard_map/reduce_sum | solution.py:93
  71.6 1.4 %reshape.209 = f32[4,144,768,1]{2,1,0,3:T(8,128)} reshape(f32[64,9,768]{2,1,0:T(8,128)S(1)} %copy.87) | data formatting | bytes 3538944 | tf_op jit(solution)/shard_map/dot_general | solution.py:97
  73.0 4.9 %fusion.3 = f32[4,4,144,144]{3,2,1,0:T(8,128)S(1)} fusion(f32[4,144,768,1]{2,1,0,3:T(8,128)} %reshape.210, f32[4,144,768,1]{2,1,0,3:T(8,128)} %reshape.209), kind=kOutput, calls=%fused_computation.8 | convolution fusion | flops 1528823808 | bytes 4866048 | tf_op jit(solution)/shard_map/dot_general | solution.py:97
  77.9 0.2 fusion.23
  78.1 0.4 squeeze.8
  78.5 0.4 squeeze.11
  78.9 0.4 squeeze.10
  79.3 5.3 %collective-permute-start.2 = (f32[4,20736]{1,0:T(4,128)S(1)}, f32[4,20736]{1,0:T(4,128)S(1)}, u32[]{:S(2)}, u32[]{:S(2)}) collective-permute-start(f32[4,20736]{1,0:T(4,128)S(1)} %squeeze.10), channel_id=1, source_target_pairs={{0,508},{4,0},{8,4},{12,8},{16,12},{20,16},{24,20},{28,24},{32,28}... | collective-permute-start | bytes 995336 | tf_op jit(solution)/shard_map/ppermute | solution.py:19
  84.6 3.2 %collective-permute-start.3 = (f32[4,20736]{1,0:T(4,128)S(1)}, f32[4,20736]{1,0:T(4,128)S(1)}, u32[]{:S(2)}, u32[]{:S(2)}) collective-permute-start(f32[4,20736]{1,0:T(4,128)S(1)} %squeeze.11), channel_id=1, source_target_pairs={{0,504},{4,508},{8,0},{12,4},{16,8},{20,12},{24,16},{28,20},{32,24... | collective-permute-start | bytes 995336 | tf_op jit(solution)/shard_map/ppermute | solution.py:19
  87.9 2.2 %collective-permute-start.1 = (f32[4,20736]{1,0:T(4,128)S(1)}, f32[4,20736]{1,0:T(4,128)}, u32[]{:S(2)}, u32[]{:S(2)}) collective-permute-start(f32[4,20736]{1,0:T(4,128)S(1)} %squeeze.8), channel_id=1, source_target_pairs={{0,4},{4,8},{8,12},{12,16},{16,20},{20,24},{24,28},{28,32},{32,36}... | collective-permute-start | bytes 995336 | tf_op jit(solution)/shard_map/ppermute | solution.py:19
  90.1 0.4 squeeze.9
  90.5 5.9 %collective-permute-done.3 = f32[4,20736]{1,0:T(4,128)S(1)} collective-permute-done((f32[4,20736]{1,0:T(4,128)S(1)}, f32[4,20736]{1,0:T(4,128)S(1)}, u32[]{:S(2)}, u32[]{:S(2)}) %collective-permute-start.3) | collective-permute-done | bytes 331808 | tf_op jit(solution)/shard_map/ppermute | solution.py:19
  96.4 1.3 %pad_add_fusion = f32[7,20736]{1,0:T(8,128)S(1)} fusion(f32[4,20736]{1,0:T(4,128)S(1)} %collective-permute-done.3, f32[4,20736]{1,0:T(4,128)S(1)} %collective-permute-done.2, f32[4,20736]{1,0:T(4,128)S(1)} %squeeze.9, f32[4,20736]{1,0:T(4,128)} %collective-permute-done.1), kind=kLoop, calls=%fused_computation.10 | loop fusion | flops 435456 | bytes 1907712 | tf_op jit(solution)/shard_map/add | solution.py:107
  97.7 1.2 %reshape.208 = f32[1,1,7,20736]{3,1,2,0:T(1,128)} reshape(f32[7,20736]{1,0:T(8,128)S(1)} %pad_add_fusion) | data formatting | bytes 1161216 | tf_op jit(solution)/shard_map/reshape | solution.py:108
  (61 shorter events, 1.8 us)
Async XLA Ops:
  0.0 3.3 %copy-start = (f32[6,768]{1,0:T(8,128)S(1)}, f32[6,768]{1,0:T(8,128)}, u32[]{:S(2)}) copy-start(f32[6,768]{1,0:T(8,128)} %param.7) | copy-start | bytes 55300
  42.3 7.0 %copy-start.1 = (f32[256]{0:T(256)S(1)}, f32[256]{0:T(256)}, u32[]{:S(2)}) copy-start(f32[256]{0:T(256)} %param.9) | copy-start | bytes 3076
  45.1 10.4 %all-to-all-start.1 = ((f32[4,26,768]{2,1,0:T(8,128)}), f32[4,26,768]{2,1,0:T(8,128)S(1)}, u32[]{:S(2)}, u32[]{:S(2)}) async-start(f32[4,26,768]{2,1,0:T(8,128)} %broadcast_in_dim.12), calls=%async_computation.1 | async-start | bytes 786432 | tf_op jit(solution)/shard_map/all_to_all | solution.py:46
  49.3 7.7 %collective-permute-start = (f32[256]{0:T(256)S(1)}, f32[256]{0:T(256)S(1)}, u32[]{:S(2)}, u32[]{:S(2)}) collective-permute-start(f32[256]{0:T(256)S(1)} %copy-done.1), channel_id=1, source_target_pairs={{0,8},{4,12},{8,16},{12,20},{16,24},{20,28},{24,32},{28,36},{32,40... | collective-permute-start | bytes 3080 | tf_op jit(solution)/shard_map/ppermute | solution.py:19
  79.3 11.2 %collective-permute-start.2 = (f32[4,20736]{1,0:T(4,128)S(1)}, f32[4,20736]{1,0:T(4,128)S(1)}, u32[]{:S(2)}, u32[]{:S(2)}) collective-permute-start(f32[4,20736]{1,0:T(4,128)S(1)} %squeeze.10), channel_id=1, source_target_pairs={{0,508},{4,0},{8,4},{12,8},{16,12},{20,16},{24,20},{28,24},{32,28}... | collective-permute-start | bytes 995336 | tf_op jit(solution)/shard_map/ppermute | solution.py:19
  84.6 11.8 %collective-permute-start.3 = (f32[4,20736]{1,0:T(4,128)S(1)}, f32[4,20736]{1,0:T(4,128)S(1)}, u32[]{:S(2)}, u32[]{:S(2)}) collective-permute-start(f32[4,20736]{1,0:T(4,128)S(1)} %squeeze.11), channel_id=1, source_target_pairs={{0,504},{4,508},{8,0},{12,4},{16,8},{20,12},{24,16},{28,20},{32,24... | collective-permute-start | bytes 995336 | tf_op jit(solution)/shard_map/ppermute | solution.py:19
  87.9 8.6 %collective-permute-start.1 = (f32[4,20736]{1,0:T(4,128)S(1)}, f32[4,20736]{1,0:T(4,128)}, u32[]{:S(2)}, u32[]{:S(2)}) collective-permute-start(f32[4,20736]{1,0:T(4,128)S(1)} %squeeze.8), channel_id=1, source_target_pairs={{0,4},{4,8},{8,12},{12,16},{16,20},{20,24},{24,28},{28,32},{32,36}... | collective-permute-start | bytes 995336 | tf_op jit(solution)/shard_map/ppermute | solution.py:19

commit v6 on v1

--- a/solution.py
+++ b/solution.py
@@ -101,12 +101,14 @@
     tiles = product.reshape((owners, TS, owners, TS)).transpose((0, 2, 1, 3))
     tiles = tiles.reshape((owners, owners, TS * TS))
     tile_count = 2 * HOPS + 1
-    summed = jnp.zeros((tile_count, TS * TS), jnp.float32)
+    summed = jnp.zeros((1, 1, tile_count, TS * TS), jnp.float32)
     for distance in range(owners - 1, -1, -1):
         by = distance - SHIFT
-        arrived = tiles[distance] if by == 0 else from_behind(tiles[distance], "trk", by)
-        summed = summed + jnp.pad(arrived, ((HOPS - distance, distance), (0, 0)))
-    return summed.reshape((1, 1, tile_count, TS * TS))
+        part = tiles[distance][None, None]
+        arrived = part if by == 0 else from_behind(part, "trk", by)
+        spread = ((0, 0), (0, 0), (HOPS - distance, distance), (0, 0))
+        summed = summed + jnp.pad(arrived, spread)
+    return summed
 
 
 def solution(mesh):

time: 98.5 us -> 99.2 us (level)
  other arithmetic: 10.5 us -> 11.6 us
    another operation x0 -> x4, local copies, waits for them, and re-layouts: none -> 2.72 us  [body(): part = tiles[distance][None, None]]
    squeeze x4 -> x0, local copies, waits for them, and re-layouts: 1.67 us -> none  [body(): tiles[distance]]
    reshape x1 -> x0, local copies, waits for them, and re-layouts: 1.21 us -> none  [body(): return summed.reshape((1, 1, tile_count, TS * TS))]
    add x1, other arithmetic: 1.26 us -> 2.34 us  [body(): summed = summed + jnp.pad(arrived, spread)]
where the time goes in v6:
time: 99.2 us; the launch traced here: 97.6 us
  blocking collectives  37.4 us (38%)
  starting transfers between devices  17.9 us (18%)
  local copies, waits for them, and re-layouts  15.4 us (16%)
  other arithmetic  11.6 us (12%)
  waiting for transfers between devices  8.78 us (9%)
  matrix products  5.89 us (6%)
    all_to_all x1, blocking collectives, body(): got = lax.all_to_all(send, 'trk', split_axis=0, concat_axis=0, tiled=True)  37.4 us
    ppermute x4, starting transfers between devices, from_behind(): return lax.ppermute(x, axis, [(i, (i + by) % size) for i in range(size)])  13.8 us
    ppermute x4, waiting for transfers between devices, from_behind(): return lax.ppermute(x, axis, [(i, (i + by) % size) for i in range(size)])  5.65 us
    reduce_sum x1, other arithmetic, panel(): return jnp.sum(sel * vals, axis=1)  5.4 us
    reduce_sum x2, local copies, waits for them, and re-layouts, panel(): return jnp.sum(sel * vals, axis=1)  5.16 us
    dot_general x1, matrix products, body(): lax.dot_general(left_flat, right_flat, (((1,), (1,)), ((), ())), precisio...  4.95 us
    all_to_all x1, starting transfers between devices, body(): lax.all_to_all(copies, 'cam', 0, 0, tiled=True).transpose((1, 0, 2))  4.18 us
    all_to_all x1, waiting for transfers between devices, body(): lax.all_to_all(copies, 'cam', 0, 0, tiled=True).transpose((1, 0, 2))  3.13 us
  transfers between devices with their start and end apart: 5, of which 2 were waited for; matrix products, arithmetic and copies ran while one was open for 2% of the time, Pallas kernels for 0%

profile of v6, /device:TPU:1, one launch (start us, length us, event | category | flops | bytes accessed | tf_op | source)
XLA Modules:
  0.0 97.6 jit_solution(16328793261828411361)
XLA Ops:
  0.0 0.7 convert_element_type.46
  0.7 0.9 pad_maximum_fusion
  1.6 0.2 copy.74
  1.9 0.2 copy.76
  2.2 0.1 copy.75
  2.3 0.1 slice.156
  2.4 0.1 copy.77
  2.5 0.1 maximum_bitcast_fusion.1
  2.6 0.1 copy.78
  2.8 37.4 %all_to_all.14 = f32[128,1,174]{2,1,0:T(1,128)S(1)} all-to-all(f32[128,1,174]{2,1,0:T(1,128)S(1)} %copy.78), channel_id=1, replica_groups=mesh['trk'=128,'cam'=4] {'trk'}, dimensions={0} | all-to-all | bytes 178176 | tf_op jit(solution)/shard_map/all_to_all | solution.py:34
  40.2 0.1 copy.79
  40.4 0.1 copy.83
  40.5 0.1 convert_element_type.48
  40.6 0.1 copy.81
  40.7 0.1 slice.162
  40.9 0.3 copy.80
  41.2 0.2 copy.82
  41.4 0.9 fusion
  42.3 0.8 broadcast_in_dim.12
  43.1 4.2 %all-to-all-start.1 = ((f32[4,28,768]{2,1,0:T(8,128)}), f32[4,28,768]{2,1,0:T(8,128)S(1)}, u32[]{:S(2)}, u32[]{:S(2)}) async-start(f32[4,28,768]{2,1,0:T(8,128)} %broadcast_in_dim.12), calls=%async_computation.1 | async-start | bytes 786432 | tf_op jit(solution)/shard_map/all_to_all | solution.py:44
  47.3 3.0 %collective-permute-start = (f32[256]{0:T(256)S(1)}, f32[256]{0:T(256)S(1)}, u32[]{:S(2)}, u32[]{:S(2)}) collective-permute-start(f32[256]{0:T(256)S(1)} %copy-done), channel_id=1, source_target_pairs={{0,8},{4,12},{8,16},{12,20},{16,24},{20,28},{24,32},{28,36},{32,40... | collective-permute-start | bytes 3080 | tf_op jit(solution)/shard_map/ppermute | solution.py:19
  50.4 3.1 %all-to-all-done.1 = f32[4,28,768]{2,1,0:T(8,128)S(1)} async-done(((f32[4,28,768]{2,1,0:T(8,128)}), f32[4,28,768]{2,1,0:T(8,128)S(1)}, u32[]{:S(2)}, u32[]{:S(2)}) %all-to-all-start.1) | async-done | bytes 344096 | tf_op jit(solution)/shard_map/all_to_all | solution.py:44
  53.6 0.3 add_reduce_fusion.4
  54.5 0.1 add_multiply_fusion.1
  55.0 0.5 multiply_add_fusion.2
  55.6 0.3 maximum_bitcast_fusion
  55.9 0.2 broadcast_in_dim.14
  56.2 0.1 mul.554
  56.2 0.2 mul.555
  56.5 0.1 mul.560
  56.6 0.2 mul.561
  56.8 0.6 compare_convert_fusion.1
  57.4 5.4 %multiply_reduce_fusion = (f32[64,9,768]{2,0,1:T(8,128)}, f32[64,9,768]{2,0,1:T(8,128)}) fusion(f32[9,12,768]{2,1,0:T(8,128)S(1)} %add_multiply_fusion, f32[64,12,768]{2,0,1:T(8,128)S(1)} %get-tuple-element.33, f32[9,12,768]{2,1,0:T(8,128)S(1)} %broadcast_in_dim.14, f32[64,12,768]{2,0,1:T(8,128)S(1)} %get-tuple-element.32), kind=kLoop, calls=%fused_computation | loop fusion | flops 20348928 | bytes 8921088 | tf_op jit(solution)/shard_map/reduce_sum | solution.py:94
  62.9 2.6 %copy.93 = f32[64,9,768]{2,1,0:T(8,128)S(1)} copy(f32[64,9,768]{2,0,1:T(8,128)} %get-tuple-element.39) | data formatting | bytes 3538944 | tf_op jit(solution)/shard_map/reduce_sum | solution.py:94
  65.4 1.6 %reshape.236 = f32[4,144,768,1]{2,1,0,3:T(8,128)} reshape(f32[64,9,768]{2,1,0:T(8,128)S(1)} %copy.93) | data formatting | bytes 3538944 | tf_op jit(solution)/shard_map/dot_general | solution.py:98
  67.0 2.6 %copy.90 = f32[64,9,768]{2,1,0:T(8,128)S(1)} copy(f32[64,9,768]{2,0,1:T(8,128)} %get-tuple-element.40) | data formatting | bytes 3538944 | tf_op jit(solution)/shard_map/reduce_sum | solution.py:94
  69.6 1.4 %reshape.235 = f32[4,144,768,1]{2,1,0,3:T(8,128)} reshape(f32[64,9,768]{2,1,0:T(8,128)S(1)} %copy.90) | data formatting | bytes 3538944 | tf_op jit(solution)/shard_map/dot_general | solution.py:98
  71.0 5.0 %fusion.3 = f32[4,4,144,144]{3,2,1,0:T(8,128)S(1)} fusion(f32[4,144,768,1]{2,1,0,3:T(8,128)} %reshape.236, f32[4,144,768,1]{2,1,0,3:T(8,128)} %reshape.235), kind=kOutput, calls=%fused_computation.8 | convolution fusion | flops 1528823808 | bytes 4866048 | tf_op jit(solution)/shard_map/dot_general | solution.py:98
  76.0 0.2 fusion.24
  76.1 0.7 broadcast_in_dim_squeeze.16
  76.8 0.7 broadcast_in_dim_squeeze.19
  77.5 0.7 broadcast_in_dim_squeeze.18
  78.2 5.3 %collective-permute-start.2 = (f32[1,1,4,20736]{3,1,2,0:T(1,128)S(1)}, f32[1,1,4,20736]{3,1,2,0:T(1,128)S(1)}, u32[]{:S(2)}, u32[]{:S(2)}) collective-permute-start(f32[1,1,4,20736]{3,1,2,0:T(1,128)S(1)} %broadcast_in_dim_squeeze.18), channel_id=1, source_target_pairs={{0,508},{4,0},{8,4},{12,8},{16,12},{20,16},{24,20},{28,24},{32,28}... | collective-permute-start | bytes 995336 | tf_op jit(solution)/shard_map/ppermute | solution.py:19
  83.5 3.2 %collective-permute-start.3 = (f32[1,1,4,20736]{3,1,2,0:T(1,128)S(1)}, f32[1,1,4,20736]{3,1,2,0:T(1,128)S(1)}, u32[]{:S(2)}, u32[]{:S(2)}) collective-permute-start(f32[1,1,4,20736]{3,1,2,0:T(1,128)S(1)} %broadcast_in_dim_squeeze.19), channel_id=1, source_target_pairs={{0,504},{4,508},{8,0},{12,4},{16,8},{20,12},{24,16},{28,20},{32,24... | collective-permute-start | bytes 995336 | tf_op jit(solution)/shard_map/ppermute | solution.py:19
  86.7 2.2 %collective-permute-start.1 = (f32[1,1,4,20736]{3,1,2,0:T(1,128)S(1)}, f32[1,1,4,20736]{3,1,2,0:T(1,128)}, u32[]{:S(2)}, u32[]{:S(2)}) collective-permute-start(f32[1,1,4,20736]{3,1,2,0:T(1,128)S(1)} %broadcast_in_dim_squeeze.16), channel_id=1, source_target_pairs={{0,4},{4,8},{8,12},{12,16},{16,20},{20,24},{24,28},{28,32},{32,36}... | collective-permute-start | bytes 995336 | tf_op jit(solution)/shard_map/ppermute | solution.py:19
  88.9 0.7 broadcast_in_dim_squeeze.17
  89.6 5.6 %collective-permute-done.3 = f32[1,1,4,20736]{3,1,2,0:T(1,128)S(1)} collective-permute-done((f32[1,1,4,20736]{3,1,2,0:T(1,128)S(1)}, f32[1,1,4,20736]{3,1,2,0:T(1,128)S(1)}, u32[]{:S(2)}, u32[]{:S(2)}) %collective-permute-start.3) | collective-permute-done | bytes 331808 | tf_op jit(solution)/shard_map/ppermute | solution.py:19
  95.3 2.3 %pad_add_fusion = f32[1,1,7,20736]{3,1,2,0:T(1,128)} fusion(f32[1,1,4,20736]{3,1,2,0:T(1,128)S(1)} %collective-permute-done.3, f32[1,1,4,20736]{3,1,2,0:T(1,128)S(1)} %collective-permute-done.2, f32[1,1,4,20736]{3,1,2,0:T(1,128)S(1)} %broadcast_in_dim_squeeze.17, f32[1,1,4,20736]{3,1,2,0:T(1,128)} %collective-permute-done.1), kind=kLoop, calls=%fused_computation.10 | loop fusion | flops 435456 | bytes 1907712 | tf_op jit(solution)/shard_map/add | solution.py:110
  (52 shorter events, 1.1 us)
Async XLA Ops:
  40.3 7.0 %copy-start = (f32[256]{0:T(256)S(1)}, f32[256]{0:T(256)}, u32[]{:S(2)}) copy-start(f32[256]{0:T(256)} %param.9) | copy-start | bytes 3076
  43.1 10.4 %all-to-all-start.1 = ((f32[4,28,768]{2,1,0:T(8,128)}), f32[4,28,768]{2,1,0:T(8,128)S(1)}, u32[]{:S(2)}, u32[]{:S(2)}) async-start(f32[4,28,768]{2,1,0:T(8,128)} %broadcast_in_dim.12), calls=%async_computation.1 | async-start | bytes 786432 | tf_op jit(solution)/shard_map/all_to_all | solution.py:44
  47.3 7.7 %collective-permute-start = (f32[256]{0:T(256)S(1)}, f32[256]{0:T(256)S(1)}, u32[]{:S(2)}, u32[]{:S(2)}) collective-permute-start(f32[256]{0:T(256)S(1)} %copy-done), channel_id=1, source_target_pairs={{0,8},{4,12},{8,16},{12,20},{16,24},{20,28},{24,32},{28,36},{32,40... | collective-permute-start | bytes 3080 | tf_op jit(solution)/shard_map/ppermute | solution.py:19
  78.2 11.4 %collective-permute-start.2 = (f32[1,1,4,20736]{3,1,2,0:T(1,128)S(1)}, f32[1,1,4,20736]{3,1,2,0:T(1,128)S(1)}, u32[]{:S(2)}, u32[]{:S(2)}) collective-permute-start(f32[1,1,4,20736]{3,1,2,0:T(1,128)S(1)} %broadcast_in_dim_squeeze.18), channel_id=1, source_target_pairs={{0,508},{4,0},{8,4},{12,8},{16,12},{20,16},{24,20},{28,24},{32,28}... | collective-permute-start | bytes 995336 | tf_op jit(solution)/shard_map/ppermute | solution.py:19
  83.5 11.8 %collective-permute-start.3 = (f32[1,1,4,20736]{3,1,2,0:T(1,128)S(1)}, f32[1,1,4,20736]{3,1,2,0:T(1,128)S(1)}, u32[]{:S(2)}, u32[]{:S(2)}) collective-permute-start(f32[1,1,4,20736]{3,1,2,0:T(1,128)S(1)} %broadcast_in_dim_squeeze.19), channel_id=1, source_target_pairs={{0,504},{4,508},{8,0},{12,4},{16,8},{20,12},{24,16},{28,20},{32,24... | collective-permute-start | bytes 995336 | tf_op jit(solution)/shard_map/ppermute | solution.py:19
  86.7 8.6 %collective-permute-start.1 = (f32[1,1,4,20736]{3,1,2,0:T(1,128)S(1)}, f32[1,1,4,20736]{3,1,2,0:T(1,128)}, u32[]{:S(2)}, u32[]{:S(2)}) collective-permute-start(f32[1,1,4,20736]{3,1,2,0:T(1,128)S(1)} %broadcast_in_dim_squeeze.16), channel_id=1, source_target_pairs={{0,4},{4,8},{8,12},{12,16},{16,20},{20,24},{24,28},{28,32},{32,36}... | collective-permute-start | bytes 995336 | tf_op jit(solution)/shard_map/ppermute | solution.py:19

commit v7 on v3

--- a/solution.py
+++ b/solution.py
@@ -97,7 +97,10 @@
     right_flat = jnp.dot(reorder, panel(key_right, coup3), precision=lax.Precision.HIGH)
     left4 = left_flat.reshape((owners, TS, 3 * tracks))
     right4 = right_flat.reshape((owners, TS, 3 * tracks))
-    tiles = jnp.einsum("kic,mjc->kmij", left4, right4, precision=lax.Precision.HIGH)
+    product = lax.dot_general(
+        left4, right4, (((2,), (2,)), ((), ())), precision=lax.Precision.HIGH
+    )
+    tiles = product.transpose((0, 2, 1, 3))
     tiles = tiles.reshape((owners, owners, TS * TS))
     tile_count = 2 * HOPS + 1
     summed = jnp.zeros((tile_count, TS * TS), jnp.float32)

time: 101 us -> 100 us (0.990)
  local copies, waits for them, and re-layouts: 10.1 us -> 8.81 us
    dot_general x1, matrix products: 1.64 us -> 3.1 us  [body(): jnp.dot(reorder, panel(key_right, coup3), precision=lax.Precision.HIGH)]
    dot_general x1, matrix products: 3.1 us -> 1.64 us  [body(): jnp.dot(reorder, panel(key_left, left3), precision=lax.Precision.HIGH)]
    reshape x1 -> x0, other arithmetic: 1.36 us -> none  [body(): return summed.reshape((1, 1, tile_count, TS * TS))]
    add x0 -> x1, other arithmetic: none -> 1.25 us  [body(): summed = summed + jnp.pad(arrived, ((HOPS - distance, distance), (0, 0)))]
    slice x5 -> x1, local copies, waits for them, and re-layouts: 1.36 us -> 0.15 us  [body(): tiles[distance]]
  transfers between devices with their start and end apart: 6 -> 6, of which waited for: 4 -> 4; matrix products, arithmetic and copies ran while one was open for 6% -> 5% of each run, Pallas kernels for 0% -> 0%
where the time goes in v7:
time: 100 us; the launch traced here: 99.9 us
  starting transfers between devices  41.5 us (42%)
  waiting for transfers between devices  27.4 us (27%)
  other arithmetic  12.7 us (13%)
  matrix products  8.89 us (9%)
  local copies, waits for them, and re-layouts  8.81 us (9%)
    all_to_all x1, starting transfers between devices, body(): got = lax.all_to_all(send, 'trk', split_axis=0, concat_axis=0, tiled=True)  20.4 us
    ppermute x4, starting transfers between devices, from_behind(): return lax.ppermute(x, axis, [(i, (i + by) % size) for i in range(size)])  16.9 us
    all_to_all x1, waiting for transfers between devices, body(): got = lax.all_to_all(send, 'trk', split_axis=0, concat_axis=0, tiled=True)  14 us
    ppermute x4, waiting for transfers between devices, from_behind(): return lax.ppermute(x, axis, [(i, (i + by) % size) for i in range(size)])  7.17 us
    reduce_sum x1, other arithmetic, panel(): jnp.sum(sel[None] * values[:, None], axis=2).reshape((width, 3 * tracks))  6.81 us
    all_to_all x1, waiting for transfers between devices, body(): lax.all_to_all(copies, 'cam', 0, 0, tiled=True).transpose((1, 0, 2))  6.19 us
    all_to_all x1, starting transfers between devices, body(): lax.all_to_all(copies, 'cam', 0, 0, tiled=True).transpose((1, 0, 2))  4.18 us
    dot_general x1, matrix products, body(): lax.dot_general(left4, right4, (((2,), (2,)), ((), ())), precision=lax.Pr...  3.21 us
  transfers between devices with their start and end apart: 6, of which 4 were waited for; matrix products, arithmetic and copies ran while one was open for 5% of the time, Pallas kernels for 0%

profile of v7, /device:TPU:1, one launch (start us, length us, event | category | flops | bytes accessed | tf_op | source)
XLA Modules:
  0.0 99.9 jit_solution(1064538746262002578)
XLA Ops:
  0.0 0.7 convert_element_type.47
  0.7 0.9 pad_maximum_fusion
  1.6 0.2 copy.54
  1.9 0.2 copy.56
  2.2 0.1 copy.55
  2.3 0.1 slice.156
  2.4 0.1 copy.57
  2.5 0.1 maximum_bitcast_fusion.1
  2.6 0.8 copy.58
  3.4 20.4 %all-to-all-start = ((f32[128,1,174]{2,1,0:T(1,128)}), f32[128,1,174]{2,1,0:T(1,128)S(1)}, u32[]{:S(2)}, u32[]{:S(2)}) async-start(f32[128,1,174]{2,1,0:T(1,128)} %copy.58), calls=%async_computation | async-start | bytes 262144 | tf_op jit(solution)/shard_map/all_to_all | solution.py:34
  23.8 3.3 %collective-permute-start = (f32[256]{0:T(256)S(1)}, f32[256]{0:T(256)S(1)}, u32[]{:S(2)}, u32[]{:S(2)}) collective-permute-start(f32[256]{0:T(256)S(1)} %copy-done), channel_id=1, source_target_pairs={{0,8},{4,12},{8,16},{12,20},{16,24},{20,28},{24,32},{28,36},{32,40... | collective-permute-start | bytes 3080 | tf_op jit(solution)/shard_map/ppermute | solution.py:19
  27.1 14.0 %all-to-all-done = f32[128,1,174]{2,1,0:T(1,128)S(1)} async-done(((f32[128,1,174]{2,1,0:T(1,128)}), f32[128,1,174]{2,1,0:T(1,128)S(1)}, u32[]{:S(2)}, u32[]{:S(2)}) %all-to-all-start) | async-done | bytes 89120 | tf_op jit(solution)/shard_map/all_to_all | solution.py:34
  41.1 0.1 copy.59
  41.3 0.3 copy.60
  41.6 0.2 copy.62
  41.7 0.1 copy.61
  41.9 0.1 slice.162
  42.0 0.1 copy.63
  42.2 0.1 convert_element_type.49
  42.3 0.9 fusion
  43.2 0.8 broadcast_in_dim.2
  44.0 4.2 %all-to-all-start.1 = ((f32[4,28,768]{2,1,0:T(8,128)}), f32[4,28,768]{2,1,0:T(8,128)S(1)}, u32[]{:S(2)}, u32[]{:S(2)}) async-start(f32[4,28,768]{2,1,0:T(8,128)} %broadcast_in_dim.2), calls=%async_computation.1 | async-start | bytes 786432 | tf_op jit(solution)/shard_map/all_to_all | solution.py:44
  48.2 6.2 %all-to-all-done.1 = f32[4,28,768]{2,1,0:T(8,128)S(1)} async-done(((f32[4,28,768]{2,1,0:T(8,128)}), f32[4,28,768]{2,1,0:T(8,128)S(1)}, u32[]{:S(2)}, u32[]{:S(2)}) %all-to-all-start.1) | async-done | bytes 344096 | tf_op jit(solution)/shard_map/all_to_all | solution.py:44
  54.4 0.3 add_reduce_fusion.4
  55.3 0.1 add_multiply_fusion.1
  55.6 0.5 multiply_add_fusion.2
  56.1 0.3 maximum_bitcast_fusion
  56.4 1.0 mul.587
  57.7 0.2 mul.593
  58.0 0.2 mul.599
  58.5 0.6 compare_convert_fusion.1
  59.0 0.8 add_multiply_fusion
  59.9 6.8 %multiply_reduce_fusion = (f32[9,64,768]{2,1,0:T(8,128)}, f32[9,64,768]{2,1,0:T(8,128)S(1)}) fusion(f32[9,12,768]{2,1,0:T(8,128)} %add_multiply_fusion, f32[64,12,768]{2,0,1:T(8,128)S(1)} %get-tuple-element.33, f32[9,12,768]{2,1,0:T(8,128)} %mul.587, f32[64,12,768]{2,0,1:T(8,128)S(1)} %get-tuple-element.32), kind=kLoop, calls=%fused_computation | loop fusion | flops 20348928 | bytes 8921088 | tf_op jit(solution)/shard_map/reduce_sum | solution.py:91
  66.7 3.1 %fusion.10 = f32[4,144,768]{2,1,0:T(8,128)S(1)} fusion(f32[576,768,1]{1,0,2:T(8,128)} %bitcast.66, s32[4,144]{1,0:T(4,128)S(1)} %fusion.28), kind=kOutput, calls=%fused_computation.12 | convolution fusion | flops 1529155584 | bytes 3541248 | tf_op jit(solution)/shard_map/dot_general | solution.py:97
  69.8 1.6 %fusion.12 = f32[4,144,768]{2,1,0:T(8,128)S(1)} fusion(f32[576,768,1]{1,0,2:T(8,128)S(1)} %bitcast.65, s32[4,144]{1,0:T(4,128)S(1)} %fusion.28), kind=kOutput, calls=%fused_computation.13 | convolution fusion | flops 1529155584 | bytes 3541248 | tf_op jit(solution)/shard_map/dot_general | solution.py:96
  71.5 3.2 %fusion.4 = f32[4,4,144,144]{3,2,1,0:T(8,128)S(1)} fusion(f32[4,144,768]{2,1,0:T(8,128)S(1)} %fusion.10, f32[4,144,768]{2,1,0:T(8,128)S(1)} %fusion.12), kind=kOutput, calls=%fused_computation.9 | convolution fusion | flops 1528823808 | bytes 4866048 | tf_op jit(solution)/shard_map/dot_general | solution.py:100
  74.7 0.2 fusion.41
  74.8 0.4 squeeze.11
  75.3 5.5 %collective-permute-start.1 = (f32[4,20736]{1,0:T(4,128)S(1)}, f32[4,20736]{1,0:T(4,128)S(1)}, u32[]{:S(2)}, u32[]{:S(2)}) collective-permute-start(f32[4,20736]{1,0:T(4,128)S(1)} %squeeze.11), channel_id=1, source_target_pairs={{0,4},{4,8},{8,12},{12,16},{16,20},{20,24},{24,28},{28,32},{32,36}... | collective-permute-start | bytes 995336 | tf_op jit(solution)/shard_map/ppermute | solution.py:19
  80.8 0.4 squeeze.13
  81.2 1.9 %collective-permute-start.2 = (f32[4,20736]{1,0:T(4,128)S(1)}, f32[4,20736]{1,0:T(4,128)S(1)}, u32[]{:S(2)}, u32[]{:S(2)}) collective-permute-start(f32[4,20736]{1,0:T(4,128)S(1)} %squeeze.13), channel_id=1, source_target_pairs={{0,508},{4,0},{8,4},{12,8},{16,12},{20,16},{24,20},{28,24},{32,28}... | collective-permute-start | bytes 995336 | tf_op jit(solution)/shard_map/ppermute | solution.py:19
  83.1 0.4 squeeze.14
  83.5 6.3 %collective-permute-start.3 = (f32[4,20736]{1,0:T(4,128)S(1)}, f32[4,20736]{1,0:T(4,128)}, u32[]{:S(2)}, u32[]{:S(2)}) collective-permute-start(f32[4,20736]{1,0:T(4,128)S(1)} %squeeze.14), channel_id=1, source_target_pairs={{0,504},{4,508},{8,0},{12,4},{16,8},{20,12},{24,16},{28,20},{32,24... | collective-permute-start | bytes 995336 | tf_op jit(solution)/shard_map/ppermute | solution.py:19
  89.8 0.4 squeeze.12
  90.2 1.2 %collective-permute-done.2 = f32[4,20736]{1,0:T(4,128)S(1)} collective-permute-done((f32[4,20736]{1,0:T(4,128)S(1)}, f32[4,20736]{1,0:T(4,128)S(1)}, u32[]{:S(2)}, u32[]{:S(2)}) %collective-permute-start.2) | collective-permute-done | bytes 331808 | tf_op jit(solution)/shard_map/ppermute | solution.py:19
  91.4 6.0 %collective-permute-done.3 = f32[4,20736]{1,0:T(4,128)} collective-permute-done((f32[4,20736]{1,0:T(4,128)S(1)}, f32[4,20736]{1,0:T(4,128)}, u32[]{:S(2)}, u32[]{:S(2)}) %collective-permute-start.3) | collective-permute-done | bytes 331808 | tf_op jit(solution)/shard_map/ppermute | solution.py:19
  97.4 1.3 %pad_add_fusion = f32[7,20736]{1,0:T(8,128)S(1)} fusion(f32[4,20736]{1,0:T(4,128)} %collective-permute-done.3, f32[4,20736]{1,0:T(4,128)S(1)} %collective-permute-done.2, f32[4,20736]{1,0:T(4,128)S(1)} %squeeze.12, f32[4,20736]{1,0:T(4,128)S(1)} %collective-permute-done.1), kind=kLoop, calls=%fused_computation.17 | loop fusion | flops 435456 | bytes 1907712 | tf_op jit(solution)/shard_map/add | solution.py:110
  98.6 1.2 %reshape.292 = f32[1,1,7,20736]{3,1,2,0:T(1,128)} reshape(f32[7,20736]{1,0:T(8,128)S(1)} %pad_add_fusion) | data formatting | bytes 1161216 | tf_op jit(solution)/shard_map/reshape | solution.py:111
  (53 shorter events, 1.2 us)
Async XLA Ops:
  1.8 22.0 %copy-start = (f32[256]{0:T(256)S(1)}, f32[256]{0:T(256)}, u32[]{:S(2)}) copy-start(f32[256]{0:T(256)} %param.9) | copy-start | bytes 3076
  3.4 37.7 %all-to-all-start = ((f32[128,1,174]{2,1,0:T(1,128)}), f32[128,1,174]{2,1,0:T(1,128)S(1)}, u32[]{:S(2)}, u32[]{:S(2)}) async-start(f32[128,1,174]{2,1,0:T(1,128)} %copy.58), calls=%async_computation | async-start | bytes 262144 | tf_op jit(solution)/shard_map/all_to_all | solution.py:34
  23.8 31.7 %collective-permute-start = (f32[256]{0:T(256)S(1)}, f32[256]{0:T(256)S(1)}, u32[]{:S(2)}, u32[]{:S(2)}) collective-permute-start(f32[256]{0:T(256)S(1)} %copy-done), channel_id=1, source_target_pairs={{0,8},{4,12},{8,16},{12,20},{16,24},{20,28},{24,32},{28,36},{32,40... | collective-permute-start | bytes 3080 | tf_op jit(solution)/shard_map/ppermute | solution.py:19
  44.0 10.4 %all-to-all-start.1 = ((f32[4,28,768]{2,1,0:T(8,128)}), f32[4,28,768]{2,1,0:T(8,128)S(1)}, u32[]{:S(2)}, u32[]{:S(2)}) async-start(f32[4,28,768]{2,1,0:T(8,128)} %broadcast_in_dim.2), calls=%async_computation.1 | async-start | bytes 786432 | tf_op jit(solution)/shard_map/all_to_all | solution.py:44
  75.3 15.0 %collective-permute-start.1 = (f32[4,20736]{1,0:T(4,128)S(1)}, f32[4,20736]{1,0:T(4,128)S(1)}, u32[]{:S(2)}, u32[]{:S(2)}) collective-permute-start(f32[4,20736]{1,0:T(4,128)S(1)} %squeeze.11), channel_id=1, source_target_pairs={{0,4},{4,8},{8,12},{12,16},{16,20},{20,24},{24,28},{28,32},{32,36}... | collective-permute-start | bytes 995336 | tf_op jit(solution)/shard_map/ppermute | solution.py:19
  81.2 10.2 %collective-permute-start.2 = (f32[4,20736]{1,0:T(4,128)S(1)}, f32[4,20736]{1,0:T(4,128)S(1)}, u32[]{:S(2)}, u32[]{:S(2)}) collective-permute-start(f32[4,20736]{1,0:T(4,128)S(1)} %squeeze.13), channel_id=1, source_target_pairs={{0,508},{4,0},{8,4},{12,8},{16,12},{20,16},{24,20},{28,24},{32,28}... | collective-permute-start | bytes 995336 | tf_op jit(solution)/shard_map/ppermute | solution.py:19
  83.5 13.9 %collective-permute-start.3 = (f32[4,20736]{1,0:T(4,128)S(1)}, f32[4,20736]{1,0:T(4,128)}, u32[]{:S(2)}, u32[]{:S(2)}) collective-permute-start(f32[4,20736]{1,0:T(4,128)S(1)} %squeeze.14), channel_id=1, source_target_pairs={{0,504},{4,508},{8,0},{12,4},{16,8},{20,12},{24,16},{28,20},{32,24... | collective-permute-start | bytes 995336 | tf_op jit(solution)/shard_map/ppermute | solution.py:19

commit v8 on v1

--- a/solution.py
+++ b/solution.py
@@ -6,7 +6,7 @@
 CAMERAS_PER_BLK = 16
 TS = 144
 HOPS = 3
-SHIFT = 2
+SHIFT = 1
 CAM_BY_ALL_TO_ALL = True
 
 

time: 98.5 us -> 103 us (1.046)
  the two profiles are of different devices: /device:TPU:1 before, /device:TPU:8 now
where the time goes in v8:
time: 103 us
  blocking collectives  37.9 us (37%)
  starting transfers between devices  17.8 us (17%)
  local copies, waits for them, and re-layouts  15.4 us (15%)
  waiting for transfers between devices  14.7 us (14%)
  other arithmetic  10.5 us (10%)
  matrix products  5.89 us (6%)
    all_to_all x1, blocking collectives, body(): got = lax.all_to_all(send, 'trk', split_axis=0, concat_axis=0, tiled=True)  37.9 us
    ppermute x4, starting transfers between devices, from_behind(): return lax.ppermute(x, axis, [(i, (i + by) % size) for i in range(size)])  12.9 us
    ppermute x4, waiting for transfers between devices, from_behind(): return lax.ppermute(x, axis, [(i, (i + by) % size) for i in range(size)])  10.9 us
    reduce_sum x1, other arithmetic, panel(): return jnp.sum(sel * vals, axis=1)  5.4 us
    reduce_sum x2, local copies, waits for them, and re-layouts, panel(): return jnp.sum(sel * vals, axis=1)  5.16 us
    dot_general x1, matrix products, body(): lax.dot_general(left_flat, right_flat, (((1,), (1,)), ((), ())), precisio...  4.95 us
    all_to_all x1, starting transfers between devices, body(): lax.all_to_all(copies, 'cam', 0, 0, tiled=True).transpose((1, 0, 2))  4.91 us
    all_to_all x1, waiting for transfers between devices, body(): lax.all_to_all(copies, 'cam', 0, 0, tiled=True).transpose((1, 0, 2))  3.76 us
  transfers between devices with their start and end apart: 5, of which 5 were waited for; matrix products, arithmetic and copies ran while one was open for 2% of the time, Pallas kernels for 0%

profile of v8, /device:TPU:8, one launch (start us, length us, event | category | flops | bytes accessed | tf_op | source)
XLA Modules:
  0.0 102.7 jit_solution(13394091592215204042)
XLA Ops:
  0.0 0.7 convert_element_type.46
  0.7 0.9 pad_maximum_fusion
  1.6 0.2 copy.54
  1.9 0.2 copy.56
  2.2 0.1 copy.55
  2.4 0.1 maximum_bitcast_fusion.1
  2.5 0.1 copy.58
  2.6 37.9 %all_to_all.14 = f32[128,1,174]{2,1,0:T(1,128)S(1)} all-to-all(f32[128,1,174]{2,1,0:T(1,128)S(1)} %copy.58), channel_id=1, replica_groups=mesh['trk'=128,'cam'=4] {'trk'}, dimensions={0} | all-to-all | bytes 178176 | tf_op jit(solution)/shard_map/all_to_all | solution.py:34
  40.5 0.1 copy.59
  40.6 0.1 copy.63
  40.8 0.1 convert_element_type.48
  40.9 0.1 copy.61
  41.0 0.1 slice.162
  41.2 0.3 copy.60
  41.5 0.2 copy.62
  41.7 0.9 fusion
  42.6 0.8 broadcast_in_dim.12
  43.4 4.9 %all-to-all-start.1 = ((f32[4,28,768]{2,1,0:T(8,128)}), f32[4,28,768]{2,1,0:T(8,128)S(1)}, u32[]{:S(2)}, u32[]{:S(2)}) async-start(f32[4,28,768]{2,1,0:T(8,128)} %broadcast_in_dim.12), calls=%async_computation.1 | async-start | bytes 786432 | tf_op jit(solution)/shard_map/all_to_all | solution.py:44
  48.3 2.1 %collective-permute-start = (f32[256]{0:T(256)S(1)}, f32[256]{0:T(256)S(1)}, u32[]{:S(2)}, u32[]{:S(2)}) collective-permute-start(f32[256]{0:T(256)S(1)} %copy-done), channel_id=1, source_target_pairs={{0,4},{4,8},{8,12},{12,16},{16,20},{20,24},{24,28},{28,32},{32,36}... | collective-permute-start | bytes 3080 | tf_op jit(solution)/shard_map/ppermute | solution.py:19
  50.5 3.8 %all-to-all-done.1 = f32[4,28,768]{2,1,0:T(8,128)S(1)} async-done(((f32[4,28,768]{2,1,0:T(8,128)}), f32[4,28,768]{2,1,0:T(8,128)S(1)}, u32[]{:S(2)}, u32[]{:S(2)}) %all-to-all-start.1) | async-done | bytes 344096 | tf_op jit(solution)/shard_map/all_to_all | solution.py:44
  54.3 0.3 add_reduce_fusion.4
  55.2 0.1 add_multiply_fusion.1
  55.7 0.8 collective-permute-done
  56.5 0.5 multiply_add_fusion.2
  57.1 0.3 maximum_bitcast_fusion
  57.4 0.2 broadcast_in_dim.14
  57.7 0.2 mul.555
  58.1 0.2 mul.561
  58.3 0.6 compare_convert_fusion.1
  58.9 5.4 %multiply_reduce_fusion = (f32[64,9,768]{2,0,1:T(8,128)}, f32[64,9,768]{2,0,1:T(8,128)}) fusion(f32[9,12,768]{2,1,0:T(8,128)S(1)} %add_multiply_fusion, f32[64,12,768]{2,0,1:T(8,128)S(1)} %get-tuple-element.33, f32[9,12,768]{2,1,0:T(8,128)S(1)} %broadcast_in_dim.14, f32[64,12,768]{2,0,1:T(8,128)S(1)} %get-tuple-element.32), kind=kLoop, calls=%fused_computation | loop fusion | flops 20348928 | bytes 8921088 | tf_op jit(solution)/shard_map/reduce_sum | solution.py:94
  64.3 2.6 %copy.73 = f32[64,9,768]{2,1,0:T(8,128)S(1)} copy(f32[64,9,768]{2,0,1:T(8,128)} %get-tuple-element.39) | data formatting | bytes 3538944 | tf_op jit(solution)/shard_map/reduce_sum | solution.py:94
  66.9 1.6 %reshape.240 = f32[4,144,768,1]{2,1,0,3:T(8,128)} reshape(f32[64,9,768]{2,1,0:T(8,128)S(1)} %copy.73) | data formatting | bytes 3538944 | tf_op jit(solution)/shard_map/dot_general | solution.py:98
  68.5 2.6 %copy.70 = f32[64,9,768]{2,1,0:T(8,128)S(1)} copy(f32[64,9,768]{2,0,1:T(8,128)} %get-tuple-element.40) | data formatting | bytes 3538944 | tf_op jit(solution)/shard_map/reduce_sum | solution.py:94
  71.1 1.4 %reshape.239 = f32[4,144,768,1]{2,1,0,3:T(8,128)} reshape(f32[64,9,768]{2,1,0:T(8,128)S(1)} %copy.70) | data formatting | bytes 3538944 | tf_op jit(solution)/shard_map/dot_general | solution.py:98
  72.5 5.0 %fusion.3 = f32[4,4,144,144]{3,2,1,0:T(8,128)S(1)} fusion(f32[4,144,768,1]{2,1,0,3:T(8,128)} %reshape.240, f32[4,144,768,1]{2,1,0,3:T(8,128)} %reshape.239), kind=kOutput, calls=%fused_computation.8 | convolution fusion | flops 1528823808 | bytes 4866048 | tf_op jit(solution)/shard_map/dot_general | solution.py:98
  77.5 0.2 fusion.24
  77.6 0.4 squeeze.11
  78.0 0.4 squeeze.14
  78.4 0.4 squeeze.12
  78.9 1.9 %collective-permute-start.2 = (f32[4,20736]{1,0:T(4,128)S(1)}, f32[4,20736]{1,0:T(4,128)S(1)}, u32[]{:S(2)}, u32[]{:S(2)}) collective-permute-start(f32[4,20736]{1,0:T(4,128)S(1)} %squeeze.12), channel_id=1, source_target_pairs={{0,4},{4,8},{8,12},{12,16},{16,20},{20,24},{24,28},{28,32},{32,36}... | collective-permute-start | bytes 995336 | tf_op jit(solution)/shard_map/ppermute | solution.py:19
  80.8 7.0 %collective-permute-start.3 = (f32[4,20736]{1,0:T(4,128)S(1)}, f32[4,20736]{1,0:T(4,128)S(1)}, u32[]{:S(2)}, u32[]{:S(2)}) collective-permute-start(f32[4,20736]{1,0:T(4,128)S(1)} %squeeze.14), channel_id=1, source_target_pairs={{0,508},{4,0},{8,4},{12,8},{16,12},{20,16},{24,20},{28,24},{32,28}... | collective-permute-start | bytes 995336 | tf_op jit(solution)/shard_map/ppermute | solution.py:19
  87.8 1.9 %collective-permute-start.1 = (f32[4,20736]{1,0:T(4,128)S(1)}, f32[4,20736]{1,0:T(4,128)}, u32[]{:S(2)}, u32[]{:S(2)}) collective-permute-start(f32[4,20736]{1,0:T(4,128)S(1)} %squeeze.11), channel_id=1, source_target_pairs={{0,8},{4,12},{8,16},{12,20},{16,24},{20,28},{24,32},{28,36},{32,40... | collective-permute-start | bytes 995336 | tf_op jit(solution)/shard_map/ppermute | solution.py:19
  89.7 0.4 squeeze.13
  90.1 0.5 collective-permute-done.2
  90.6 1.8 %collective-permute-done.3 = f32[4,20736]{1,0:T(4,128)S(1)} collective-permute-done((f32[4,20736]{1,0:T(4,128)S(1)}, f32[4,20736]{1,0:T(4,128)S(1)}, u32[]{:S(2)}, u32[]{:S(2)}) %collective-permute-start.3) | collective-permute-done | bytes 331808 | tf_op jit(solution)/shard_map/ppermute | solution.py:19
  92.4 7.8 %collective-permute-done.1 = f32[4,20736]{1,0:T(4,128)} collective-permute-done((f32[4,20736]{1,0:T(4,128)S(1)}, f32[4,20736]{1,0:T(4,128)}, u32[]{:S(2)}, u32[]{:S(2)}) %collective-permute-start.1) | collective-permute-done | bytes 331808 | tf_op jit(solution)/shard_map/ppermute | solution.py:19
  100.2 1.3 %pad_add_fusion = f32[7,20736]{1,0:T(8,128)S(1)} fusion(f32[4,20736]{1,0:T(4,128)S(1)} %collective-permute-done.3, f32[4,20736]{1,0:T(4,128)S(1)} %squeeze.13, f32[4,20736]{1,0:T(4,128)S(1)} %collective-permute-done.2, f32[4,20736]{1,0:T(4,128)} %collective-permute-done.1), kind=kLoop, calls=%fused_computation.10 | loop fusion | flops 435456 | bytes 1907712 | tf_op jit(solution)/shard_map/add | solution.py:108
  101.5 1.2 %reshape.235 = f32[1,1,7,20736]{3,1,2,0:T(1,128)} reshape(f32[7,20736]{1,0:T(8,128)S(1)} %pad_add_fusion) | data formatting | bytes 1161216 | tf_op jit(solution)/shard_map/reshape | solution.py:109
  (52 shorter events, 1.3 us)
Async XLA Ops:
  40.6 7.7 %copy-start = (f32[256]{0:T(256)S(1)}, f32[256]{0:T(256)}, u32[]{:S(2)}) copy-start(f32[256]{0:T(256)} %param.9) | copy-start | bytes 3076
  43.4 10.8 %all-to-all-start.1 = ((f32[4,28,768]{2,1,0:T(8,128)}), f32[4,28,768]{2,1,0:T(8,128)S(1)}, u32[]{:S(2)}, u32[]{:S(2)}) async-start(f32[4,28,768]{2,1,0:T(8,128)} %broadcast_in_dim.12), calls=%async_computation.1 | async-start | bytes 786432 | tf_op jit(solution)/shard_map/all_to_all | solution.py:44
  48.3 8.2 %collective-permute-start = (f32[256]{0:T(256)S(1)}, f32[256]{0:T(256)S(1)}, u32[]{:S(2)}, u32[]{:S(2)}) collective-permute-start(f32[256]{0:T(256)S(1)} %copy-done), channel_id=1, source_target_pairs={{0,4},{4,8},{8,12},{12,16},{16,20},{20,24},{24,28},{28,32},{32,36}... | collective-permute-start | bytes 3080 | tf_op jit(solution)/shard_map/ppermute | solution.py:19
  78.9 11.8 %collective-permute-start.2 = (f32[4,20736]{1,0:T(4,128)S(1)}, f32[4,20736]{1,0:T(4,128)S(1)}, u32[]{:S(2)}, u32[]{:S(2)}) collective-permute-start(f32[4,20736]{1,0:T(4,128)S(1)} %squeeze.12), channel_id=1, source_target_pairs={{0,4},{4,8},{8,12},{12,16},{16,20},{20,24},{24,28},{28,32},{32,36}... | collective-permute-start | bytes 995336 | tf_op jit(solution)/shard_map/ppermute | solution.py:19
  80.8 11.6 %collective-permute-start.3 = (f32[4,20736]{1,0:T(4,128)S(1)}, f32[4,20736]{1,0:T(4,128)S(1)}, u32[]{:S(2)}, u32[]{:S(2)}) collective-permute-start(f32[4,20736]{1,0:T(4,128)S(1)} %squeeze.14), channel_id=1, source_target_pairs={{0,508},{4,0},{8,4},{12,8},{16,12},{20,16},{24,20},{28,24},{32,28}... | collective-permute-start | bytes 995336 | tf_op jit(solution)/shard_map/ppermute | solution.py:19
  87.8 12.4 %collective-permute-start.1 = (f32[4,20736]{1,0:T(4,128)S(1)}, f32[4,20736]{1,0:T(4,128)}, u32[]{:S(2)}, u32[]{:S(2)}) collective-permute-start(f32[4,20736]{1,0:T(4,128)S(1)} %squeeze.11), channel_id=1, source_target_pairs={{0,8},{4,12},{8,16},{12,20},{16,24},{20,28},{24,32},{28,36},{32,40... | collective-permute-start | bytes 995336 | tf_op jit(solution)/shard_map/ppermute | solution.py:19

commit v9 on v5

--- a/solution.py
+++ b/solution.py
@@ -24,10 +24,8 @@
     tracks = damping.shape[0]
     rows = residuals.shape[1]
     per_dest = rows // strip_count
-    magnitude = jnp.sqrt(residuals[0] * residuals[0] + residuals[1] * residuals[1])
-    weight = obs_index[2].astype(jnp.float32) * (HUBER_DELTA / jnp.maximum(magnitude, HUBER_DELTA))
     fields = jnp.concatenate(
-        [camera_jac, point_jac, weight[None], obs_index[:2].astype(jnp.float32)], axis=0
+        [residuals, camera_jac, point_jac, obs_index.astype(jnp.float32)], axis=0
     )
     nf = fields.shape[0]
     send = fields.reshape((nf, strip_count, per_dest)).transpose((1, 0, 2))
@@ -35,10 +33,12 @@
     send = jnp.roll(send, SHIFT, axis=0)
     got = lax.all_to_all(send, "trk", split_axis=0, concat_axis=0, tiled=True)
     got = got.reshape((strip_count, nf, per_dest)).transpose((1, 0, 2)).reshape((nf, rows))
-    position = got[nf - 2].astype(jnp.int32)
+    position = got[nf - 3].astype(jnp.int32)
     local_slots = rows // tracks
     onehot = (position[:, None] == jnp.arange(rows, dtype=jnp.int32)[None, :]).astype(jnp.float32)
-    kept = jnp.concatenate([got[: nf - 2], got[nf - 1 :]], axis=0)
+    magnitude = jnp.sqrt(got[0] * got[0] + got[1] * got[1])
+    weight = got[nf - 1] * (HUBER_DELTA / jnp.maximum(magnitude, HUBER_DELTA))
+    kept = jnp.concatenate([got[2 : nf - 3], weight[None], got[nf - 2 : nf - 1]], axis=0)
     placed = jnp.dot(kept, onehot, precision=lax.Precision.HIGHEST)
     if CAM_BY_ALL_TO_ALL:
         n_cam = lax.axis_size("cam")

time: 101 us -> 98.7 us (0.977)
  local copies, waits for them, and re-layouts: 17.6 us -> 15.7 us
    unnamed x13 -> x10, local copies, waits for them, and re-layouts: 1.17 us -> 0.11 us
    concatenate x8 -> x1, local copies, waits for them, and re-layouts: 1.21 us -> 0.18 us  [body(): jnp.concatenate([residuals, camera_jac, point_jac, obs_index.astype(jnp.f...]
where the time goes in v9:
time: 98.7 us; the launch traced here: 97.1 us
  blocking collectives  37.4 us (38%)
  starting transfers between devices  17.9 us (18%)
  local copies, waits for them, and re-layouts  15.7 us (16%)
  other arithmetic  10.5 us (11%)
  waiting for transfers between devices  9.05 us (9%)
  matrix products  5.89 us (6%)
    all_to_all x1, blocking collectives, body(): got = lax.all_to_all(send, 'trk', split_axis=0, concat_axis=0, tiled=True)  37.4 us
    ppermute x4, starting transfers between devices, from_behind(): return lax.ppermute(x, axis, [(i, (i + by) % size) for i in range(size)])  13.7 us
    ppermute x4, waiting for transfers between devices, from_behind(): return lax.ppermute(x, axis, [(i, (i + by) % size) for i in range(size)])  5.92 us
    reduce_sum x1, other arithmetic, panel(): return jnp.sum(sel * vals, axis=1)  5.4 us
    reduce_sum x2, local copies, waits for them, and re-layouts, panel(): return jnp.sum(sel * vals, axis=1)  5.16 us
    dot_general x1, matrix products, body(): lax.dot_general(left_flat, right_flat, (((1,), (1,)), ((), ())), precisio...  4.95 us
    all_to_all x1, starting transfers between devices, body(): lax.all_to_all(copies, 'cam', 0, 0, tiled=True).transpose((1, 0, 2))  4.18 us
    all_to_all x1, waiting for transfers between devices, body(): lax.all_to_all(copies, 'cam', 0, 0, tiled=True).transpose((1, 0, 2))  3.13 us
  transfers between devices with their start and end apart: 5, of which 2 were waited for; matrix products, arithmetic and copies ran while one was open for 2% of the time, Pallas kernels for 0%

profile of v9, /device:TPU:1, one launch (start us, length us, event | category | flops | bytes accessed | tf_op | source)
XLA Modules:
  0.0 97.1 jit_solution(3218025239618895306)
XLA Ops:
  0.0 0.7 convert_element_type.46
  0.7 0.9 pad_maximum_fusion
  1.6 0.2 copy.61
  1.9 0.2 copy.63
  2.2 0.1 copy.62
  2.3 0.1 slice.156
  2.4 0.1 copy.64
  2.5 0.1 maximum_bitcast_fusion.1
  2.6 0.1 copy.65
  2.8 37.4 %all_to_all.14 = f32[128,1,174]{2,1,0:T(1,128)S(1)} all-to-all(f32[128,1,174]{2,1,0:T(1,128)S(1)} %copy.65), channel_id=1, replica_groups=mesh['trk'=128,'cam'=4] {'trk'}, dimensions={0} | all-to-all | bytes 178176 | tf_op jit(solution)/shard_map/all_to_all | solution.py:34
  40.3 0.1 copy.68
  40.5 0.1 reshape.264
  40.6 0.1 copy.71
  40.7 0.1 convert_element_type.48
  40.9 0.1 copy.69
  41.0 0.1 slice.165
  41.1 0.2 copy.67
  41.4 0.1 copy.70
  41.6 0.9 fusion
  42.5 0.8 broadcast_in_dim.12
  43.3 4.2 %all-to-all-start.1 = ((f32[4,26,768]{2,1,0:T(8,128)}), f32[4,26,768]{2,1,0:T(8,128)S(1)}, u32[]{:S(2)}, u32[]{:S(2)}) async-start(f32[4,26,768]{2,1,0:T(8,128)} %broadcast_in_dim.12), calls=%async_computation.1 | async-start | bytes 786432 | tf_op jit(solution)/shard_map/all_to_all | solution.py:46
  47.5 3.0 %collective-permute-start = (f32[256]{0:T(256)S(1)}, f32[256]{0:T(256)S(1)}, u32[]{:S(2)}, u32[]{:S(2)}) collective-permute-start(f32[256]{0:T(256)S(1)} %copy-done), channel_id=1, source_target_pairs={{0,8},{4,12},{8,16},{12,20},{16,24},{20,28},{24,32},{28,36},{32,40... | collective-permute-start | bytes 3080 | tf_op jit(solution)/shard_map/ppermute | solution.py:19
  50.6 3.1 %all-to-all-done.1 = f32[4,26,768]{2,1,0:T(8,128)S(1)} async-done(((f32[4,26,768]{2,1,0:T(8,128)}), f32[4,26,768]{2,1,0:T(8,128)S(1)}, u32[]{:S(2)}, u32[]{:S(2)}) %all-to-all-start.1) | async-done | bytes 319520 | tf_op jit(solution)/shard_map/all_to_all | solution.py:46
  53.8 0.3 add_reduce_fusion.4
  54.6 0.1 add_multiply_fusion.1
  55.2 0.5 multiply_add_fusion.2
  55.7 0.3 maximum_bitcast_fusion
  56.1 0.2 broadcast_in_dim.14
  56.4 0.2 mul.495
  56.7 0.2 mul.501
  56.9 0.6 compare_convert_fusion.1
  57.6 5.4 %multiply_reduce_fusion = (f32[64,9,768]{2,0,1:T(8,128)}, f32[64,9,768]{2,0,1:T(8,128)}) fusion(f32[9,12,768]{2,1,0:T(8,128)S(1)} %add_multiply_fusion, f32[64,12,768]{2,0,1:T(8,128)S(1)} %get-tuple-element.36, f32[9,12,768]{2,1,0:T(8,128)S(1)} %broadcast_in_dim.14, f32[64,12,768]{2,0,1:T(8,128)S(1)} %get-tuple-element.35), kind=kLoop, calls=%fused_computation | loop fusion | flops 20348928 | bytes 8921088 | tf_op jit(solution)/shard_map/reduce_sum | solution.py:93
  63.0 2.6 %copy.81 = f32[64,9,768]{2,1,0:T(8,128)S(1)} copy(f32[64,9,768]{2,0,1:T(8,128)} %get-tuple-element.42) | data formatting | bytes 3538944 | tf_op jit(solution)/shard_map/reduce_sum | solution.py:93
  65.6 1.6 %reshape.266 = f32[4,144,768,1]{2,1,0,3:T(8,128)} reshape(f32[64,9,768]{2,1,0:T(8,128)S(1)} %copy.81) | data formatting | bytes 3538944 | tf_op jit(solution)/shard_map/dot_general | solution.py:97
  67.2 2.6 %copy.78 = f32[64,9,768]{2,1,0:T(8,128)S(1)} copy(f32[64,9,768]{2,0,1:T(8,128)} %get-tuple-element.43) | data formatting | bytes 3538944 | tf_op jit(solution)/shard_map/reduce_sum | solution.py:93
  69.8 1.4 %reshape.265 = f32[4,144,768,1]{2,1,0,3:T(8,128)} reshape(f32[64,9,768]{2,1,0:T(8,128)S(1)} %copy.78) | data formatting | bytes 3538944 | tf_op jit(solution)/shard_map/dot_general | solution.py:97
  71.1 5.0 %fusion.3 = f32[4,4,144,144]{3,2,1,0:T(8,128)S(1)} fusion(f32[4,144,768,1]{2,1,0,3:T(8,128)} %reshape.266, f32[4,144,768,1]{2,1,0,3:T(8,128)} %reshape.265), kind=kOutput, calls=%fused_computation.8 | convolution fusion | flops 1528823808 | bytes 4866048 | tf_op jit(solution)/shard_map/dot_general | solution.py:97
  76.1 0.2 fusion.29
  76.3 0.4 squeeze.11
  76.7 0.4 squeeze.14
  77.1 0.4 squeeze.13
  77.5 5.3 %collective-permute-start.2 = (f32[4,20736]{1,0:T(4,128)S(1)}, f32[4,20736]{1,0:T(4,128)S(1)}, u32[]{:S(2)}, u32[]{:S(2)}) collective-permute-start(f32[4,20736]{1,0:T(4,128)S(1)} %squeeze.13), channel_id=1, source_target_pairs={{0,508},{4,0},{8,4},{12,8},{16,12},{20,16},{24,20},{28,24},{32,28}... | collective-permute-start | bytes 995336 | tf_op jit(solution)/shard_map/ppermute | solution.py:19
  82.8 3.2 %collective-permute-start.3 = (f32[4,20736]{1,0:T(4,128)S(1)}, f32[4,20736]{1,0:T(4,128)S(1)}, u32[]{:S(2)}, u32[]{:S(2)}) collective-permute-start(f32[4,20736]{1,0:T(4,128)S(1)} %squeeze.14), channel_id=1, source_target_pairs={{0,504},{4,508},{8,0},{12,4},{16,8},{20,12},{24,16},{28,20},{32,24... | collective-permute-start | bytes 995336 | tf_op jit(solution)/shard_map/ppermute | solution.py:19
  86.0 2.2 %collective-permute-start.1 = (f32[4,20736]{1,0:T(4,128)S(1)}, f32[4,20736]{1,0:T(4,128)}, u32[]{:S(2)}, u32[]{:S(2)}) collective-permute-start(f32[4,20736]{1,0:T(4,128)S(1)} %squeeze.11), channel_id=1, source_target_pairs={{0,4},{4,8},{8,12},{12,16},{16,20},{20,24},{24,28},{28,32},{32,36}... | collective-permute-start | bytes 995336 | tf_op jit(solution)/shard_map/ppermute | solution.py:19
  88.3 0.4 squeeze.12
  88.7 5.9 %collective-permute-done.3 = f32[4,20736]{1,0:T(4,128)S(1)} collective-permute-done((f32[4,20736]{1,0:T(4,128)S(1)}, f32[4,20736]{1,0:T(4,128)S(1)}, u32[]{:S(2)}, u32[]{:S(2)}) %collective-permute-start.3) | collective-permute-done | bytes 331808 | tf_op jit(solution)/shard_map/ppermute | solution.py:19
  94.6 1.3 %pad_add_fusion = f32[7,20736]{1,0:T(8,128)S(1)} fusion(f32[4,20736]{1,0:T(4,128)S(1)} %collective-permute-done.3, f32[4,20736]{1,0:T(4,128)S(1)} %collective-permute-done.2, f32[4,20736]{1,0:T(4,128)S(1)} %squeeze.12, f32[4,20736]{1,0:T(4,128)} %collective-permute-done.1), kind=kLoop, calls=%fused_computation.10 | loop fusion | flops 435456 | bytes 1907712 | tf_op jit(solution)/shard_map/add | solution.py:107
  95.9 1.2 %reshape.261 = f32[1,1,7,20736]{3,1,2,0:T(1,128)} reshape(f32[7,20736]{1,0:T(8,128)S(1)} %pad_add_fusion) | data formatting | bytes 1161216 | tf_op jit(solution)/shard_map/reshape | solution.py:108
  (54 shorter events, 1.3 us)
Async XLA Ops:
  40.3 7.2 %copy-start = (f32[256]{0:T(256)S(1)}, f32[256]{0:T(256)}, u32[]{:S(2)}) copy-start(f32[256]{0:T(256)} %param.9) | copy-start | bytes 3076
  43.3 10.4 %all-to-all-start.1 = ((f32[4,26,768]{2,1,0:T(8,128)}), f32[4,26,768]{2,1,0:T(8,128)S(1)}, u32[]{:S(2)}, u32[]{:S(2)}) async-start(f32[4,26,768]{2,1,0:T(8,128)} %broadcast_in_dim.12), calls=%async_computation.1 | async-start | bytes 786432 | tf_op jit(solution)/shard_map/all_to_all | solution.py:46
  47.5 7.7 %collective-permute-start = (f32[256]{0:T(256)S(1)}, f32[256]{0:T(256)S(1)}, u32[]{:S(2)}, u32[]{:S(2)}) collective-permute-start(f32[256]{0:T(256)S(1)} %copy-done), channel_id=1, source_target_pairs={{0,8},{4,12},{8,16},{12,20},{16,24},{20,28},{24,32},{28,36},{32,40... | collective-permute-start | bytes 3080 | tf_op jit(solution)/shard_map/ppermute | solution.py:19
  77.5 11.2 %collective-permute-start.2 = (f32[4,20736]{1,0:T(4,128)S(1)}, f32[4,20736]{1,0:T(4,128)S(1)}, u32[]{:S(2)}, u32[]{:S(2)}) collective-permute-start(f32[4,20736]{1,0:T(4,128)S(1)} %squeeze.13), channel_id=1, source_target_pairs={{0,508},{4,0},{8,4},{12,8},{16,12},{20,16},{24,20},{28,24},{32,28}... | collective-permute-start | bytes 995336 | tf_op jit(solution)/shard_map/ppermute | solution.py:19
  82.8 11.8 %collective-permute-start.3 = (f32[4,20736]{1,0:T(4,128)S(1)}, f32[4,20736]{1,0:T(4,128)S(1)}, u32[]{:S(2)}, u32[]{:S(2)}) collective-permute-start(f32[4,20736]{1,0:T(4,128)S(1)} %squeeze.14), channel_id=1, source_target_pairs={{0,504},{4,508},{8,0},{12,4},{16,8},{20,12},{24,16},{28,20},{32,24... | collective-permute-start | bytes 995336 | tf_op jit(solution)/shard_map/ppermute | solution.py:19
  86.0 8.6 %collective-permute-start.1 = (f32[4,20736]{1,0:T(4,128)S(1)}, f32[4,20736]{1,0:T(4,128)}, u32[]{:S(2)}, u32[]{:S(2)}) collective-permute-start(f32[4,20736]{1,0:T(4,128)S(1)} %squeeze.11), channel_id=1, source_target_pairs={{0,4},{4,8},{8,12},{12,16},{16,20},{20,24},{24,28},{28,32},{32,36}... | collective-permute-start | bytes 995336 | tf_op jit(solution)/shard_map/ppermute | solution.py:19

commit v10 on v1

--- a/solution.py
+++ b/solution.py
@@ -37,7 +37,7 @@
     local_slots = rows // tracks
     onehot = (position[:, None] == jnp.arange(rows, dtype=jnp.int32)[None, :]).astype(jnp.float32)
     kept = jnp.concatenate([got[: nf - 3], got[nf - 2 :]], axis=0)
-    placed = jnp.dot(kept, onehot, precision=lax.Precision.HIGHEST)
+    placed = jnp.dot(kept, onehot, precision=lax.Precision.HIGH)
     if CAM_BY_ALL_TO_ALL:
         n_cam = lax.axis_size("cam")
         copies = jnp.broadcast_to(placed[None], (n_cam,) + placed.shape)

time: 98.5 us -> 98.3 us (level)
  no operation moved by 1% of the time
where the time goes in v10:
time: 98.3 us; the launch traced here: 96.7 us
  blocking collectives  37.4 us (38%)
  starting transfers between devices  17.9 us (18%)
  local copies, waits for them, and re-layouts  15.5 us (16%)
  other arithmetic  10.5 us (11%)
  waiting for transfers between devices  9.05 us (9%)
  matrix products  5.66 us (6%)
    all_to_all x1, blocking collectives, body(): got = lax.all_to_all(send, 'trk', split_axis=0, concat_axis=0, tiled=True)  37.4 us
    ppermute x4, starting transfers between devices, from_behind(): return lax.ppermute(x, axis, [(i, (i + by) % size) for i in range(size)])  13.7 us
    ppermute x4, waiting for transfers between devices, from_behind(): return lax.ppermute(x, axis, [(i, (i + by) % size) for i in range(size)])  5.92 us
    reduce_sum x1, other arithmetic, panel(): return jnp.sum(sel * vals, axis=1)  5.4 us
    reduce_sum x2, local copies, waits for them, and re-layouts, panel(): return jnp.sum(sel * vals, axis=1)  5.16 us
    dot_general x1, matrix products, body(): lax.dot_general(left_flat, right_flat, (((1,), (1,)), ((), ())), precisio...  4.95 us
    all_to_all x1, starting transfers between devices, body(): lax.all_to_all(copies, 'cam', 0, 0, tiled=True).transpose((1, 0, 2))  4.18 us
    all_to_all x1, waiting for transfers between devices, body(): lax.all_to_all(copies, 'cam', 0, 0, tiled=True).transpose((1, 0, 2))  3.13 us
  transfers between devices with their start and end apart: 5, of which 2 were waited for; matrix products, arithmetic and copies ran while one was open for 2% of the time, Pallas kernels for 0%

profile of v10, /device:TPU:1, one launch (start us, length us, event | category | flops | bytes accessed | tf_op | source)
XLA Modules:
  0.0 96.7 jit_solution(12535852043526944185)
XLA Ops:
  0.0 0.7 convert_element_type.46
  0.7 0.9 pad_maximum_fusion
  1.6 0.2 copy.54
  1.9 0.2 copy.56
  2.2 0.1 copy.55
  2.3 0.1 slice.156
  2.4 0.1 copy.57
  2.5 0.1 maximum_bitcast_fusion.1
  2.6 0.1 copy.58
  2.8 37.4 %all_to_all.14 = f32[128,1,174]{2,1,0:T(1,128)S(1)} all-to-all(f32[128,1,174]{2,1,0:T(1,128)S(1)} %copy.58), channel_id=1, replica_groups=mesh['trk'=128,'cam'=4] {'trk'}, dimensions={0} | all-to-all | bytes 178176 | tf_op jit(solution)/shard_map/all_to_all | solution.py:34
  40.2 0.1 copy.59
  40.4 0.1 copy.63
  40.5 0.1 convert_element_type.48
  40.6 0.1 copy.61
  40.7 0.1 slice.162
  40.9 0.3 copy.60
  41.2 0.2 copy.62
  41.4 0.7 fusion
  42.1 0.8 broadcast_in_dim.12
  42.9 4.2 %all-to-all-start.1 = ((f32[4,28,768]{2,1,0:T(8,128)}), f32[4,28,768]{2,1,0:T(8,128)S(1)}, u32[]{:S(2)}, u32[]{:S(2)}) async-start(f32[4,28,768]{2,1,0:T(8,128)} %broadcast_in_dim.12), calls=%async_computation.1 | async-start | bytes 786432 | tf_op jit(solution)/shard_map/all_to_all | solution.py:44
  47.1 3.0 %collective-permute-start = (f32[256]{0:T(256)S(1)}, f32[256]{0:T(256)S(1)}, u32[]{:S(2)}, u32[]{:S(2)}) collective-permute-start(f32[256]{0:T(256)S(1)} %copy-done), channel_id=1, source_target_pairs={{0,8},{4,12},{8,16},{12,20},{16,24},{20,28},{24,32},{28,36},{32,40... | collective-permute-start | bytes 3080 | tf_op jit(solution)/shard_map/ppermute | solution.py:19
  50.2 3.1 %all-to-all-done.1 = f32[4,28,768]{2,1,0:T(8,128)S(1)} async-done(((f32[4,28,768]{2,1,0:T(8,128)}), f32[4,28,768]{2,1,0:T(8,128)S(1)}, u32[]{:S(2)}, u32[]{:S(2)}) %all-to-all-start.1) | async-done | bytes 344096 | tf_op jit(solution)/shard_map/all_to_all | solution.py:44
  53.3 0.3 add_reduce_fusion.4
  54.3 0.1 add_multiply_fusion.1
  54.8 0.5 multiply_add_fusion.2
  55.4 0.3 maximum_bitcast_fusion
  55.7 0.2 broadcast_in_dim.14
  55.9 0.1 mul.554
  56.0 0.2 mul.555
  56.3 0.2 mul.561
  56.6 0.6 compare_convert_fusion.1
  57.2 5.4 %multiply_reduce_fusion = (f32[64,9,768]{2,0,1:T(8,128)}, f32[64,9,768]{2,0,1:T(8,128)}) fusion(f32[9,12,768]{2,1,0:T(8,128)S(1)} %add_multiply_fusion, f32[64,12,768]{2,0,1:T(8,128)S(1)} %get-tuple-element.33, f32[9,12,768]{2,1,0:T(8,128)S(1)} %broadcast_in_dim.14, f32[64,12,768]{2,0,1:T(8,128)S(1)} %get-tuple-element.32), kind=kLoop, calls=%fused_computation | loop fusion | flops 20348928 | bytes 8921088 | tf_op jit(solution)/shard_map/reduce_sum | solution.py:94
  62.6 2.6 %copy.73 = f32[64,9,768]{2,1,0:T(8,128)S(1)} copy(f32[64,9,768]{2,0,1:T(8,128)} %get-tuple-element.39) | data formatting | bytes 3538944 | tf_op jit(solution)/shard_map/reduce_sum | solution.py:94
  65.2 1.6 %reshape.240 = f32[4,144,768,1]{2,1,0,3:T(8,128)} reshape(f32[64,9,768]{2,1,0:T(8,128)S(1)} %copy.73) | data formatting | bytes 3538944 | tf_op jit(solution)/shard_map/dot_general | solution.py:98
  66.8 2.6 %copy.70 = f32[64,9,768]{2,1,0:T(8,128)S(1)} copy(f32[64,9,768]{2,0,1:T(8,128)} %get-tuple-element.40) | data formatting | bytes 3538944 | tf_op jit(solution)/shard_map/reduce_sum | solution.py:94
  69.4 1.4 %reshape.239 = f32[4,144,768,1]{2,1,0,3:T(8,128)} reshape(f32[64,9,768]{2,1,0:T(8,128)S(1)} %copy.70) | data formatting | bytes 3538944 | tf_op jit(solution)/shard_map/dot_general | solution.py:98
  70.8 5.0 %fusion.3 = f32[4,4,144,144]{3,2,1,0:T(8,128)S(1)} fusion(f32[4,144,768,1]{2,1,0,3:T(8,128)} %reshape.240, f32[4,144,768,1]{2,1,0,3:T(8,128)} %reshape.239), kind=kOutput, calls=%fused_computation.8 | convolution fusion | flops 1528823808 | bytes 4866048 | tf_op jit(solution)/shard_map/dot_general | solution.py:98
  75.7 0.2 fusion.24
  75.9 0.4 squeeze.11
  76.3 0.4 squeeze.14
  76.7 0.4 squeeze.13
  77.2 5.3 %collective-permute-start.2 = (f32[4,20736]{1,0:T(4,128)S(1)}, f32[4,20736]{1,0:T(4,128)S(1)}, u32[]{:S(2)}, u32[]{:S(2)}) collective-permute-start(f32[4,20736]{1,0:T(4,128)S(1)} %squeeze.13), channel_id=1, source_target_pairs={{0,508},{4,0},{8,4},{12,8},{16,12},{20,16},{24,20},{28,24},{32,28}... | collective-permute-start | bytes 995336 | tf_op jit(solution)/shard_map/ppermute | solution.py:19
  82.4 3.2 %collective-permute-start.3 = (f32[4,20736]{1,0:T(4,128)S(1)}, f32[4,20736]{1,0:T(4,128)S(1)}, u32[]{:S(2)}, u32[]{:S(2)}) collective-permute-start(f32[4,20736]{1,0:T(4,128)S(1)} %squeeze.14), channel_id=1, source_target_pairs={{0,504},{4,508},{8,0},{12,4},{16,8},{20,12},{24,16},{28,20},{32,24... | collective-permute-start | bytes 995336 | tf_op jit(solution)/shard_map/ppermute | solution.py:19
  85.7 2.2 %collective-permute-start.1 = (f32[4,20736]{1,0:T(4,128)S(1)}, f32[4,20736]{1,0:T(4,128)}, u32[]{:S(2)}, u32[]{:S(2)}) collective-permute-start(f32[4,20736]{1,0:T(4,128)S(1)} %squeeze.11), channel_id=1, source_target_pairs={{0,4},{4,8},{8,12},{12,16},{16,20},{20,24},{24,28},{28,32},{32,36}... | collective-permute-start | bytes 995336 | tf_op jit(solution)/shard_map/ppermute | solution.py:19
  87.9 0.4 squeeze.12
  88.3 5.9 %collective-permute-done.3 = f32[4,20736]{1,0:T(4,128)S(1)} collective-permute-done((f32[4,20736]{1,0:T(4,128)S(1)}, f32[4,20736]{1,0:T(4,128)S(1)}, u32[]{:S(2)}, u32[]{:S(2)}) %collective-permute-start.3) | collective-permute-done | bytes 331808 | tf_op jit(solution)/shard_map/ppermute | solution.py:19
  94.2 1.3 %pad_add_fusion = f32[7,20736]{1,0:T(8,128)S(1)} fusion(f32[4,20736]{1,0:T(4,128)S(1)} %collective-permute-done.3, f32[4,20736]{1,0:T(4,128)S(1)} %collective-permute-done.2, f32[4,20736]{1,0:T(4,128)S(1)} %squeeze.12, f32[4,20736]{1,0:T(4,128)} %collective-permute-done.1), kind=kLoop, calls=%fused_computation.10 | loop fusion | flops 435456 | bytes 1907712 | tf_op jit(solution)/shard_map/add | solution.py:108
  95.5 1.2 %reshape.235 = f32[1,1,7,20736]{3,1,2,0:T(1,128)} reshape(f32[7,20736]{1,0:T(8,128)S(1)} %pad_add_fusion) | data formatting | bytes 1161216 | tf_op jit(solution)/shard_map/reshape | solution.py:109
  (53 shorter events, 1.2 us)
Async XLA Ops:
  40.3 6.7 %copy-start = (f32[256]{0:T(256)S(1)}, f32[256]{0:T(256)}, u32[]{:S(2)}) copy-start(f32[256]{0:T(256)} %param.9) | copy-start | bytes 3076
  42.9 10.4 %all-to-all-start.1 = ((f32[4,28,768]{2,1,0:T(8,128)}), f32[4,28,768]{2,1,0:T(8,128)S(1)}, u32[]{:S(2)}, u32[]{:S(2)}) async-start(f32[4,28,768]{2,1,0:T(8,128)} %broadcast_in_dim.12), calls=%async_computation.1 | async-start | bytes 786432 | tf_op jit(solution)/shard_map/all_to_all | solution.py:44
  47.1 7.7 %collective-permute-start = (f32[256]{0:T(256)S(1)}, f32[256]{0:T(256)S(1)}, u32[]{:S(2)}, u32[]{:S(2)}) collective-permute-start(f32[256]{0:T(256)S(1)} %copy-done), channel_id=1, source_target_pairs={{0,8},{4,12},{8,16},{12,20},{16,24},{20,28},{24,32},{28,36},{32,40... | collective-permute-start | bytes 3080 | tf_op jit(solution)/shard_map/ppermute | solution.py:19
  77.2 11.2 %collective-permute-start.2 = (f32[4,20736]{1,0:T(4,128)S(1)}, f32[4,20736]{1,0:T(4,128)S(1)}, u32[]{:S(2)}, u32[]{:S(2)}) collective-permute-start(f32[4,20736]{1,0:T(4,128)S(1)} %squeeze.13), channel_id=1, source_target_pairs={{0,508},{4,0},{8,4},{12,8},{16,12},{20,16},{24,20},{28,24},{32,28}... | collective-permute-start | bytes 995336 | tf_op jit(solution)/shard_map/ppermute | solution.py:19
  82.4 11.8 %collective-permute-start.3 = (f32[4,20736]{1,0:T(4,128)S(1)}, f32[4,20736]{1,0:T(4,128)S(1)}, u32[]{:S(2)}, u32[]{:S(2)}) collective-permute-start(f32[4,20736]{1,0:T(4,128)S(1)} %squeeze.14), channel_id=1, source_target_pairs={{0,504},{4,508},{8,0},{12,4},{16,8},{20,12},{24,16},{28,20},{32,24... | collective-permute-start | bytes 995336 | tf_op jit(solution)/shard_map/ppermute | solution.py:19
  85.7 8.6 %collective-permute-start.1 = (f32[4,20736]{1,0:T(4,128)S(1)}, f32[4,20736]{1,0:T(4,128)}, u32[]{:S(2)}, u32[]{:S(2)}) collective-permute-start(f32[4,20736]{1,0:T(4,128)S(1)} %squeeze.11), channel_id=1, source_target_pairs={{0,4},{4,8},{8,12},{12,16},{16,20},{20,24},{24,28},{28,32},{32,36}... | collective-permute-start | bytes 995336 | tf_op jit(solution)/shard_map/ppermute | solution.py:19

commit v11 on v9

--- a/solution.py
+++ b/solution.py
@@ -39,7 +39,7 @@
     magnitude = jnp.sqrt(got[0] * got[0] + got[1] * got[1])
     weight = got[nf - 1] * (HUBER_DELTA / jnp.maximum(magnitude, HUBER_DELTA))
     kept = jnp.concatenate([got[2 : nf - 3], weight[None], got[nf - 2 : nf - 1]], axis=0)
-    placed = jnp.dot(kept, onehot, precision=lax.Precision.HIGHEST)
+    placed = jnp.dot(kept, onehot, precision=lax.Precision.HIGH)
     if CAM_BY_ALL_TO_ALL:
         n_cam = lax.axis_size("cam")
         copies = jnp.broadcast_to(placed[None], (n_cam,) + placed.shape)

time: 98.7 us -> 98.4 us (level)
  no operation moved by 1% of the time
where the time goes in v11:
time: 98.4 us; the launch traced here: 96.9 us
  blocking collectives  37.4 us (38%)
  starting transfers between devices  17.9 us (18%)
  local copies, waits for them, and re-layouts  15.7 us (16%)
  other arithmetic  10.5 us (11%)
  waiting for transfers between devices  9.04 us (9%)
  matrix products  5.66 us (6%)
    all_to_all x1, blocking collectives, body(): got = lax.all_to_all(send, 'trk', split_axis=0, concat_axis=0, tiled=True)  37.4 us
    ppermute x4, starting transfers between devices, from_behind(): return lax.ppermute(x, axis, [(i, (i + by) % size) for i in range(size)])  13.8 us
    ppermute x4, waiting for transfers between devices, from_behind(): return lax.ppermute(x, axis, [(i, (i + by) % size) for i in range(size)])  5.92 us
    reduce_sum x1, other arithmetic, panel(): return jnp.sum(sel * vals, axis=1)  5.4 us
    reduce_sum x2, local copies, waits for them, and re-layouts, panel(): return jnp.sum(sel * vals, axis=1)  5.16 us
    dot_general x1, matrix products, body(): lax.dot_general(left_flat, right_flat, (((1,), (1,)), ((), ())), precisio...  4.95 us
    all_to_all x1, starting transfers between devices, body(): lax.all_to_all(copies, 'cam', 0, 0, tiled=True).transpose((1, 0, 2))  4.18 us
    all_to_all x1, waiting for transfers between devices, body(): lax.all_to_all(copies, 'cam', 0, 0, tiled=True).transpose((1, 0, 2))  3.13 us
  transfers between devices with their start and end apart: 5, of which 2 were waited for; matrix products, arithmetic and copies ran while one was open for 2% of the time, Pallas kernels for 0%

profile of v11, /device:TPU:1, one launch (start us, length us, event | category | flops | bytes accessed | tf_op | source)
XLA Modules:
  0.0 96.9 jit_solution(17838523275165809152)
XLA Ops:
  0.0 0.7 convert_element_type.46
  0.7 0.9 pad_maximum_fusion
  1.6 0.2 copy.61
  1.9 0.2 copy.63
  2.2 0.1 copy.62
  2.3 0.1 slice.156
  2.4 0.1 copy.64
  2.5 0.1 maximum_bitcast_fusion.1
  2.6 0.1 copy.65
  2.8 37.4 %all_to_all.14 = f32[128,1,174]{2,1,0:T(1,128)S(1)} all-to-all(f32[128,1,174]{2,1,0:T(1,128)S(1)} %copy.65), channel_id=1, replica_groups=mesh['trk'=128,'cam'=4] {'trk'}, dimensions={0} | all-to-all | bytes 178176 | tf_op jit(solution)/shard_map/all_to_all | solution.py:34
  40.3 0.1 copy.68
  40.5 0.1 reshape.264
  40.6 0.1 copy.71
  40.7 0.1 convert_element_type.48
  40.9 0.1 copy.69
  41.0 0.1 slice.165
  41.1 0.2 copy.67
  41.4 0.1 copy.70
  41.6 0.7 fusion
  42.3 0.8 broadcast_in_dim.12
  43.1 4.2 %all-to-all-start.1 = ((f32[4,26,768]{2,1,0:T(8,128)}), f32[4,26,768]{2,1,0:T(8,128)S(1)}, u32[]{:S(2)}, u32[]{:S(2)}) async-start(f32[4,26,768]{2,1,0:T(8,128)} %broadcast_in_dim.12), calls=%async_computation.1 | async-start | bytes 786432 | tf_op jit(solution)/shard_map/all_to_all | solution.py:46
  47.2 3.0 %collective-permute-start = (f32[256]{0:T(256)S(1)}, f32[256]{0:T(256)S(1)}, u32[]{:S(2)}, u32[]{:S(2)}) collective-permute-start(f32[256]{0:T(256)S(1)} %copy-done), channel_id=1, source_target_pairs={{0,8},{4,12},{8,16},{12,20},{16,24},{20,28},{24,32},{28,36},{32,40... | collective-permute-start | bytes 3080 | tf_op jit(solution)/shard_map/ppermute | solution.py:19
  50.3 3.1 %all-to-all-done.1 = f32[4,26,768]{2,1,0:T(8,128)S(1)} async-done(((f32[4,26,768]{2,1,0:T(8,128)}), f32[4,26,768]{2,1,0:T(8,128)S(1)}, u32[]{:S(2)}, u32[]{:S(2)}) %all-to-all-start.1) | async-done | bytes 319520 | tf_op jit(solution)/shard_map/all_to_all | solution.py:46
  53.5 0.3 add_reduce_fusion.4
  54.4 0.1 add_multiply_fusion.1
  55.0 0.5 multiply_add_fusion.2
  55.5 0.3 maximum_bitcast_fusion
  55.8 0.2 broadcast_in_dim.14
  56.2 0.2 mul.495
  56.5 0.2 mul.501
  56.7 0.6 compare_convert_fusion.1
  57.4 5.4 %multiply_reduce_fusion = (f32[64,9,768]{2,0,1:T(8,128)}, f32[64,9,768]{2,0,1:T(8,128)}) fusion(f32[9,12,768]{2,1,0:T(8,128)S(1)} %add_multiply_fusion, f32[64,12,768]{2,0,1:T(8,128)S(1)} %get-tuple-element.36, f32[9,12,768]{2,1,0:T(8,128)S(1)} %broadcast_in_dim.14, f32[64,12,768]{2,0,1:T(8,128)S(1)} %get-tuple-element.35), kind=kLoop, calls=%fused_computation | loop fusion | flops 20348928 | bytes 8921088 | tf_op jit(solution)/shard_map/reduce_sum | solution.py:93
  62.8 2.6 %copy.81 = f32[64,9,768]{2,1,0:T(8,128)S(1)} copy(f32[64,9,768]{2,0,1:T(8,128)} %get-tuple-element.42) | data formatting | bytes 3538944 | tf_op jit(solution)/shard_map/reduce_sum | solution.py:93
  65.3 1.6 %reshape.266 = f32[4,144,768,1]{2,1,0,3:T(8,128)} reshape(f32[64,9,768]{2,1,0:T(8,128)S(1)} %copy.81) | data formatting | bytes 3538944 | tf_op jit(solution)/shard_map/dot_general | solution.py:97
  66.9 2.6 %copy.78 = f32[64,9,768]{2,1,0:T(8,128)S(1)} copy(f32[64,9,768]{2,0,1:T(8,128)} %get-tuple-element.43) | data formatting | bytes 3538944 | tf_op jit(solution)/shard_map/reduce_sum | solution.py:93
  69.5 1.4 %reshape.265 = f32[4,144,768,1]{2,1,0,3:T(8,128)} reshape(f32[64,9,768]{2,1,0:T(8,128)S(1)} %copy.78) | data formatting | bytes 3538944 | tf_op jit(solution)/shard_map/dot_general | solution.py:97
  70.9 4.9 %fusion.3 = f32[4,4,144,144]{3,2,1,0:T(8,128)S(1)} fusion(f32[4,144,768,1]{2,1,0,3:T(8,128)} %reshape.266, f32[4,144,768,1]{2,1,0,3:T(8,128)} %reshape.265), kind=kOutput, calls=%fused_computation.8 | convolution fusion | flops 1528823808 | bytes 4866048 | tf_op jit(solution)/shard_map/dot_general | solution.py:97
  75.9 0.2 fusion.29
  76.0 0.4 squeeze.11
  76.5 0.4 squeeze.14
  76.9 0.4 squeeze.13
  77.3 5.3 %collective-permute-start.2 = (f32[4,20736]{1,0:T(4,128)S(1)}, f32[4,20736]{1,0:T(4,128)S(1)}, u32[]{:S(2)}, u32[]{:S(2)}) collective-permute-start(f32[4,20736]{1,0:T(4,128)S(1)} %squeeze.13), channel_id=1, source_target_pairs={{0,508},{4,0},{8,4},{12,8},{16,12},{20,16},{24,20},{28,24},{32,28}... | collective-permute-start | bytes 995336 | tf_op jit(solution)/shard_map/ppermute | solution.py:19
  82.6 3.2 %collective-permute-start.3 = (f32[4,20736]{1,0:T(4,128)S(1)}, f32[4,20736]{1,0:T(4,128)S(1)}, u32[]{:S(2)}, u32[]{:S(2)}) collective-permute-start(f32[4,20736]{1,0:T(4,128)S(1)} %squeeze.14), channel_id=1, source_target_pairs={{0,504},{4,508},{8,0},{12,4},{16,8},{20,12},{24,16},{28,20},{32,24... | collective-permute-start | bytes 995336 | tf_op jit(solution)/shard_map/ppermute | solution.py:19
  85.8 2.2 %collective-permute-start.1 = (f32[4,20736]{1,0:T(4,128)S(1)}, f32[4,20736]{1,0:T(4,128)}, u32[]{:S(2)}, u32[]{:S(2)}) collective-permute-start(f32[4,20736]{1,0:T(4,128)S(1)} %squeeze.11), channel_id=1, source_target_pairs={{0,4},{4,8},{8,12},{12,16},{16,20},{20,24},{24,28},{28,32},{32,36}... | collective-permute-start | bytes 995336 | tf_op jit(solution)/shard_map/ppermute | solution.py:19
  88.0 0.4 squeeze.12
  88.5 5.9 %collective-permute-done.3 = f32[4,20736]{1,0:T(4,128)S(1)} collective-permute-done((f32[4,20736]{1,0:T(4,128)S(1)}, f32[4,20736]{1,0:T(4,128)S(1)}, u32[]{:S(2)}, u32[]{:S(2)}) %collective-permute-start.3) | collective-permute-done | bytes 331808 | tf_op jit(solution)/shard_map/ppermute | solution.py:19
  94.4 1.3 %pad_add_fusion = f32[7,20736]{1,0:T(8,128)S(1)} fusion(f32[4,20736]{1,0:T(4,128)S(1)} %collective-permute-done.3, f32[4,20736]{1,0:T(4,128)S(1)} %collective-permute-done.2, f32[4,20736]{1,0:T(4,128)S(1)} %squeeze.12, f32[4,20736]{1,0:T(4,128)} %collective-permute-done.1), kind=kLoop, calls=%fused_computation.10 | loop fusion | flops 435456 | bytes 1907712 | tf_op jit(solution)/shard_map/add | solution.py:107
  95.6 1.2 %reshape.261 = f32[1,1,7,20736]{3,1,2,0:T(1,128)} reshape(f32[7,20736]{1,0:T(8,128)S(1)} %pad_add_fusion) | data formatting | bytes 1161216 | tf_op jit(solution)/shard_map/reshape | solution.py:108
  (54 shorter events, 1.3 us)
Async XLA Ops:
  40.3 6.9 %copy-start = (f32[256]{0:T(256)S(1)}, f32[256]{0:T(256)}, u32[]{:S(2)}) copy-start(f32[256]{0:T(256)} %param.9) | copy-start | bytes 3076
  43.1 10.4 %all-to-all-start.1 = ((f32[4,26,768]{2,1,0:T(8,128)}), f32[4,26,768]{2,1,0:T(8,128)S(1)}, u32[]{:S(2)}, u32[]{:S(2)}) async-start(f32[4,26,768]{2,1,0:T(8,128)} %broadcast_in_dim.12), calls=%async_computation.1 | async-start | bytes 786432 | tf_op jit(solution)/shard_map/all_to_all | solution.py:46
  47.2 7.7 %collective-permute-start = (f32[256]{0:T(256)S(1)}, f32[256]{0:T(256)S(1)}, u32[]{:S(2)}, u32[]{:S(2)}) collective-permute-start(f32[256]{0:T(256)S(1)} %copy-done), channel_id=1, source_target_pairs={{0,8},{4,12},{8,16},{12,20},{16,24},{20,28},{24,32},{28,36},{32,40... | collective-permute-start | bytes 3080 | tf_op jit(solution)/shard_map/ppermute | solution.py:19
  77.3 11.2 %collective-permute-start.2 = (f32[4,20736]{1,0:T(4,128)S(1)}, f32[4,20736]{1,0:T(4,128)S(1)}, u32[]{:S(2)}, u32[]{:S(2)}) collective-permute-start(f32[4,20736]{1,0:T(4,128)S(1)} %squeeze.13), channel_id=1, source_target_pairs={{0,508},{4,0},{8,4},{12,8},{16,12},{20,16},{24,20},{28,24},{32,28}... | collective-permute-start | bytes 995336 | tf_op jit(solution)/shard_map/ppermute | solution.py:19
  82.6 11.8 %collective-permute-start.3 = (f32[4,20736]{1,0:T(4,128)S(1)}, f32[4,20736]{1,0:T(4,128)S(1)}, u32[]{:S(2)}, u32[]{:S(2)}) collective-permute-start(f32[4,20736]{1,0:T(4,128)S(1)} %squeeze.14), channel_id=1, source_target_pairs={{0,504},{4,508},{8,0},{12,4},{16,8},{20,12},{24,16},{28,20},{32,24... | collective-permute-start | bytes 995336 | tf_op jit(solution)/shard_map/ppermute | solution.py:19
  85.8 8.6 %collective-permute-start.1 = (f32[4,20736]{1,0:T(4,128)S(1)}, f32[4,20736]{1,0:T(4,128)}, u32[]{:S(2)}, u32[]{:S(2)}) collective-permute-start(f32[4,20736]{1,0:T(4,128)S(1)} %squeeze.11), channel_id=1, source_target_pairs={{0,4},{4,8},{8,12},{12,16},{16,20},{20,24},{24,28},{28,32},{32,36}... | collective-permute-start | bytes 995336 | tf_op jit(solution)/shard_map/ppermute | solution.py:19

commit v12 on v6

--- a/solution.py
+++ b/solution.py
@@ -37,7 +37,7 @@
     local_slots = rows // tracks
     onehot = (position[:, None] == jnp.arange(rows, dtype=jnp.int32)[None, :]).astype(jnp.float32)
     kept = jnp.concatenate([got[: nf - 3], got[nf - 2 :]], axis=0)
-    placed = jnp.dot(kept, onehot, precision=lax.Precision.HIGHEST)
+    placed = jnp.dot(kept, onehot, precision=lax.Precision.HIGH)
     if CAM_BY_ALL_TO_ALL:
         n_cam = lax.axis_size("cam")
         copies = jnp.broadcast_to(placed[None], (n_cam,) + placed.shape)

time: 99.2 us -> 99 us (level)
  no operation moved by 1% of the time
where the time goes in v12:
time: 99 us; the launch traced here: 97.4 us
  blocking collectives  37.4 us (38%)
  starting transfers between devices  17.9 us (18%)
  local copies, waits for them, and re-layouts  15.4 us (16%)
  other arithmetic  11.6 us (12%)
  waiting for transfers between devices  8.77 us (9%)
  matrix products  5.66 us (6%)
    all_to_all x1, blocking collectives, body(): got = lax.all_to_all(send, 'trk', split_axis=0, concat_axis=0, tiled=True)  37.4 us
    ppermute x4, starting transfers between devices, from_behind(): return lax.ppermute(x, axis, [(i, (i + by) % size) for i in range(size)])  13.7 us
    ppermute x4, waiting for transfers between devices, from_behind(): return lax.ppermute(x, axis, [(i, (i + by) % size) for i in range(size)])  5.65 us
    reduce_sum x1, other arithmetic, panel(): return jnp.sum(sel * vals, axis=1)  5.4 us
    reduce_sum x2, local copies, waits for them, and re-layouts, panel(): return jnp.sum(sel * vals, axis=1)  5.16 us
    dot_general x1, matrix products, body(): lax.dot_general(left_flat, right_flat, (((1,), (1,)), ((), ())), precisio...  4.95 us
    all_to_all x1, starting transfers between devices, body(): lax.all_to_all(copies, 'cam', 0, 0, tiled=True).transpose((1, 0, 2))  4.18 us
    all_to_all x1, waiting for transfers between devices, body(): lax.all_to_all(copies, 'cam', 0, 0, tiled=True).transpose((1, 0, 2))  3.13 us
  transfers between devices with their start and end apart: 5, of which 2 were waited for; matrix products, arithmetic and copies ran while one was open for 2% of the time, Pallas kernels for 0%

profile of v12, /device:TPU:1, one launch (start us, length us, event | category | flops | bytes accessed | tf_op | source)
XLA Modules:
  0.0 97.4 jit_solution(16782829148832522092)
XLA Ops:
  0.0 0.7 convert_element_type.46
  0.7 0.9 pad_maximum_fusion
  1.6 0.2 copy.74
  1.9 0.2 copy.76
  2.2 0.1 copy.75
  2.3 0.1 slice.156
  2.4 0.1 copy.77
  2.5 0.1 maximum_bitcast_fusion.1
  2.6 0.1 copy.78
  2.8 37.4 %all_to_all.14 = f32[128,1,174]{2,1,0:T(1,128)S(1)} all-to-all(f32[128,1,174]{2,1,0:T(1,128)S(1)} %copy.78), channel_id=1, replica_groups=mesh['trk'=128,'cam'=4] {'trk'}, dimensions={0} | all-to-all | bytes 178176 | tf_op jit(solution)/shard_map/all_to_all | solution.py:34
  40.2 0.1 copy.79
  40.4 0.1 copy.83
  40.5 0.1 convert_element_type.48
  40.6 0.1 copy.81
  40.7 0.1 slice.162
  40.9 0.3 copy.80
  41.2 0.2 copy.82
  41.4 0.7 fusion
  42.1 0.8 broadcast_in_dim.12
  42.9 4.2 %all-to-all-start.1 = ((f32[4,28,768]{2,1,0:T(8,128)}), f32[4,28,768]{2,1,0:T(8,128)S(1)}, u32[]{:S(2)}, u32[]{:S(2)}) async-start(f32[4,28,768]{2,1,0:T(8,128)} %broadcast_in_dim.12), calls=%async_computation.1 | async-start | bytes 786432 | tf_op jit(solution)/shard_map/all_to_all | solution.py:44
  47.1 3.0 %collective-permute-start = (f32[256]{0:T(256)S(1)}, f32[256]{0:T(256)S(1)}, u32[]{:S(2)}, u32[]{:S(2)}) collective-permute-start(f32[256]{0:T(256)S(1)} %copy-done), channel_id=1, source_target_pairs={{0,8},{4,12},{8,16},{12,20},{16,24},{20,28},{24,32},{28,36},{32,40... | collective-permute-start | bytes 3080 | tf_op jit(solution)/shard_map/ppermute | solution.py:19
  50.2 3.1 %all-to-all-done.1 = f32[4,28,768]{2,1,0:T(8,128)S(1)} async-done(((f32[4,28,768]{2,1,0:T(8,128)}), f32[4,28,768]{2,1,0:T(8,128)S(1)}, u32[]{:S(2)}, u32[]{:S(2)}) %all-to-all-start.1) | async-done | bytes 344096 | tf_op jit(solution)/shard_map/all_to_all | solution.py:44
  53.3 0.3 add_reduce_fusion.4
  54.3 0.1 add_multiply_fusion.1
  54.8 0.5 multiply_add_fusion.2
  55.4 0.3 maximum_bitcast_fusion
  55.7 0.2 broadcast_in_dim.14
  55.9 0.1 mul.554
  56.0 0.2 mul.555
  56.2 0.1 mul.560
  56.3 0.2 mul.561
  56.6 0.6 compare_convert_fusion.1
  57.2 5.4 %multiply_reduce_fusion = (f32[64,9,768]{2,0,1:T(8,128)}, f32[64,9,768]{2,0,1:T(8,128)}) fusion(f32[9,12,768]{2,1,0:T(8,128)S(1)} %add_multiply_fusion, f32[64,12,768]{2,0,1:T(8,128)S(1)} %get-tuple-element.33, f32[9,12,768]{2,1,0:T(8,128)S(1)} %broadcast_in_dim.14, f32[64,12,768]{2,0,1:T(8,128)S(1)} %get-tuple-element.32), kind=kLoop, calls=%fused_computation | loop fusion | flops 20348928 | bytes 8921088 | tf_op jit(solution)/shard_map/reduce_sum | solution.py:94
  62.6 2.6 %copy.93 = f32[64,9,768]{2,1,0:T(8,128)S(1)} copy(f32[64,9,768]{2,0,1:T(8,128)} %get-tuple-element.39) | data formatting | bytes 3538944 | tf_op jit(solution)/shard_map/reduce_sum | solution.py:94
  65.2 1.6 %reshape.236 = f32[4,144,768,1]{2,1,0,3:T(8,128)} reshape(f32[64,9,768]{2,1,0:T(8,128)S(1)} %copy.93) | data formatting | bytes 3538944 | tf_op jit(solution)/shard_map/dot_general | solution.py:98
  66.8 2.6 %copy.90 = f32[64,9,768]{2,1,0:T(8,128)S(1)} copy(f32[64,9,768]{2,0,1:T(8,128)} %get-tuple-element.40) | data formatting | bytes 3538944 | tf_op jit(solution)/shard_map/reduce_sum | solution.py:94
  69.4 1.4 %reshape.235 = f32[4,144,768,1]{2,1,0,3:T(8,128)} reshape(f32[64,9,768]{2,1,0:T(8,128)S(1)} %copy.90) | data formatting | bytes 3538944 | tf_op jit(solution)/shard_map/dot_general | solution.py:98
  70.8 5.0 %fusion.3 = f32[4,4,144,144]{3,2,1,0:T(8,128)S(1)} fusion(f32[4,144,768,1]{2,1,0,3:T(8,128)} %reshape.236, f32[4,144,768,1]{2,1,0,3:T(8,128)} %reshape.235), kind=kOutput, calls=%fused_computation.8 | convolution fusion | flops 1528823808 | bytes 4866048 | tf_op jit(solution)/shard_map/dot_general | solution.py:98
  75.7 0.2 fusion.24
  75.9 0.7 broadcast_in_dim_squeeze.16
  76.6 0.7 broadcast_in_dim_squeeze.19
  77.3 0.7 broadcast_in_dim_squeeze.18
  78.0 5.3 %collective-permute-start.2 = (f32[1,1,4,20736]{3,1,2,0:T(1,128)S(1)}, f32[1,1,4,20736]{3,1,2,0:T(1,128)S(1)}, u32[]{:S(2)}, u32[]{:S(2)}) collective-permute-start(f32[1,1,4,20736]{3,1,2,0:T(1,128)S(1)} %broadcast_in_dim_squeeze.18), channel_id=1, source_target_pairs={{0,508},{4,0},{8,4},{12,8},{16,12},{20,16},{24,20},{28,24},{32,28}... | collective-permute-start | bytes 995336 | tf_op jit(solution)/shard_map/ppermute | solution.py:19
  83.2 3.2 %collective-permute-start.3 = (f32[1,1,4,20736]{3,1,2,0:T(1,128)S(1)}, f32[1,1,4,20736]{3,1,2,0:T(1,128)S(1)}, u32[]{:S(2)}, u32[]{:S(2)}) collective-permute-start(f32[1,1,4,20736]{3,1,2,0:T(1,128)S(1)} %broadcast_in_dim_squeeze.19), channel_id=1, source_target_pairs={{0,504},{4,508},{8,0},{12,4},{16,8},{20,12},{24,16},{28,20},{32,24... | collective-permute-start | bytes 995336 | tf_op jit(solution)/shard_map/ppermute | solution.py:19
  86.5 2.2 %collective-permute-start.1 = (f32[1,1,4,20736]{3,1,2,0:T(1,128)S(1)}, f32[1,1,4,20736]{3,1,2,0:T(1,128)}, u32[]{:S(2)}, u32[]{:S(2)}) collective-permute-start(f32[1,1,4,20736]{3,1,2,0:T(1,128)S(1)} %broadcast_in_dim_squeeze.16), channel_id=1, source_target_pairs={{0,4},{4,8},{8,12},{12,16},{16,20},{20,24},{24,28},{28,32},{32,36}... | collective-permute-start | bytes 995336 | tf_op jit(solution)/shard_map/ppermute | solution.py:19
  88.7 0.7 broadcast_in_dim_squeeze.17
  89.4 5.6 %collective-permute-done.3 = f32[1,1,4,20736]{3,1,2,0:T(1,128)S(1)} collective-permute-done((f32[1,1,4,20736]{3,1,2,0:T(1,128)S(1)}, f32[1,1,4,20736]{3,1,2,0:T(1,128)S(1)}, u32[]{:S(2)}, u32[]{:S(2)}) %collective-permute-start.3) | collective-permute-done | bytes 331808 | tf_op jit(solution)/shard_map/ppermute | solution.py:19
  95.1 2.3 %pad_add_fusion = f32[1,1,7,20736]{3,1,2,0:T(1,128)} fusion(f32[1,1,4,20736]{3,1,2,0:T(1,128)S(1)} %collective-permute-done.3, f32[1,1,4,20736]{3,1,2,0:T(1,128)S(1)} %collective-permute-done.2, f32[1,1,4,20736]{3,1,2,0:T(1,128)S(1)} %broadcast_in_dim_squeeze.17, f32[1,1,4,20736]{3,1,2,0:T(1,128)} %collective-permute-done.1), kind=kLoop, calls=%fused_computation.10 | loop fusion | flops 435456 | bytes 1907712 | tf_op jit(solution)/shard_map/add | solution.py:110
  (52 shorter events, 1.1 us)
Async XLA Ops:
  40.3 6.7 %copy-start = (f32[256]{0:T(256)S(1)}, f32[256]{0:T(256)}, u32[]{:S(2)}) copy-start(f32[256]{0:T(256)} %param.9) | copy-start | bytes 3076
  42.9 10.4 %all-to-all-start.1 = ((f32[4,28,768]{2,1,0:T(8,128)}), f32[4,28,768]{2,1,0:T(8,128)S(1)}, u32[]{:S(2)}, u32[]{:S(2)}) async-start(f32[4,28,768]{2,1,0:T(8,128)} %broadcast_in_dim.12), calls=%async_computation.1 | async-start | bytes 786432 | tf_op jit(solution)/shard_map/all_to_all | solution.py:44
  47.1 7.7 %collective-permute-start = (f32[256]{0:T(256)S(1)}, f32[256]{0:T(256)S(1)}, u32[]{:S(2)}, u32[]{:S(2)}) collective-permute-start(f32[256]{0:T(256)S(1)} %copy-done), channel_id=1, source_target_pairs={{0,8},{4,12},{8,16},{12,20},{16,24},{20,28},{24,32},{28,36},{32,40... | collective-permute-start | bytes 3080 | tf_op jit(solution)/shard_map/ppermute | solution.py:19
  78.0 11.4 %collective-permute-start.2 = (f32[1,1,4,20736]{3,1,2,0:T(1,128)S(1)}, f32[1,1,4,20736]{3,1,2,0:T(1,128)S(1)}, u32[]{:S(2)}, u32[]{:S(2)}) collective-permute-start(f32[1,1,4,20736]{3,1,2,0:T(1,128)S(1)} %broadcast_in_dim_squeeze.18), channel_id=1, source_target_pairs={{0,508},{4,0},{8,4},{12,8},{16,12},{20,16},{24,20},{28,24},{32,28}... | collective-permute-start | bytes 995336 | tf_op jit(solution)/shard_map/ppermute | solution.py:19
  83.2 11.8 %collective-permute-start.3 = (f32[1,1,4,20736]{3,1,2,0:T(1,128)S(1)}, f32[1,1,4,20736]{3,1,2,0:T(1,128)S(1)}, u32[]{:S(2)}, u32[]{:S(2)}) collective-permute-start(f32[1,1,4,20736]{3,1,2,0:T(1,128)S(1)} %broadcast_in_dim_squeeze.19), channel_id=1, source_target_pairs={{0,504},{4,508},{8,0},{12,4},{16,8},{20,12},{24,16},{28,20},{32,24... | collective-permute-start | bytes 995336 | tf_op jit(solution)/shard_map/ppermute | solution.py:19
  86.5 8.6 %collective-permute-start.1 = (f32[1,1,4,20736]{3,1,2,0:T(1,128)S(1)}, f32[1,1,4,20736]{3,1,2,0:T(1,128)}, u32[]{:S(2)}, u32[]{:S(2)}) collective-permute-start(f32[1,1,4,20736]{3,1,2,0:T(1,128)S(1)} %broadcast_in_dim_squeeze.16), channel_id=1, source_target_pairs={{0,4},{4,8},{8,12},{12,16},{16,20},{20,24},{24,28},{28,32},{32,36}... | collective-permute-start | bytes 995336 | tf_op jit(solution)/shard_map/ppermute | solution.py:19
